TPU v7x, 128 devices: a whole 4x4x4 slice. The times are simulated.
128 devices in a mesh: expert: 32 (over y, x, core), pair: 4 (over z).
Axes of the slice: x: 4, y: 4, z: 4, core: 2. Of those that a mesh axis runs over, the one named last changes fastest.
Arguments:
- tokens: bfloat16 [16384, 4096], P(('expert', 'pair')), may hold values from -6 to 6
- expert_ids: int32 [16384, 8], P(('expert', 'pair')), may hold values from 0 to 127, all different within a row
- route_weight: float32 [16384, 8], P(('expert', 'pair')), may hold values from 0.1 to 1
- gate_weight: bfloat16 [32, 4096, 768], P('expert'), may hold values from -0.09375 to 0.09375
- up_weight: bfloat16 [32, 4096, 768], P('expert'), may hold values from -0.09375 to 0.09375
- down_weight: bfloat16 [32, 768, 4096], P('expert'), may hold values from -0.21875 to 0.21875
Outputs:
- combined: bfloat16 [16384, 4096], P(('expert', 'pair'))
- hessian: float32 [32, 768, 768], P('expert', 'pair')
- panel: float32 [32, 768, 128], P('expert', 'pair')
Inputs may be any that keep to these rules, and one draw needn't show every extreme that they name: `expert_ids`: each row names 8 different experts, and every expert is named by some row.
All inputs are finite; a program needn't handle non-finite values.
Results may differ from a plain program's by a relative error of at most 0.0057.
Values may be sent and summed in bfloat16 or wider, within the bound.
No kernel may reach another device: no remote copies, remote signals or barrier semaphores. Data moves between devices by JAX's collectives and lax.ppermute only.
A program may use at most 128 MiB of HBM per device.

v0:
```python
import jax
import jax.numpy as jnp
from jax import lax
from jax.sharding import PartitionSpec as P

EXPERTS = 128
FF = 768
PANEL = 128
CAP = 16


def swiglu_rows(flat_rows, gate_matrix, upper_matrix, down_matrix):
    gate_value = jnp.dot(flat_rows, gate_matrix, preferred_element_type=jnp.float32)
    upper_value = jnp.dot(flat_rows, upper_matrix, preferred_element_type=jnp.float32)
    hidden = (jax.nn.silu(gate_value) * upper_value).astype(jnp.bfloat16)
    output = jnp.dot(hidden, down_matrix, preferred_element_type=jnp.float32).astype(jnp.bfloat16)
    return (hidden, output)


def split_bf16(values):
    high = values.astype(jnp.bfloat16)
    low = (values - high.astype(jnp.float32)).astype(jnp.bfloat16)
    return high, low


def per_device(tokens, expert_ids, route_weight, gate_weight, up_weight, down_weight):
    owners = lax.axis_size("expert")
    pair_count = lax.axis_size("pair")
    tok_count = tokens.shape[0]
    model_width = tokens.shape[1]
    per_owner = EXPERTS // owners
    in_flight = expert_ids % per_owner == 0
    owner_of = expert_ids // per_owner
    columns = lax.broadcasted_iota(jnp.int32, (1, 1, owners), 2)
    route_hit = (in_flight[:, :, None] & (owner_of[:, :, None] == columns)).astype(jnp.int32)
    picked = jnp.sum(route_hit, axis=1)
    before = jnp.cumsum(picked, axis=0) - picked
    kept_rows = picked * (before < CAP).astype(jnp.int32)
    slot_ids = lax.broadcasted_iota(jnp.int32, (1, 1, CAP), 2)
    slot_marks = kept_rows[:, :, None] * (before[:, :, None] == slot_ids).astype(jnp.int32)
    marks_flat = slot_marks.reshape(tok_count, owners * CAP)
    selector = marks_flat.astype(jnp.bfloat16)
    outgoing = lax.dot_general(
        selector, tokens, (((0,), (0,)), ((), ())), preferred_element_type=jnp.float32
    ).astype(jnp.bfloat16)
    outgoing = outgoing.reshape(owners, CAP, model_width)
    gate_matrix = gate_weight[0]
    upper_matrix = up_weight[0]
    down_matrix = down_weight[0]
    arrived = lax.all_to_all(outgoing, "expert", split_axis=0, concat_axis=0, tiled=True)
    item_count = arrived.shape[1]
    hidden, output = swiglu_rows(
        arrived.reshape(-1, model_width), gate_matrix, upper_matrix, down_matrix
    )
    results = output.reshape(owners, item_count, model_width)
    returned = lax.all_to_all(results, "expert", split_axis=0, concat_axis=0, tiled=True)
    returned_flat = returned.reshape(-1, model_width)
    owner_weight = jnp.sum(route_hit.astype(jnp.float32) * route_weight[:, :, None], axis=1)
    combine_matrix = (
        slot_marks.astype(jnp.float32) * owner_weight[:, :, None]
    ).reshape(tok_count, owners * CAP)
    weight_high, weight_low = split_bf16(combine_matrix)
    combined = jnp.dot(weight_high, returned_flat, preferred_element_type=jnp.float32) + jnp.dot(
        weight_low, returned_flat, preferred_element_type=jnp.float32
    )
    hess_scale = 2.0 / (CAP * owners * pair_count)
    all_hidden = lax.all_gather(hidden, "pair", axis=0, tiled=True)
    whole_sum = (
        lax.dot_general(
            all_hidden, all_hidden, (((0,), (0,)), ((), ())), preferred_element_type=jnp.float32
        )
        * hess_scale
    )
    row_share = FF // pair_count
    pair_place = lax.axis_index("pair")
    damping = 0.01 * jnp.trace(whole_sum) / FF
    corner = whole_sum[:PANEL, :PANEL]
    my_rows = lax.dynamic_slice_in_dim(whole_sum, pair_place * row_share, row_share, 0)
    lower_factor = jnp.linalg.cholesky(corner + damping * jnp.eye(PANEL, dtype=jnp.float32))
    row_ids = pair_place * row_share + lax.broadcasted_iota(jnp.int32, (row_share, PANEL), 0)
    column_ids = lax.broadcasted_iota(jnp.int32, (row_share, PANEL), 1)
    leading = my_rows[:, :PANEL] + damping * (row_ids == column_ids).astype(jnp.float32)
    panel_rows = jax.scipy.linalg.solve_triangular(lower_factor, leading.T, lower=True).T
    return (combined.astype(jnp.bfloat16), my_rows[None], panel_rows[None])


def solution(mesh):
    in_specs = (
        P(("expert", "pair"), None),
        P(("expert", "pair"), None),
        P(("expert", "pair"), None),
        P("expert", None, None),
        P("expert", None, None),
        P("expert", None, None),
    )
    out_specs = (P(("expert", "pair"), None), P("expert", "pair", None), P("expert", "pair", None))
    return jax.shard_map(
        per_device, mesh=mesh, in_specs=in_specs, out_specs=out_specs, check_vma=False
    )
```

profile of v0, /device:TPU:0, one launch (start us, length us, event | category | flops | bytes accessed | tf_op | source)
XLA Modules:
  0.0 188.6 jit_solution(9141202033740325093)
XLA Ops:
  7.2 0.8 fusion.34
  8.0 0.7 add_select_fusion
  8.8 0.1 copy.31
  8.9 0.2 reduce_window_sum.11
  9.2 0.2 fusion.13
  9.4 1.2 convolution_convert_fusion
  10.7 58.4 %all_to_all.10 = bf16[32,16,4096]{2,1,0:T(8,128)(2,1)S(1)} all-to-all(bf16[32,16,4096]{2,1,0:T(8,128)(2,1)S(1)} %bitcast.54), channel_id=1, replica_groups=mesh['expert'=32,'pair'=4] {'expert'}, dimensions={0} | all-to-all | bytes 8388608 | tf_op jit(solution)/shard_map/all_to_all | solution.py:50
  69.1 3.4 %fusion.4 = f32[512,768]{1,0:T(8,128)S(1)} fusion(bf16[512,4096]{1,0:T(8,128)(2,1)S(1)} %bitcast.56, bf16[1,4096,768]{2,1,0:T(8,128)(2,1)S(1)} %bitcast.59), kind=kOutput, calls=%fused_computation.4 | convolution fusion | flops 3221225472 | bytes 12058624 | tf_op jit(solution)/shard_map/dot_general | solution.py:13
  72.5 3.5 %multiply_convert_fusion = bf16[512,768]{1,0:T(8,128)(2,1)S(1)} fusion(f32[512,768]{1,0:T(8,128)S(1)} %fusion.4, bf16[512,4096]{1,0:T(8,128)(2,1)S(1)} %bitcast.57, bf16[1,4096,768]{2,1,0:T(8,128)(2,1)S(1)} %bitcast.61), kind=kOutput, calls=%fused_computation.15 | convolution fusion | flops 3223584768 | bytes 12845056 | tf_op jit(solution)/shard_map/dot_general | solution.py:14
  76.1 8.0 %fusion.6 = bf16[512,4096]{1,0:T(8,128)(2,1)} fusion(bf16[512,768]{1,0:T(8,128)(2,1)S(1)} %multiply_convert_fusion, bf16[1,768,4096]{2,1,0:T(8,128)(2,1)} %param.11), kind=kOutput, calls=%fused_computation.7 | convolution fusion | flops 3223322624 | bytes 11272192 | tf_op jit(solution)/shard_map/dot_general | solution.py:16
  84.1 5.0 %all-to-all-start.1 = ((bf16[32,16,4096]{2,1,0:T(8,128)(2,1)}), bf16[32,16,4096]{2,1,0:T(8,128)(2,1)}, u32[]{:S(2)}, u32[]{:S(2)}) async-start(bf16[32,16,4096]{2,1,0:T(8,128)(2,1)} %bitcast.55), calls=%async_computation.1 | async-start | bytes 8388608 | tf_op jit(solution)/shard_map/all_to_all | solution.py:56
  89.1 0.2 all-gather.2.cloned.1.call-start
  89.3 0.5 all-gather.2.cloned.1.call-update
  89.9 53.2 %all-to-all-done.1 = bf16[32,16,4096]{2,1,0:T(8,128)(2,1)} async-done(((bf16[32,16,4096]{2,1,0:T(8,128)(2,1)}), bf16[32,16,4096]{2,1,0:T(8,128)(2,1)}, u32[]{:S(2)}, u32[]{:S(2)}) %all-to-all-start.1) | async-done | bytes 4194336 | tf_op jit(solution)/shard_map/all_to_all | solution.py:56
  143.1 2.9 %convolution_bitcast_fusion = f32[128,4096]{1,0:T(8,128)S(1)} fusion(bf16[32,16,4096]{2,1,0:T(8,128)(2,1)} %all-to-all-done.1, f32[128,32]{0,1:T(8,128)S(1)} %fusion.17, s32[128,32]{0,1:T(8,128)S(1)} %copy.35, s32[128,32]{0,1:T(8,128)S(1)} %copy.33), kind=kOutput, calls=%fused_computation.8 | convolution fusion | flops 537395200 | bytes 6340608 | tf_op jit(solution)/shard_map/dot_general | solution.py:63
  146.0 4.0 %fusion.10 = bf16[128,4096]{1,0:T(8,128)(2,1)} fusion(f32[128,4096]{1,0:T(8,128)S(1)} %convolution_bitcast_fusion, bf16[32,16,4096]{2,1,0:T(8,128)(2,1)} %all-to-all-done.1, f32[128,32]{0,1:T(8,128)S(1)} %fusion.17, s32[128,32]{0,1:T(8,128)S(1)} %copy.35, s32[128,32]{0,1:T(8,128)S(1)} %copy.33), kind=kOutput, calls=%fused_computation.11 | convolution fusion | flops 538247168 | bytes 7389184 | tf_op jit(solution)/shard_map/dot_general | solution.py:63
  150.0 6.3 %select_reduce_fusion = (f32[]{:T(128)}, f32[768,768]{1,0:T(8,128)S(1)}) fusion(bf16[2048,768]{1,0:T(8,128)(2,1)} %all-gather.2.cloned.1.call-done), kind=kOutput, calls=%fused_computation.12 | convolution fusion | flops 2418278400 | bytes 5505028 | tf_op jit(solution)/shard_map/dot_general | solution.py:69
  156.9 0.1 copy.36
  157.1 11.7 %cholesky.16 = f32[128,128]{1,0:T(8,128)S(1)} custom-call(f32[128,128]{1,0:T(8,128)S(1)} %fusion.30), custom_call_target="Cholesky" | custom-call | tf_op jit(solution)/shard_map/jit(cholesky)/cholesky | solution.py:79
  168.8 0.6 compare_reduce_fusion
  169.5 0.7 fusion.28
  170.1 9.8 %custom-call.7 = f32[1,128,128]{1,2,0:T(8,128)S(1)} custom-call(f32[1,128,128]{2,1,0:T(8,128)S(1)} %fusion.28), custom_call_target="InvertDiagBlocksLowerTriangular" | custom-call | tf_op jit(solution)/shard_map/jit(_solve_triangular)/triangular_solve | solution.py:83
  179.9 0.9 dynamic-slice_bitcast_fusion
  180.8 0.9 convolution_bitcast_fusion.2
  (28 shorter events, 0.4 us)
Async XLA Ops:
  7.2 2.2 %copy-start = (bf16[128,4096]{1,0:T(8,128)(2,1)S(1)}, bf16[128,4096]{1,0:T(8,128)(2,1)}, u32[]{:S(2)}) copy-start(bf16[128,4096]{1,0:T(8,128)(2,1)} %param.6) | copy-start | bytes 3145732
  9.4 59.7 %slice-start = ((s8[6291456]{0:T(1024)(128)(4,1)}), s8[4194304]{0:T(1024)(128)(4,1)S(1)}, s32[]{:S(2)}) async-start(s8[6291456]{0:T(1024)(128)(4,1)} %bitcast.58), calls=%async_computation.3 | async-start | bytes 8388608
  10.6 58.4 %slice-start.1 = ((s8[6291456]{0:T(1024)(128)(4,1)}), s8[2097152]{0:T(1024)(128)(4,1)S(1)}, s32[]{:S(2)}) async-start(s8[6291456]{0:T(1024)(128)(4,1)} %bitcast.58), calls=%async_computation.4 | async-start | bytes 4194304
  10.6 61.9 %slice-start.2 = ((s8[6291456]{0:T(1024)(128)(4,1)}), s8[4194304]{0:T(1024)(128)(4,1)S(1)}, s32[]{:S(2)}) async-start(s8[6291456]{0:T(1024)(128)(4,1)} %bitcast.60), calls=%async_computation.5 | async-start | bytes 8388608
  69.1 3.5 %slice-start.3 = ((s8[6291456]{0:T(1024)(128)(4,1)}), s8[2097152]{0:T(1024)(128)(4,1)S(1)}, s32[]{:S(2)}) async-start(s8[6291456]{0:T(1024)(128)(4,1)} %bitcast.60), calls=%async_computation.6 | async-start | bytes 4194304
  76.1 8.0 %copy-start.1 = (bf16[512,768]{1,0:T(8,128)(2,1)}, bf16[512,768]{1,0:T(8,128)(2,1)S(1)}, u32[]{:S(2)}) copy-start(bf16[512,768]{1,0:T(8,128)(2,1)S(1)} %multiply_convert_fusion) | copy-start | bytes 2359300
  84.1 5.8 %copy-start.2 = (f32[128,8]{0,1:T(8,128)S(1)}, f32[128,8]{0,1:T(8,128)}, u32[]{:S(2)}) copy-start(f32[128,8]{0,1:T(8,128)} %param.8) | copy-start | bytes 12292
  84.1 59.0 %all-to-all-start.1 = ((bf16[32,16,4096]{2,1,0:T(8,128)(2,1)}), bf16[32,16,4096]{2,1,0:T(8,128)(2,1)}, u32[]{:S(2)}, u32[]{:S(2)}) async-start(bf16[32,16,4096]{2,1,0:T(8,128)(2,1)} %bitcast.55), calls=%async_computation.1 | async-start | bytes 8388608 | tf_op jit(solution)/shard_map/all_to_all | solution.py:56
  89.1 60.9 %all-gather.2.cloned.1.call-start = ((), (), s32[]{:S(2)}) async-start(), calls=%async_computation.2 | async-start | bytes 3932160 | tf_op jit(solution)/shard_map/all_gather | solution.py:67
Sparse Core Ops, SparseCore 0:
  91.6 42.0 all-gather.1
where the time goes:
time: 189 us
  blocking collectives  58.4 us (31%)
  waiting for transfers between devices  53.7 us (28%)
  matrix products  30.3 us (16%)
  other arithmetic  24.8 us (13%)
  between operations  14.9 us (8%)
  starting transfers between devices  5.22 us (3%)
    all_to_all x1, blocking collectives, per_device(): lax.all_to_all(outgoing, 'expert', split_axis=0, concat_axis=0, tiled=True)  58.4 us
    all_to_all x1, waiting for transfers between devices, per_device(): lax.all_to_all(results, 'expert', split_axis=0, concat_axis=0, tiled=True)  53.2 us
    another operation x3, other arithmetic, per_device(): jnp.linalg.cholesky(corner + damping * jnp.eye(PANEL, dtype=jnp.float32))  12.4 us
    another operation x2, other arithmetic, per_device(): jax.scipy.linalg.solve_triangular(lower_factor, leading.T, lower=True)  10.5 us
    dot_general x1, matrix products, swiglu_rows(): jnp.dot(hidden, down_matrix, preferred_element_type=jnp.float32)  8.03 us
    dot_general x1, matrix products, per_device(): lax.dot_general(all_hidden, all_hidden, (((0,), (0,)), ((), ())), preferr...  6.31 us
    all_to_all x1, starting transfers between devices, per_device(): lax.all_to_all(results, 'expert', split_axis=0, concat_axis=0, tiled=True)  5 us
    dot_general x1, matrix products, per_device(): jnp.dot(weight_high, returned_flat, preferred_element_type=jnp.float32)  3.95 us
  transfers between devices with their start and end apart: 2, of which 1 were waited for; matrix products, arithmetic and copies ran while one was open for 4% of the time, Pallas kernels for 0%

commit v1 on v0

--- a/solution.py
+++ b/solution.py
@@ -64,19 +64,30 @@
         weight_low, returned_flat, preferred_element_type=jnp.float32
     )
     hess_scale = 2.0 / (CAP * owners * pair_count)
+    row_share = FF // pair_count
+    pair_place = lax.axis_index("pair")
+    hidden_wide = hidden.astype(jnp.float32)
+    corner_part = lax.dot_general(
+        hidden[:, :PANEL], hidden[:, :PANEL], (((0,), (0,)), ((), ())),
+        preferred_element_type=jnp.float32,
+    )
+    square_part = jnp.broadcast_to(jnp.sum(hidden_wide * hidden_wide), (8, PANEL))
+    pack = jnp.concatenate([corner_part, square_part], axis=0)
+    pack_sum = pack
+    for shift in range(1, pair_count):
+        ring = [(i, (i + shift) % pair_count) for i in range(pair_count)]
+        pack_sum = pack_sum + lax.ppermute(pack, "pair", ring)
+    corner = pack_sum[:PANEL] * hess_scale
+    damping = 0.01 * (pack_sum[PANEL, 0] * hess_scale) / FF
+    lower_factor = jnp.linalg.cholesky(corner + damping * jnp.eye(PANEL, dtype=jnp.float32))
     all_hidden = lax.all_gather(hidden, "pair", axis=0, tiled=True)
-    whole_sum = (
+    my_columns = lax.dynamic_slice_in_dim(all_hidden, pair_place * row_share, row_share, 1)
+    my_rows = (
         lax.dot_general(
-            all_hidden, all_hidden, (((0,), (0,)), ((), ())), preferred_element_type=jnp.float32
+            my_columns, all_hidden, (((0,), (0,)), ((), ())), preferred_element_type=jnp.float32
         )
         * hess_scale
     )
-    row_share = FF // pair_count
-    pair_place = lax.axis_index("pair")
-    damping = 0.01 * jnp.trace(whole_sum) / FF
-    corner = whole_sum[:PANEL, :PANEL]
-    my_rows = lax.dynamic_slice_in_dim(whole_sum, pair_place * row_share, row_share, 0)
-    lower_factor = jnp.linalg.cholesky(corner + damping * jnp.eye(PANEL, dtype=jnp.float32))
     row_ids = pair_place * row_share + lax.broadcasted_iota(jnp.int32, (row_share, PANEL), 0)
     column_ids = lax.broadcasted_iota(jnp.int32, (row_share, PANEL), 1)
     leading = my_rows[:, :PANEL] + damping * (row_ids == column_ids).astype(jnp.float32)

time: 189 us -> 163 us (0.86)
  waiting for transfers between devices: 53.7 us -> 20.5 us
  starting transfers between devices: 5.22 us -> 11.6 us
    all_to_all x1, waiting for transfers between devices: 53.2 us -> 16.6 us  [per_device(): lax.all_to_all(results, 'expert', split_axis=0, concat_axis=0, tiled=True)]
    ppermute x0 -> x3, starting transfers between devices: none -> 6.57 us  [per_device(): pack_sum = pack_sum + lax.ppermute(pack, 'pair', ring)]
    ppermute x0 -> x3, waiting for transfers between devices: none -> 3.3 us  [per_device(): pack_sum = pack_sum + lax.ppermute(pack, 'pair', ring)]
    dot_general x1 -> x2, matrix products: 6.31 us -> 4.62 us  [the longest x1 3.42 us: per_device(): lax.dot_general(my_columns, all_hidden, (((0,), (0,)), ((), ())), preferr...]
  transfers between devices with their start and end apart: 2 -> 5, of which waited for: 1 -> 3; matrix products, arithmetic and copies ran while one was open for 4% -> 20% of each run, Pallas kernels for 0% -> 0%
where the time goes in v1:
time: 163 us; the launch traced here: 162 us
  blocking collectives  58.4 us (36%)
  matrix products  29.6 us (18%)
  other arithmetic  25.4 us (16%)
  waiting for transfers between devices  20.5 us (13%)
  between operations  14.9 us (9%)
  starting transfers between devices  11.6 us (7%)
    all_to_all x1, blocking collectives, per_device(): lax.all_to_all(outgoing, 'expert', split_axis=0, concat_axis=0, tiled=True)  58.4 us
    all_to_all x1, waiting for transfers between devices, per_device(): lax.all_to_all(results, 'expert', split_axis=0, concat_axis=0, tiled=True)  16.6 us
    another operation x3, other arithmetic, per_device(): jnp.linalg.cholesky(corner + damping * jnp.eye(PANEL, dtype=jnp.float32))  12.4 us
    another operation x2, other arithmetic, per_device(): jax.scipy.linalg.solve_triangular(lower_factor, leading.T, lower=True)  10.5 us
    dot_general x1, matrix products, swiglu_rows(): jnp.dot(hidden, down_matrix, preferred_element_type=jnp.float32)  8.2 us
    ppermute x3, starting transfers between devices, per_device(): pack_sum = pack_sum + lax.ppermute(pack, 'pair', ring)  6.57 us
    all_to_all x1, starting transfers between devices, per_device(): lax.all_to_all(results, 'expert', split_axis=0, concat_axis=0, tiled=True)  5 us
    dot_general x1, matrix products, swiglu_rows(): jnp.dot(flat_rows, upper_matrix, preferred_element_type=jnp.float32)  4.32 us
  transfers between devices with their start and end apart: 5, of which 3 were waited for; matrix products, arithmetic and copies ran while one was open for 20% of the time, Pallas kernels for 0%

profile of v1, /device:TPU:0, one launch (start us, length us, event | category | flops | bytes accessed | tf_op | source)
XLA Modules:
  0.0 162.1 jit_solution(1576770460953862837)
XLA Ops:
  7.2 0.8 add_select_fusion
  8.0 0.7 fusion.38
  9.4 1.2 convolution_convert_fusion
  10.7 58.4 %all_to_all.10 = bf16[32,16,4096]{2,1,0:T(8,128)(2,1)S(1)} all-to-all(bf16[32,16,4096]{2,1,0:T(8,128)(2,1)S(1)} %bitcast.55), channel_id=1, replica_groups=mesh['expert'=32,'pair'=4] {'expert'}, dimensions={0} | all-to-all | bytes 8388608 | tf_op jit(solution)/shard_map/all_to_all | solution.py:50
  69.1 3.4 %fusion.4 = f32[512,768]{1,0:T(8,128)S(1)} fusion(bf16[512,4096]{1,0:T(8,128)(2,1)S(1)} %bitcast.57, bf16[1,4096,768]{2,1,0:T(8,128)(2,1)S(1)} %bitcast.61), kind=kOutput, calls=%fused_computation.4 | convolution fusion | flops 3221225472 | bytes 12058624 | tf_op jit(solution)/shard_map/dot_general | solution.py:13
  72.6 4.3 %multiply_reduce_fusion = (f32[]{:T(128)}, bf16[512,768]{1,0:T(8,128)(2,1)S(1)}) fusion(bf16[512,4096]{1,0:T(8,128)(2,1)S(1)} %bitcast.58, bf16[1,4096,768]{2,1,0:T(8,128)(2,1)S(1)} %bitcast.63, f32[512,768]{1,0:T(8,128)S(1)} %fusion.4), kind=kOutput, calls=%fused_computation.12 | convolution fusion | flops 3224764416 | bytes 12845060 | tf_op jit(solution)/shard_map/dot_general | solution.py:14
  76.9 8.2 %fusion.6 = bf16[512,4096]{1,0:T(8,128)(2,1)} fusion(bf16[512,768]{1,0:T(8,128)(2,1)S(1)} %get-tuple-element.6, bf16[1,768,4096]{2,1,0:T(8,128)(2,1)} %param.11), kind=kOutput, calls=%fused_computation.7 | convolution fusion | flops 3223322624 | bytes 11272192 | tf_op jit(solution)/shard_map/dot_general | solution.py:16
  85.1 5.0 %all-to-all-start.1 = ((bf16[32,16,4096]{2,1,0:T(8,128)(2,1)}), bf16[32,16,4096]{2,1,0:T(8,128)(2,1)}, u32[]{:S(2)}, u32[]{:S(2)}) async-start(bf16[32,16,4096]{2,1,0:T(8,128)(2,1)} %bitcast.56), calls=%async_computation.1 | async-start | bytes 8388608 | tf_op jit(solution)/shard_map/all_to_all | solution.py:56
  90.1 0.7 all-gather.2.cloned.1.call-update
  90.9 1.2 fusion.19
  92.7 2.0 %collective-permute-start = (f32[136,128]{1,0:T(8,128)S(1)}, f32[136,128]{1,0:T(8,128)S(1)}, u32[]{:S(2)}, u32[]{:S(2)}) collective-permute-start(f32[136,128]{1,0:T(8,128)S(1)} %concatenate.3), channel_id=1, source_target_pairs={{0,1},{1,2},{2,3},{3,0},{4,5},{5,6},{6,7},{7,4},{8,9},{9,10},{10,1... | collective-permute-start | bytes 208904 | tf_op jit(solution)/shard_map/ppermute | solution.py:79
  94.7 3.6 %collective-permute-start.1 = (f32[136,128]{1,0:T(8,128)S(1)}, f32[136,128]{1,0:T(8,128)S(1)}, u32[]{:S(2)}, u32[]{:S(2)}) collective-permute-start(f32[136,128]{1,0:T(8,128)S(1)} %concatenate.3), channel_id=1, source_target_pairs={{0,2},{1,3},{2,0},{3,1},{4,6},{5,7},{6,4},{7,5},{8,10},{9,11},{10,... | collective-permute-start | bytes 208904 | tf_op jit(solution)/shard_map/ppermute | solution.py:79
  98.3 1.0 collective-permute-start.2
  99.3 2.6 %collective-permute-done.1 = f32[136,128]{1,0:T(8,128)S(1)} collective-permute-done((f32[136,128]{1,0:T(8,128)S(1)}, f32[136,128]{1,0:T(8,128)S(1)}, u32[]{:S(2)}, u32[]{:S(2)}) %collective-permute-start.1) | collective-permute-done | bytes 69664 | tf_op jit(solution)/shard_map/ppermute | solution.py:79
  102.0 0.7 collective-permute-done.2
  102.6 0.7 add_add_fusion
  104.6 11.7 %cholesky.16 = f32[128,128]{1,0:T(8,128)S(1)} custom-call(f32[128,128]{1,0:T(8,128)S(1)} %fusion.34), custom_call_target="Cholesky" | custom-call | tf_op jit(solution)/shard_map/jit(cholesky)/cholesky | solution.py:82
  117.0 0.7 fusion.31
  117.7 9.8 %custom-call.7 = f32[1,128,128]{1,2,0:T(8,128)S(1)} custom-call(f32[1,128,128]{2,1,0:T(8,128)S(1)} %fusion.31), custom_call_target="InvertDiagBlocksLowerTriangular" | custom-call | tf_op jit(solution)/shard_map/jit(_solve_triangular)/triangular_solve | solution.py:94
  127.5 16.6 %all-to-all-done.1 = bf16[32,16,4096]{2,1,0:T(8,128)(2,1)} async-done(((bf16[32,16,4096]{2,1,0:T(8,128)(2,1)}), bf16[32,16,4096]{2,1,0:T(8,128)(2,1)}, u32[]{:S(2)}, u32[]{:S(2)}) %all-to-all-start.1) | async-done | bytes 4194336 | tf_op jit(solution)/shard_map/all_to_all | solution.py:56
  144.0 2.9 %convolution_bitcast_fusion = f32[128,4096]{1,0:T(8,128)S(1)} fusion(bf16[32,16,4096]{2,1,0:T(8,128)(2,1)} %all-to-all-done.1, f32[128,32]{0,1:T(8,128)S(1)} %fusion.18, s32[128,32]{0,1:T(8,128)S(1)} %copy.35, s32[128,32]{0,1:T(8,128)S(1)} %copy.33), kind=kOutput, calls=%fused_computation.8 | convolution fusion | flops 537395200 | bytes 6340608 | tf_op jit(solution)/shard_map/dot_general | solution.py:63
  147.0 3.9 %fusion.10 = bf16[128,4096]{1,0:T(8,128)(2,1)} fusion(f32[128,4096]{1,0:T(8,128)S(1)} %convolution_bitcast_fusion, bf16[32,16,4096]{2,1,0:T(8,128)(2,1)} %all-to-all-done.1, f32[128,32]{0,1:T(8,128)S(1)} %fusion.18, s32[128,32]{0,1:T(8,128)S(1)} %copy.35, s32[128,32]{0,1:T(8,128)S(1)} %copy.33), kind=kOutput, calls=%fused_computation.11 | convolution fusion | flops 538247168 | bytes 7389184 | tf_op jit(solution)/shard_map/dot_general | solution.py:63
  150.9 3.4 %convolution_multiply_fusion = f32[192,768]{1,0:T(8,128)S(1)} fusion(bf16[2048,768]{1,0:T(8,128)(2,1)} %all-gather.2.cloned.1.call-done, s32[]{:T(128)S(6)} %select_n.21), kind=kOutput, calls=%fused_computation.14 | convolution fusion | flops 604127232 | bytes 4784132 | tf_op jit(solution)/shard_map/dot_general | solution.py:86
  154.3 0.9 convolution_bitcast_fusion.2
  (39 shorter events, 2.8 us)
Async XLA Ops:
  7.2 2.2 %copy-start = (bf16[128,4096]{1,0:T(8,128)(2,1)S(1)}, bf16[128,4096]{1,0:T(8,128)(2,1)}, u32[]{:S(2)}) copy-start(bf16[128,4096]{1,0:T(8,128)(2,1)} %param.6) | copy-start | bytes 3145732
  9.4 59.7 %slice-start = ((s8[6291456]{0:T(1024)(128)(4,1)}), s8[4194304]{0:T(1024)(128)(4,1)S(1)}, s32[]{:S(2)}) async-start(s8[6291456]{0:T(1024)(128)(4,1)} %bitcast.60), calls=%async_computation.3 | async-start | bytes 8388608
  10.6 58.4 %slice-start.1 = ((s8[6291456]{0:T(1024)(128)(4,1)}), s8[2097152]{0:T(1024)(128)(4,1)S(1)}, s32[]{:S(2)}) async-start(s8[6291456]{0:T(1024)(128)(4,1)} %bitcast.60), calls=%async_computation.4 | async-start | bytes 4194304
  10.7 61.9 %slice-start.2 = ((s8[6291456]{0:T(1024)(128)(4,1)}), s8[4194304]{0:T(1024)(128)(4,1)S(1)}, s32[]{:S(2)}) async-start(s8[6291456]{0:T(1024)(128)(4,1)} %bitcast.62), calls=%async_computation.5 | async-start | bytes 8388608
  69.1 3.5 %slice-start.3 = ((s8[6291456]{0:T(1024)(128)(4,1)}), s8[2097152]{0:T(1024)(128)(4,1)S(1)}, s32[]{:S(2)}) async-start(s8[6291456]{0:T(1024)(128)(4,1)} %bitcast.62), calls=%async_computation.6 | async-start | bytes 4194304
  76.9 8.2 %copy-start.1 = (bf16[512,768]{1,0:T(8,128)(2,1)}, bf16[512,768]{1,0:T(8,128)(2,1)S(1)}, u32[]{:S(2)}) copy-start(bf16[512,768]{1,0:T(8,128)(2,1)S(1)} %get-tuple-element.6) | copy-start | bytes 2359300
  85.1 5.8 %copy-start.3 = (f32[128,8]{0,1:T(8,128)S(1)}, f32[128,8]{0,1:T(8,128)}, u32[]{:S(2)}) copy-start(f32[128,8]{0,1:T(8,128)} %param.8) | copy-start | bytes 12292
  85.1 59.0 %all-to-all-start.1 = ((bf16[32,16,4096]{2,1,0:T(8,128)(2,1)}), bf16[32,16,4096]{2,1,0:T(8,128)(2,1)}, u32[]{:S(2)}, u32[]{:S(2)}) async-start(bf16[32,16,4096]{2,1,0:T(8,128)(2,1)} %bitcast.56), calls=%async_computation.1 | async-start | bytes 8388608 | tf_op jit(solution)/shard_map/all_to_all | solution.py:56
  90.1 60.8 %all-gather.2.cloned.1.call-start = ((), (), s32[]{:S(2)}) async-start(), calls=%async_computation.2 | async-start | bytes 3932160 | tf_op jit(solution)/shard_map/all_gather | solution.py:83
  92.7 6.6 %collective-permute-start = (f32[136,128]{1,0:T(8,128)S(1)}, f32[136,128]{1,0:T(8,128)S(1)}, u32[]{:S(2)}, u32[]{:S(2)}) collective-permute-start(f32[136,128]{1,0:T(8,128)S(1)} %concatenate.3), channel_id=1, source_target_pairs={{0,1},{1,2},{2,3},{3,0},{4,5},{5,6},{6,7},{7,4},{8,9},{9,10},{10,1... | collective-permute-start | bytes 208904 | tf_op jit(solution)/shard_map/ppermute | solution.py:79
  94.7 7.2 %collective-permute-start.1 = (f32[136,128]{1,0:T(8,128)S(1)}, f32[136,128]{1,0:T(8,128)S(1)}, u32[]{:S(2)}, u32[]{:S(2)}) collective-permute-start(f32[136,128]{1,0:T(8,128)S(1)} %concatenate.3), channel_id=1, source_target_pairs={{0,2},{1,3},{2,0},{3,1},{4,6},{5,7},{6,4},{7,5},{8,10},{9,11},{10,... | collective-permute-start | bytes 208904 | tf_op jit(solution)/shard_map/ppermute | solution.py:79
  98.3 4.3 %collective-permute-start.2 = (f32[136,128]{1,0:T(8,128)S(1)}, f32[136,128]{1,0:T(8,128)S(1)}, u32[]{:S(2)}, u32[]{:S(2)}) collective-permute-start(f32[136,128]{1,0:T(8,128)S(1)} %concatenate.3), channel_id=1, source_target_pairs={{0,3},{1,0},{2,1},{3,2},{4,7},{5,4},{6,5},{7,6},{8,11},{9,8},{10,9... | collective-permute-start | bytes 208904 | tf_op jit(solution)/shard_map/ppermute | solution.py:79
  154.3 1.0 copy-start.2
Sparse Core Ops, SparseCore 0:
  92.6 42.1 all-gather.1

commit v2 on v1

v2 whole, which is shorter than its diff:
```python
import jax
import jax.numpy as jnp
from jax import lax
from jax.sharding import PartitionSpec as P

EXPERTS = 128
FF = 768
PANEL = 128
CAP = 16
CHUNKS = 2


def swiglu_rows(flat_rows, gate_matrix, upper_matrix, down_matrix):
    gate_value = jnp.dot(flat_rows, gate_matrix, preferred_element_type=jnp.float32)
    upper_value = jnp.dot(flat_rows, upper_matrix, preferred_element_type=jnp.float32)
    hidden = (jax.nn.silu(gate_value) * upper_value).astype(jnp.bfloat16)
    output = jnp.dot(hidden, down_matrix, preferred_element_type=jnp.float32).astype(jnp.bfloat16)
    return (hidden, output)


def split_bf16(values):
    rounded = lax.reduce_precision(values, exponent_bits=8, mantissa_bits=7)
    return rounded.astype(jnp.bfloat16), (values - rounded).astype(jnp.bfloat16)


def per_device(tokens, expert_ids, route_weight, gate_weight, up_weight, down_weight):
    owners = lax.axis_size("expert")
    pair_count = lax.axis_size("pair")
    tok_count = tokens.shape[0]
    model_width = tokens.shape[1]
    per_owner = EXPERTS // owners
    in_flight = expert_ids % per_owner == 0
    owner_of = expert_ids // per_owner
    columns = lax.broadcasted_iota(jnp.int32, (1, 1, owners), 2)
    route_hit = (in_flight[:, :, None] & (owner_of[:, :, None] == columns)).astype(jnp.int32)
    picked = jnp.sum(route_hit, axis=1)
    before = jnp.cumsum(picked, axis=0) - picked
    kept_rows = picked * (before < CAP).astype(jnp.int32)
    slot_ids = lax.broadcasted_iota(jnp.int32, (1, 1, CAP), 2)
    slot_marks = kept_rows[:, :, None] * (before[:, :, None] == slot_ids).astype(jnp.int32)
    gate_matrix = gate_weight[0]
    upper_matrix = up_weight[0]
    down_matrix = down_weight[0]
    owner_weight = jnp.sum(route_hit.astype(jnp.float32) * route_weight[:, :, None], axis=1)
    combine_weights = slot_marks.astype(jnp.float32) * owner_weight[:, :, None]
    chunk = CAP // CHUNKS
    combined = jnp.zeros((tok_count, model_width), jnp.float32)
    hidden_parts = []
    for part in range(CHUNKS):
        marks_part = slot_marks[:, :, part * chunk : (part + 1) * chunk]
        selector = marks_part.reshape(tok_count, owners * chunk).astype(jnp.bfloat16)
        outgoing = lax.dot_general(
            selector, tokens, (((0,), (0,)), ((), ())), preferred_element_type=jnp.float32
        ).astype(jnp.bfloat16)
        outgoing = outgoing.reshape(owners, chunk, model_width)
        arrived = lax.all_to_all(outgoing, "expert", split_axis=0, concat_axis=0, tiled=True)
        hidden, output = swiglu_rows(
            arrived.reshape(-1, model_width), gate_matrix, upper_matrix, down_matrix
        )
        hidden_parts.append(hidden)
        results = output.reshape(owners, chunk, model_width)
        returned = lax.all_to_all(results, "expert", split_axis=0, concat_axis=0, tiled=True)
        returned_flat = returned.reshape(-1, model_width)
        weights_part = combine_weights[:, :, part * chunk : (part + 1) * chunk]
        weight_high, weight_low = split_bf16(weights_part.reshape(tok_count, owners * chunk))
        combined = combined + jnp.dot(
            weight_high, returned_flat, preferred_element_type=jnp.float32
        ) + jnp.dot(weight_low, returned_flat, preferred_element_type=jnp.float32)
    hess_scale = 2.0 / (CAP * owners * pair_count)
    row_share = FF // pair_count
    pair_place = lax.axis_index("pair")
    corner_part = jnp.zeros((PANEL, PANEL), jnp.float32)
    square_sum = jnp.zeros((), jnp.float32)
    for hidden in hidden_parts:
        hidden_wide = hidden.astype(jnp.float32)
        corner_part = corner_part + lax.dot_general(
            hidden[:, :PANEL], hidden[:, :PANEL], (((0,), (0,)), ((), ())),
            preferred_element_type=jnp.float32,
        )
        square_sum = square_sum + jnp.sum(hidden_wide * hidden_wide)
    square_part = jnp.broadcast_to(square_sum, (8, PANEL))
    pack = jnp.concatenate([corner_part, square_part], axis=0)
    pack_sum = pack
    for shift in range(1, pair_count):
        ring = [(i, (i + shift) % pair_count) for i in range(pair_count)]
        pack_sum = pack_sum + lax.ppermute(pack, "pair", ring)
    corner = pack_sum[:PANEL] * hess_scale
    damping = 0.01 * (pack_sum[PANEL, 0] * hess_scale) / FF
    lower_factor = jnp.linalg.cholesky(corner + damping * jnp.eye(PANEL, dtype=jnp.float32))
    row_sum = jnp.zeros((row_share, FF), jnp.float32)
    for hidden in hidden_parts:
        all_hidden = lax.all_gather(hidden, "pair", axis=0, tiled=True)
        my_columns = lax.dynamic_slice_in_dim(all_hidden, pair_place * row_share, row_share, 1)
        row_sum = row_sum + lax.dot_general(
            my_columns, all_hidden, (((0,), (0,)), ((), ())), preferred_element_type=jnp.float32
        )
    my_rows = row_sum * hess_scale
    row_ids = pair_place * row_share + lax.broadcasted_iota(jnp.int32, (row_share, PANEL), 0)
    column_ids = lax.broadcasted_iota(jnp.int32, (row_share, PANEL), 1)
    leading = my_rows[:, :PANEL] + damping * (row_ids == column_ids).astype(jnp.float32)
    panel_rows = jax.scipy.linalg.solve_triangular(lower_factor, leading.T, lower=True).T
    return (combined.astype(jnp.bfloat16), my_rows[None], panel_rows[None])


def solution(mesh):
    in_specs = (
        P(("expert", "pair"), None),
        P(("expert", "pair"), None),
        P(("expert", "pair"), None),
        P("expert", None, None),
        P("expert", None, None),
        P("expert", None, None),
    )
    out_specs = (P(("expert", "pair"), None), P("expert", "pair", None), P("expert", "pair", None))
    return jax.shard_map(
        per_device, mesh=mesh, in_specs=in_specs, out_specs=out_specs, check_vma=False
    )
```

time: 163 us -> 195 us (1.20)
  blocking collectives: 58.4 us -> 0 us
  waiting for transfers between devices: 20.5 us -> 58 us
  matrix products: 29.6 us -> 59.1 us
  starting transfers between devices: 11.6 us -> 26.4 us
  local copies, waits for them, and re-layouts: 1.63 us -> 6.27 us
  other arithmetic: 25.4 us -> 27.7 us
    all_to_all x1 -> x0, blocking collectives: 58.4 us -> none  [per_device(): lax.all_to_all(outgoing, 'expert', split_axis=0, concat_axis=0, tiled=True)]
    all_to_all x0 -> x2, waiting for transfers between devices: none -> 41.2 us  [per_device(): lax.all_to_all(outgoing, 'expert', split_axis=0, concat_axis=0, tiled=True)]
    all_to_all x0 -> x2, starting transfers between devices: none -> 11.4 us  [per_device(): lax.all_to_all(outgoing, 'expert', split_axis=0, concat_axis=0, tiled=True)]
    dot_general x1 -> x2, matrix products: 3.43 us -> 10.7 us  [swiglu_rows(): jnp.dot(flat_rows, gate_matrix, preferred_element_type=jnp.float32)]
    dot_general x1 -> x2, matrix products: 4.32 us -> 11.5 us  [swiglu_rows(): jnp.dot(flat_rows, upper_matrix, preferred_element_type=jnp.float32)]
    all_to_all x1 -> x2, waiting for transfers between devices: 16.6 us -> 12.2 us  [per_device(): lax.all_to_all(results, 'expert', split_axis=0, concat_axis=0, tiled=True)]
    dot_general x1 -> x2, matrix products: 8.2 us -> 12.1 us  [swiglu_rows(): jnp.dot(hidden, down_matrix, preferred_element_type=jnp.float32)]
    unnamed x16 -> x34, local copies, waits for them, and re-layouts: 0.05 us -> 3.95 us
  transfers between devices with their start and end apart: 5 -> 9, of which waited for: 3 -> 6; matrix products, arithmetic and copies ran while one was open for 20% -> 42% of each run, Pallas kernels for 0% -> 0%
where the time goes in v2:
time: 195 us; the launch traced here: 194 us
  matrix products  59.1 us (30%)
  waiting for transfers between devices  58 us (30%)
  other arithmetic  27.7 us (14%)
  starting transfers between devices  26.4 us (14%)
  between operations  16.3 us (8%)
  local copies, waits for them, and re-layouts  6.27 us (3%)
    all_to_all x2, waiting for transfers between devices, per_device(): lax.all_to_all(outgoing, 'expert', split_axis=0, concat_axis=0, tiled=True)  41.2 us
    another operation x3, other arithmetic, per_device(): jnp.linalg.cholesky(corner + damping * jnp.eye(PANEL, dtype=jnp.float32))  13.2 us
    all_to_all x2, waiting for transfers between devices, per_device(): lax.all_to_all(results, 'expert', split_axis=0, concat_axis=0, tiled=True)  12.2 us
    dot_general x2, matrix products, swiglu_rows(): jnp.dot(hidden, down_matrix, preferred_element_type=jnp.float32)  12.1 us
    dot_general x2, matrix products, swiglu_rows(): jnp.dot(flat_rows, upper_matrix, preferred_element_type=jnp.float32)  11.5 us
    all_to_all x2, starting transfers between devices, per_device(): lax.all_to_all(outgoing, 'expert', split_axis=0, concat_axis=0, tiled=True)  11.4 us
    dot_general x2, matrix products, swiglu_rows(): jnp.dot(flat_rows, gate_matrix, preferred_element_type=jnp.float32)  10.7 us
    another operation x2, other arithmetic, per_device(): jax.scipy.linalg.solve_triangular(lower_factor, leading.T, lower=True)  10.5 us
  transfers between devices with their start and end apart: 9, of which 6 were waited for; matrix products, arithmetic and copies ran while one was open for 42% of the time, Pallas kernels for 0%

profile of v2, /device:TPU:0, one launch (start us, length us, event | category | flops | bytes accessed | tf_op | source)
XLA Modules:
  0.0 193.8 jit_solution(17012811306188812851)
XLA Ops:
  10.4 2.0 %fusion.25 = bf16[32,8,4096]{2,1,0:T(8,128)(2,1)} fusion(bf16[128,4096]{1,0:T(8,128)(2,1)S(1)} %copy-done, bf16[128,32,8]{0,1,2:T(8,128)(2,1)S(1)} %get-tuple-element.6), kind=kOutput, calls=%fused_computation.19 | convolution fusion | flops 269484032 | bytes 3211264 | tf_op jit(solution)/shard_map/dot_general | solution.py:52
  12.4 7.4 %all-to-all-start.2 = ((bf16[32,8,4096]{2,1,0:T(8,128)(2,1)}), bf16[32,8,4096]{2,1,0:T(8,128)(2,1)S(1)}, u32[]{:S(2)}, u32[]{:S(2)}) async-start(bf16[32,8,4096]{2,1,0:T(8,128)(2,1)} %fusion.25), calls=%async_computation.2 | async-start | bytes 4194304 | tf_op jit(solution)/shard_map/all_to_all | solution.py:56
  21.9 28.0 %all-to-all-done.2 = bf16[32,8,4096]{2,1,0:T(8,128)(2,1)S(1)} async-done(((bf16[32,8,4096]{2,1,0:T(8,128)(2,1)}), bf16[32,8,4096]{2,1,0:T(8,128)(2,1)S(1)}, u32[]{:S(2)}, u32[]{:S(2)}) %all-to-all-start.2) | async-done | bytes 2097184 | tf_op jit(solution)/shard_map/all_to_all | solution.py:56
  51.3 4.0 %all-to-all-start = ((bf16[32,8,4096]{2,1,0:T(8,128)(2,1)}), bf16[32,8,4096]{2,1,0:T(8,128)(2,1)S(1)}, u32[]{:S(2)}, u32[]{:S(2)}) async-start(bf16[32,8,4096]{2,1,0:T(8,128)(2,1)} %fusion.24), calls=%async_computation | async-start | bytes 4194304 | tf_op jit(solution)/shard_map/all_to_all | solution.py:56
  55.3 5.3 %fusion.8 = f32[256,768]{1,0:T(8,128)S(1)} fusion(bf16[1,4096,768]{2,1,0:T(8,128)(2,1)} %param.9, bf16[32,8,4096]{2,1,0:T(8,128)(2,1)} %copy-done.5), kind=kOutput, calls=%fused_computation.8 | convolution fusion | flops 1610612736 | bytes 9175040 | tf_op jit(solution)/shard_map/dot_general | solution.py:14
  60.7 5.4 %multiply_reduce_fusion = (f32[]{:T(128)}, bf16[256,768]{1,0:T(8,128)(2,1)S(1)}) fusion(bf16[1,4096,768]{2,1,0:T(8,128)(2,1)} %param.10, bf16[32,8,4096]{2,1,0:T(8,128)(2,1)S(1)} %copy-done.6, f32[256,768]{1,0:T(8,128)S(1)} %fusion.8), kind=kOutput, calls=%fused_computation.44 | convolution fusion | flops 1612382208 | bytes 9568260 | tf_op jit(solution)/shard_map/dot_general | solution.py:15
  66.1 6.1 %fusion.18 = bf16[32,8,4096]{2,1,0:T(8,128)(2,1)} fusion(bf16[256,768]{1,0:T(8,128)(2,1)S(1)} %get-tuple-element.10, bf16[1,768,4096]{2,1,0:T(8,128)(2,1)} %param.11), kind=kOutput, calls=%fused_computation.16 | convolution fusion | flops 1611661312 | bytes 8781824 | tf_op jit(solution)/shard_map/dot_general | solution.py:17
  72.2 13.2 %all-to-all-done = bf16[32,8,4096]{2,1,0:T(8,128)(2,1)S(1)} async-done(((bf16[32,8,4096]{2,1,0:T(8,128)(2,1)}), bf16[32,8,4096]{2,1,0:T(8,128)(2,1)S(1)}, u32[]{:S(2)}, u32[]{:S(2)}) %all-to-all-start) | async-done | bytes 2097184 | tf_op jit(solution)/shard_map/all_to_all | solution.py:56
  86.7 4.0 %all-to-all-start.3 = ((bf16[32,8,4096]{2,1,0:T(8,128)(2,1)}), bf16[32,8,4096]{2,1,0:T(8,128)(2,1)S(1)}, u32[]{:S(2)}, u32[]{:S(2)}) async-start(bf16[32,8,4096]{2,1,0:T(8,128)(2,1)} %fusion.18), calls=%async_computation.3 | async-start | bytes 4194304 | tf_op jit(solution)/shard_map/all_to_all | solution.py:62
  91.0 5.3 %fusion.10 = f32[256,768]{1,0:T(8,128)S(1)} fusion(bf16[1,4096,768]{2,1,0:T(8,128)(2,1)} %param.9, bf16[32,8,4096]{2,1,0:T(8,128)(2,1)} %copy-done.3), kind=kOutput, calls=%fused_computation.10 | convolution fusion | flops 1610612736 | bytes 9175040 | tf_op jit(solution)/shard_map/dot_general | solution.py:14
  96.4 6.0 %multiply_reduce_fusion.1 = (f32[]{:T(128)}, bf16[256,768]{1,0:T(8,128)(2,1)}) fusion(bf16[1,4096,768]{2,1,0:T(8,128)(2,1)} %param.10, bf16[32,8,4096]{2,1,0:T(8,128)(2,1)S(1)} %copy-done.4, f32[256,768]{1,0:T(8,128)S(1)} %fusion.10), kind=kOutput, calls=%fused_computation.45 | convolution fusion | flops 1612382208 | bytes 9568260 | tf_op jit(solution)/shard_map/dot_general | solution.py:15
  102.6 6.1 %fusion.21 = bf16[32,8,4096]{2,1,0:T(8,128)(2,1)} fusion(bf16[256,768]{1,0:T(8,128)(2,1)} %get-tuple-element.8, bf16[1,768,4096]{2,1,0:T(8,128)(2,1)} %param.11), kind=kOutput, calls=%fused_computation.17 | convolution fusion | flops 1611661312 | bytes 8781824 | tf_op jit(solution)/shard_map/dot_general | solution.py:17
  108.6 12.2 %all-to-all-done.3 = bf16[32,8,4096]{2,1,0:T(8,128)(2,1)S(1)} async-done(((bf16[32,8,4096]{2,1,0:T(8,128)(2,1)}), bf16[32,8,4096]{2,1,0:T(8,128)(2,1)S(1)}, u32[]{:S(2)}, u32[]{:S(2)}) %all-to-all-start.3) | async-done | bytes 2097184 | tf_op jit(solution)/shard_map/all_to_all | solution.py:62
  120.8 4.8 %all-to-all-start.1 = ((bf16[32,8,4096]{2,1,0:T(8,128)(2,1)}), bf16[32,8,4096]{2,1,0:T(8,128)(2,1)}, u32[]{:S(2)}, u32[]{:S(2)}) async-start(bf16[32,8,4096]{2,1,0:T(8,128)(2,1)} %fusion.21), calls=%async_computation.1 | async-start | bytes 4194304 | tf_op jit(solution)/shard_map/all_to_all | solution.py:62
  129.8 3.9 %collective-permute-start.1 = (f32[136,128]{1,0:T(8,128)}, f32[136,128]{1,0:T(8,128)S(1)}, u32[]{:S(2)}, u32[]{:S(2)}) collective-permute-start(f32[136,128]{1,0:T(8,128)} %concatenate.3), channel_id=1, source_target_pairs={{0,2},{1,3},{2,0},{3,1},{4,6},{5,7},{6,4},{7,5},{8,10},{9,11},{10,... | collective-permute-start | bytes 208904 | tf_op jit(solution)/shard_map/ppermute | solution.py:86
  136.3 2.3 %collective-permute-done.2 = f32[136,128]{1,0:T(8,128)} collective-permute-done((f32[136,128]{1,0:T(8,128)}, f32[136,128]{1,0:T(8,128)}, u32[]{:S(2)}, u32[]{:S(2)}) %collective-permute-start.2) | collective-permute-done | bytes 69664 | tf_op jit(solution)/shard_map/ppermute | solution.py:86
  144.6 12.6 %cholesky.16 = f32[128,128]{1,0:T(8,128)S(1)} custom-call(f32[128,128]{1,0:T(8,128)} %fusion.77), custom_call_target="Cholesky" | custom-call | tf_op jit(solution)/shard_map/jit(cholesky)/cholesky | solution.py:89
  158.5 9.8 %custom-call.7 = f32[1,128,128]{1,2,0:T(8,128)S(1)} custom-call(f32[1,128,128]{2,1,0:T(8,128)S(1)} %fusion.69), custom_call_target="InvertDiagBlocksLowerTriangular" | custom-call | tf_op jit(solution)/shard_map/jit(_solve_triangular)/triangular_solve | solution.py:101
  168.3 2.8 %convolution_bitcast_fusion.1 = f32[128,4096]{1,0:T(8,128)} fusion(bf16[32,8,4096]{2,1,0:T(8,128)(2,1)S(1)} %all-to-all-done.3, f32[128,32,16]{0,1,2:T(8,128)S(1)} %fusion.62), kind=kOutput, calls=%fused_computation.21 | convolution fusion | flops 268500992 | bytes 4325376 | tf_op jit(solution)/shard_map/dot_general | solution.py:66
  171.1 2.8 %convolution_bitcast_fusion = f32[128,4096]{1,0:T(8,128)} fusion(bf16[32,8,4096]{2,1,0:T(8,128)(2,1)S(1)} %all-to-all-done.3, f32[128,32,16]{0,1,2:T(8,128)S(1)} %fusion.62), kind=kOutput, calls=%fused_computation.20 | convolution fusion | flops 268533760 | bytes 4325376 | tf_op jit(solution)/shard_map/dot_general | solution.py:68
  173.9 3.2 %convolution_bitcast_fusion.2 = f32[128,4096]{1,0:T(8,128)S(1)} fusion(bf16[32,8,4096]{2,1,0:T(8,128)(2,1)} %all-to-all-done.1, f32[128,32,16]{0,1,2:T(8,128)S(1)} %fusion.62), kind=kOutput, calls=%fused_computation.22 | convolution fusion | flops 268533760 | bytes 4325376 | tf_op jit(solution)/shard_map/dot_general | solution.py:68
  177.0 4.3 %fusion.29 = bf16[128,4096]{1,0:T(8,128)(2,1)} fusion(f32[128,4096]{1,0:T(8,128)S(1)} %copy-done.2, f32[128,4096]{1,0:T(8,128)S(1)} %copy-done.1, f32[128,4096]{1,0:T(8,128)S(1)} %convolution_bitcast_fusion.2, bf16[32,8,4096]{2,1,0:T(8,128)(2,1)} %all-to-all-done.1, f32[128,32,16]{0,1,2:T(8,128)S(1)} %fusion.62), kind=kOutput, calls=%fused_computation.27 | convolution fusion | flops 270598144 | bytes 9568256 | tf_op jit(solution)/shard_map/dot_general | solution.py:66
  181.3 2.3 %fusion.60 = f32[192,768]{1,0:T(8,128)S(1)} fusion(bf16[1024,768]{1,0:T(8,128)(2,1)} %all-gather.3.cloned.1.call-done, s32[]{:T(128)S(6)} %select_n.22), kind=kOutput, calls=%fused_computation.47 | convolution fusion | flops 301989888 | bytes 2686980 | tf_op jit(solution)/shard_map/dot_general | solution.py:94
  183.7 2.3 %fusion.58 = f32[192,768]{1,0:T(8,128)S(1)} fusion(f32[192,768]{1,0:T(8,128)S(1)} %fusion.60, bf16[1024,768]{1,0:T(8,128)(2,1)} %all-gather.5.cloned.1.call-done, s32[]{:T(128)S(6)} %select_n.22), kind=kOutput, calls=%fused_computation.41 | convolution fusion | flops 302284800 | bytes 3276804 | tf_op jit(solution)/shard_map/dot_general | solution.py:94
  (71 shorter events, 21.3 us)
Async XLA Ops:
  7.2 3.2 %copy-start = (bf16[128,4096]{1,0:T(8,128)(2,1)S(1)}, bf16[128,4096]{1,0:T(8,128)(2,1)}, u32[]{:S(2)}) copy-start(bf16[128,4096]{1,0:T(8,128)(2,1)} %param.6) | copy-start | bytes 3145732
  8.0 0.7 copy-start.14
  12.4 37.5 %all-to-all-start.2 = ((bf16[32,8,4096]{2,1,0:T(8,128)(2,1)}), bf16[32,8,4096]{2,1,0:T(8,128)(2,1)S(1)}, u32[]{:S(2)}, u32[]{:S(2)}) async-start(bf16[32,8,4096]{2,1,0:T(8,128)(2,1)} %fusion.25), calls=%async_computation.2 | async-start | bytes 4194304 | tf_op jit(solution)/shard_map/all_to_all | solution.py:56
  49.9 1.3 copy-start.5
  51.3 34.1 %all-to-all-start = ((bf16[32,8,4096]{2,1,0:T(8,128)(2,1)}), bf16[32,8,4096]{2,1,0:T(8,128)(2,1)S(1)}, u32[]{:S(2)}, u32[]{:S(2)}) async-start(bf16[32,8,4096]{2,1,0:T(8,128)(2,1)} %fusion.24), calls=%async_computation | async-start | bytes 4194304 | tf_op jit(solution)/shard_map/all_to_all | solution.py:56
  55.3 5.4 %copy-start.6 = (bf16[32,8,4096]{2,1,0:T(8,128)(2,1)S(1)}, bf16[32,8,4096]{2,1,0:T(8,128)(2,1)}, u32[]{:S(2)}) copy-start(bf16[32,8,4096]{2,1,0:T(8,128)(2,1)} %copy-done.5) | copy-start | bytes 6291460
  66.1 6.1 %copy-start.8 = (bf16[256,768]{1,0:T(8,128)(2,1)}, bf16[256,768]{1,0:T(8,128)(2,1)S(1)}, u32[]{:S(2)}) copy-start(bf16[256,768]{1,0:T(8,128)(2,1)S(1)} %get-tuple-element.10) | copy-start | bytes 1179652
  85.4 1.3 copy-start.3
  86.7 34.1 %all-to-all-start.3 = ((bf16[32,8,4096]{2,1,0:T(8,128)(2,1)}), bf16[32,8,4096]{2,1,0:T(8,128)(2,1)S(1)}, u32[]{:S(2)}, u32[]{:S(2)}) async-start(bf16[32,8,4096]{2,1,0:T(8,128)(2,1)} %fusion.18), calls=%async_computation.3 | async-start | bytes 4194304 | tf_op jit(solution)/shard_map/all_to_all | solution.py:62
  90.8 90.6 %all-gather.3.cloned.1.call-start = ((), (), s32[]{:S(2)}) async-start(), calls=%async_computation.4 | async-start | bytes 1966080 | tf_op jit(solution)/shard_map/all_gather | solution.py:92
  91.0 5.4 %copy-start.4 = (bf16[32,8,4096]{2,1,0:T(8,128)(2,1)S(1)}, bf16[32,8,4096]{2,1,0:T(8,128)(2,1)}, u32[]{:S(2)}) copy-start(bf16[32,8,4096]{2,1,0:T(8,128)(2,1)} %copy-done.3) | copy-start | bytes 6291460
  96.4 6.1 %copy-start.13 = (s32[128,8]{0,1:T(8,128)S(1)}, s32[128,8]{0,1:T(8,128)}, u32[]{:S(2)}) copy-start(s32[128,8]{0,1:T(8,128)} %copy-done.12) | copy-start | bytes 12292
  96.4 6.1 %copy-start.15 = (pred[128,8]{0,1:T(8,128)(4,1)S(1)}, pred[128,8]{0,1:T(8,128)(4,1)}, u32[]{:S(2)}) copy-start(pred[128,8]{0,1:T(8,128)(4,1)} %copy-done.14) | copy-start | bytes 3076
  96.4 6.1 %copy-start.16 = (f32[128,8]{0,1:T(8,128)S(1)}, f32[128,8]{0,1:T(8,128)}, u32[]{:S(2)}) copy-start(f32[128,8]{0,1:T(8,128)} %param.8) | copy-start | bytes 12292
  96.4 6.1 %copy-start.10 = (s32[128,32]{0,1:T(8,128)S(1)}, s32[128,32]{0,1:T(8,128)}, u32[]{:S(2)}) copy-start(s32[128,32]{0,1:T(8,128)} %copy-done.9) | copy-start | bytes 49156
  120.8 53.0 %all-to-all-start.1 = ((bf16[32,8,4096]{2,1,0:T(8,128)(2,1)}), bf16[32,8,4096]{2,1,0:T(8,128)(2,1)}, u32[]{:S(2)}, u32[]{:S(2)}) async-start(bf16[32,8,4096]{2,1,0:T(8,128)(2,1)} %fusion.21), calls=%async_computation.1 | async-start | bytes 4194304 | tf_op jit(solution)/shard_map/all_to_all | solution.py:62
  125.6 58.0 %all-gather.5.cloned.1.call-start = ((), (), s32[]{:S(2)}) async-start(), calls=%async_computation.5 | async-start | bytes 1966080 | tf_op jit(solution)/shard_map/all_gather | solution.py:92
  129.8 6.5 %collective-permute-start.1 = (f32[136,128]{1,0:T(8,128)}, f32[136,128]{1,0:T(8,128)S(1)}, u32[]{:S(2)}, u32[]{:S(2)}) collective-permute-start(f32[136,128]{1,0:T(8,128)} %concatenate.3), channel_id=1, source_target_pairs={{0,2},{1,3},{2,0},{3,1},{4,6},{5,7},{6,4},{7,5},{8,10},{9,11},{10,... | collective-permute-start | bytes 208904 | tf_op jit(solution)/shard_map/ppermute | solution.py:86
  133.7 5.0 %collective-permute-start.2 = (f32[136,128]{1,0:T(8,128)}, f32[136,128]{1,0:T(8,128)}, u32[]{:S(2)}, u32[]{:S(2)}) collective-permute-start(f32[136,128]{1,0:T(8,128)} %concatenate.3), channel_id=1, source_target_pairs={{0,3},{1,0},{2,1},{3,2},{4,7},{5,4},{6,5},{7,6},{8,11},{9,8},{10,9... | collective-permute-start | bytes 208904 | tf_op jit(solution)/shard_map/ppermute | solution.py:86
  134.4 5.8 %collective-permute-start = (f32[136,128]{1,0:T(8,128)}, f32[136,128]{1,0:T(8,128)}, u32[]{:S(2)}, u32[]{:S(2)}) collective-permute-start(f32[136,128]{1,0:T(8,128)} %concatenate.3), channel_id=1, source_target_pairs={{0,1},{1,2},{2,3},{3,0},{4,5},{5,6},{6,7},{7,4},{8,9},{9,10},{10,1... | collective-permute-start | bytes 208904 | tf_op jit(solution)/shard_map/ppermute | solution.py:86
  136.3 2.3 %copy-start.11 = (f32[136,128]{1,0:T(8,128)}, f32[136,128]{1,0:T(8,128)S(1)}, u32[]{:S(2)}) copy-start(f32[136,128]{1,0:T(8,128)S(1)} %collective-permute-done.1) | copy-start | bytes 208900
  173.9 3.2 %copy-start.1 = (f32[128,4096]{1,0:T(8,128)S(1)}, f32[128,4096]{1,0:T(8,128)}, u32[]{:S(2)}) copy-start(f32[128,4096]{1,0:T(8,128)} %convolution_bitcast_fusion.1) | copy-start | bytes 6291460
  173.9 3.2 %copy-start.2 = (f32[128,4096]{1,0:T(8,128)S(1)}, f32[128,4096]{1,0:T(8,128)}, u32[]{:S(2)}) copy-start(f32[128,4096]{1,0:T(8,128)} %convolution_bitcast_fusion) | copy-start | bytes 6291460
  186.0 1.0 copy-start.7
  (2 other events, 1.2 us)
Sparse Core Ops, SparseCore 0:
  102.6 29.1 all-gather.2
  135.9 27.0 all-gather.4

commit v3 on v1

--- a/solution.py
+++ b/solution.py
@@ -18,9 +18,8 @@
 
 
 def split_bf16(values):
-    high = values.astype(jnp.bfloat16)
-    low = (values - high.astype(jnp.float32)).astype(jnp.bfloat16)
-    return high, low
+    rounded = lax.reduce_precision(values, exponent_bits=8, mantissa_bits=7)
+    return rounded.astype(jnp.bfloat16), (values - rounded).astype(jnp.bfloat16)
 
 
 def per_device(tokens, expert_ids, route_weight, gate_weight, up_weight, down_weight):
@@ -80,7 +79,11 @@
     corner = pack_sum[:PANEL] * hess_scale
     damping = 0.01 * (pack_sum[PANEL, 0] * hess_scale) / FF
     lower_factor = jnp.linalg.cholesky(corner + damping * jnp.eye(PANEL, dtype=jnp.float32))
-    all_hidden = lax.all_gather(hidden, "pair", axis=0, tiled=True)
+    gathered = [hidden]
+    for shift in range(1, pair_count):
+        ring = [(i, (i + shift) % pair_count) for i in range(pair_count)]
+        gathered.append(lax.ppermute(hidden, "pair", ring))
+    all_hidden = jnp.concatenate(gathered, axis=0)
     my_columns = lax.dynamic_slice_in_dim(all_hidden, pair_place * row_share, row_share, 1)
     my_rows = (
         lax.dot_general(

time: 163 us -> 142 us (0.87)
  between operations: 14.9 us -> 1.5 us
  waiting for transfers between devices: 20.5 us -> 8.64 us
  matrix products: 29.6 us -> 23 us
  other arithmetic: 25.4 us -> 31.2 us
  starting transfers between devices: 11.6 us -> 15.3 us
    all_to_all x1, waiting for transfers between devices: 16.6 us -> 5.57 us  [per_device(): lax.all_to_all(results, 'expert', split_axis=0, concat_axis=0, tiled=True)]
    ppermute x0 -> x3, starting transfers between devices: none -> 3.7 us  [per_device(): gathered.append(lax.ppermute(hidden, 'pair', ring))]
    ppermute x3, waiting for transfers between devices: 3.3 us -> 0.01 us  [per_device(): pack_sum = pack_sum + lax.ppermute(pack, 'pair', ring)]
    dot_general x1, matrix products: 8.2 us -> 4.95 us  [swiglu_rows(): jnp.dot(hidden, down_matrix, preferred_element_type=jnp.float32)]
    ppermute x0 -> x3, waiting for transfers between devices: none -> 3.07 us  [per_device(): gathered.append(lax.ppermute(hidden, 'pair', ring))]
    dot_general x1, matrix products: 3.42 us -> 1.08 us  [per_device(): lax.dot_general(my_columns, all_hidden, (((0,), (0,)), ((), ())), preferr...]
  transfers between devices with their start and end apart: 5 -> 7, of which waited for: 3 -> 3; matrix products, arithmetic and copies ran while one was open for 20% -> 24% of each run, Pallas kernels for 0% -> 0%
where the time goes in v3:
time: 142 us; the launch traced here: 141 us
  blocking collectives  58.4 us (41%)
  other arithmetic  31.2 us (22%)
  matrix products  23 us (16%)
  starting transfers between devices  15.3 us (11%)
  waiting for transfers between devices  8.64 us (6%)
  local copies, waits for them, and re-layouts  3.12 us (2%)
  between operations  1.5 us (1%)
    all_to_all x1, blocking collectives, per_device(): lax.all_to_all(outgoing, 'expert', split_axis=0, concat_axis=0, tiled=True)  58.4 us
    another operation x3, other arithmetic, per_device(): jnp.linalg.cholesky(corner + damping * jnp.eye(PANEL, dtype=jnp.float32))  13.2 us
    another operation x2, other arithmetic, per_device(): jax.scipy.linalg.solve_triangular(lower_factor, leading.T, lower=True)  11.9 us
    ppermute x3, starting transfers between devices, per_device(): pack_sum = pack_sum + lax.ppermute(pack, 'pair', ring)  6.57 us
    all_to_all x1, waiting for transfers between devices, per_device(): lax.all_to_all(results, 'expert', split_axis=0, concat_axis=0, tiled=True)  5.57 us
    all_to_all x1, starting transfers between devices, per_device(): lax.all_to_all(results, 'expert', split_axis=0, concat_axis=0, tiled=True)  5 us
    dot_general x1, matrix products, swiglu_rows(): jnp.dot(hidden, down_matrix, preferred_element_type=jnp.float32)  4.95 us
    dot_general x1, matrix products, swiglu_rows(): jnp.dot(flat_rows, upper_matrix, preferred_element_type=jnp.float32)  4.26 us
  transfers between devices with their start and end apart: 7, of which 3 were waited for; matrix products, arithmetic and copies ran while one was open for 24% of the time, Pallas kernels for 0%

profile of v3, /device:TPU:0, one launch (start us, length us, event | category | flops | bytes accessed | tf_op | source)
XLA Modules:
  0.0 141.1 jit_solution(11990420064325713825)
XLA Ops:
  0.6 0.8 add_select_fusion
  2.9 1.2 convolution_convert_fusion
  4.1 58.4 %all_to_all.10 = bf16[32,16,4096]{2,1,0:T(8,128)(2,1)S(1)} all-to-all(bf16[32,16,4096]{2,1,0:T(8,128)(2,1)S(1)} %bitcast.55), channel_id=1, replica_groups=mesh['expert'=32,'pair'=4] {'expert'}, dimensions={0} | all-to-all | bytes 8388608 | tf_op jit(solution)/shard_map/all_to_all | solution.py:49
  62.6 3.4 %fusion.4 = f32[512,768]{1,0:T(8,128)S(1)} fusion(bf16[512,4096]{1,0:T(8,128)(2,1)S(1)} %bitcast.57, bf16[1,4096,768]{2,1,0:T(8,128)(2,1)S(1)} %bitcast.61), kind=kOutput, calls=%fused_computation.4 | convolution fusion | flops 3221225472 | bytes 12058624 | tf_op jit(solution)/shard_map/dot_general | solution.py:13
  66.0 4.3 %multiply_reduce_fusion = (f32[]{:T(128)}, bf16[512,768]{1,0:T(8,128)(2,1)S(1)}) fusion(bf16[512,4096]{1,0:T(8,128)(2,1)S(1)} %bitcast.58, bf16[1,4096,768]{2,1,0:T(8,128)(2,1)S(1)} %bitcast.63, f32[512,768]{1,0:T(8,128)S(1)} %fusion.4), kind=kOutput, calls=%fused_computation.13 | convolution fusion | flops 3224764416 | bytes 12845060 | tf_op jit(solution)/shard_map/dot_general | solution.py:14
  70.3 4.9 %fusion.6 = bf16[512,4096]{1,0:T(8,128)(2,1)} fusion(bf16[512,768]{1,0:T(8,128)(2,1)S(1)} %get-tuple-element.6, bf16[1,768,4096]{2,1,0:T(8,128)(2,1)S(1)} %bitcast.65), kind=kOutput, calls=%fused_computation.7 | convolution fusion | flops 3223322624 | bytes 11272192 | tf_op jit(solution)/shard_map/dot_general | solution.py:16
  75.2 5.0 %all-to-all-start.1 = ((bf16[32,16,4096]{2,1,0:T(8,128)(2,1)}), bf16[32,16,4096]{2,1,0:T(8,128)(2,1)}, u32[]{:S(2)}, u32[]{:S(2)}) async-start(bf16[32,16,4096]{2,1,0:T(8,128)(2,1)} %bitcast.56), calls=%async_computation.1 | async-start | bytes 8388608 | tf_op jit(solution)/shard_map/all_to_all | solution.py:55
  81.2 2.0 %collective-permute-start.3 = (f32[136,128]{1,0:T(8,128)S(1)}, f32[136,128]{1,0:T(8,128)S(1)}, u32[]{:S(2)}, u32[]{:S(2)}) collective-permute-start(f32[136,128]{1,0:T(8,128)S(1)} %concatenate.7), channel_id=1, source_target_pairs={{0,1},{1,2},{2,3},{3,0},{4,5},{5,6},{6,7},{7,4},{8,9},{9,10},{10,1... | collective-permute-start | bytes 208904 | tf_op jit(solution)/shard_map/ppermute | solution.py:78
  83.2 3.6 %collective-permute-start.4 = (f32[136,128]{1,0:T(8,128)S(1)}, f32[136,128]{1,0:T(8,128)S(1)}, u32[]{:S(2)}, u32[]{:S(2)}) collective-permute-start(f32[136,128]{1,0:T(8,128)S(1)} %concatenate.7), channel_id=1, source_target_pairs={{0,2},{1,3},{2,0},{3,1},{4,6},{5,7},{6,4},{7,5},{8,10},{9,11},{10,... | collective-permute-start | bytes 208904 | tf_op jit(solution)/shard_map/ppermute | solution.py:78
  86.8 1.0 collective-permute-start.5
  87.8 1.0 collective-permute-start
  89.2 2.2 %collective-permute-start.2 = (bf16[512,768]{1,0:T(8,128)(2,1)S(1)}, bf16[512,768]{1,0:T(8,128)(2,1)}, u32[]{:S(2)}, u32[]{:S(2)}) collective-permute-start(bf16[512,768]{1,0:T(8,128)(2,1)S(1)} %get-tuple-element.6), channel_id=1, source_target_pairs={{0,3},{1,0},{2,1},{3,2},{4,7},{5,4},{6,5},{7,6},{8,11},{9,8},{10,9... | collective-permute-start | bytes 2359304 | tf_op jit(solution)/shard_map/ppermute | solution.py:85
  94.0 1.6 %copy.36 = f32[128,128]{0,1:T(8,128)} copy(f32[128,128]{1,0:T(8,128)} %fusion.32) | data formatting | bytes 131072 | tf_op jit(solution)/shard_map/add | solution.py:81
  95.5 1.5 %fusion.34 = f32[128,128]{1,0:T(8,128)} fusion(f32[128,128]{0,1:T(8,128)} %copy.36, f32[]{:T(128)} %bitcast.11, f32[136,128]{1,0:T(8,128)S(1)} %add_add_fusion), kind=kLoop, calls=%fused_computation.52 | loop fusion | flops 98304 | bytes 196612 | tf_op jit(solution)/shard_map/jit(cholesky)/div | solution.py:81
  97.0 12.5 %cholesky.16 = f32[128,128]{1,0:T(8,128)S(1)} custom-call(f32[128,128]{1,0:T(8,128)} %fusion.34), custom_call_target="Cholesky" | custom-call | tf_op jit(solution)/shard_map/jit(cholesky)/cholesky | solution.py:81
  110.2 1.3 fusion.31
  111.5 10.6 %custom-call.7 = f32[1,128,128]{1,2,0:T(8,128)S(1)} custom-call(f32[1,128,128]{2,1,0:T(8,128)} %fusion.31), custom_call_target="InvertDiagBlocksLowerTriangular" | custom-call | tf_op jit(solution)/shard_map/jit(_solve_triangular)/triangular_solve | solution.py:97
  122.2 2.6 %collective-permute-done = bf16[512,768]{1,0:T(8,128)(2,1)S(1)} collective-permute-done((bf16[512,768]{1,0:T(8,128)(2,1)S(1)}, bf16[512,768]{1,0:T(8,128)(2,1)S(1)}, u32[]{:S(2)}, u32[]{:S(2)}) %collective-permute-start) | collective-permute-done | bytes 786464 | tf_op jit(solution)/shard_map/ppermute | solution.py:85
  125.2 1.3 pad_maximum_fusion
  126.6 1.1 convolution_multiply_fusion
  127.7 0.9 convolution_bitcast_fusion.2
  128.6 5.6 %all-to-all-done.1 = bf16[32,16,4096]{2,1,0:T(8,128)(2,1)} async-done(((bf16[32,16,4096]{2,1,0:T(8,128)(2,1)}), bf16[32,16,4096]{2,1,0:T(8,128)(2,1)}, u32[]{:S(2)}, u32[]{:S(2)}) %all-to-all-start.1) | async-done | bytes 4194336 | tf_op jit(solution)/shard_map/all_to_all | solution.py:55
  134.2 3.0 %convolution_bitcast_fusion = f32[128,4096]{1,0:T(8,128)S(1)} fusion(bf16[32,16,4096]{2,1,0:T(8,128)(2,1)} %all-to-all-done.1, f32[128,32]{0,1:T(8,128)S(1)} %fusion.18, s32[128,32]{0,1:T(8,128)S(1)} %copy.35, s32[128,32]{0,1:T(8,128)S(1)} %copy.33), kind=kOutput, calls=%fused_computation.8 | convolution fusion | flops 537329664 | bytes 6340608 | tf_op jit(solution)/shard_map/dot_general | solution.py:62
  137.2 4.0 %fusion.10 = bf16[128,4096]{1,0:T(8,128)(2,1)} fusion(f32[128,4096]{1,0:T(8,128)S(1)} %convolution_bitcast_fusion, bf16[32,16,4096]{2,1,0:T(8,128)(2,1)} %all-to-all-done.1, f32[128,32]{0,1:T(8,128)S(1)} %fusion.18, s32[128,32]{0,1:T(8,128)S(1)} %copy.35, s32[128,32]{0,1:T(8,128)S(1)} %copy.33), kind=kOutput, calls=%fused_computation.11 | convolution fusion | flops 538312704 | bytes 7389184 | tf_op jit(solution)/shard_map/dot_general | solution.py:62
  (46 shorter events, 5.8 us)
Async XLA Ops:
  0.6 2.2 %copy-start = (bf16[128,4096]{1,0:T(8,128)(2,1)S(1)}, bf16[128,4096]{1,0:T(8,128)(2,1)}, u32[]{:S(2)}) copy-start(bf16[128,4096]{1,0:T(8,128)(2,1)} %param.6) | copy-start | bytes 3145732
  2.8 59.7 %slice-start = ((s8[6291456]{0:T(1024)(128)(4,1)}), s8[4194304]{0:T(1024)(128)(4,1)S(1)}, s32[]{:S(2)}) async-start(s8[6291456]{0:T(1024)(128)(4,1)} %bitcast.60), calls=%async_computation.2 | async-start | bytes 8388608
  4.1 58.5 %slice-start.1 = ((s8[6291456]{0:T(1024)(128)(4,1)}), s8[2097152]{0:T(1024)(128)(4,1)S(1)}, s32[]{:S(2)}) async-start(s8[6291456]{0:T(1024)(128)(4,1)} %bitcast.60), calls=%async_computation.3 | async-start | bytes 4194304
  4.1 61.9 %slice-start.2 = ((s8[6291456]{0:T(1024)(128)(4,1)}), s8[4194304]{0:T(1024)(128)(4,1)S(1)}, s32[]{:S(2)}) async-start(s8[6291456]{0:T(1024)(128)(4,1)} %bitcast.62), calls=%async_computation.4 | async-start | bytes 8388608
  4.1 66.1 %slice-start.4 = ((s8[6291456]{0:T(1024)(128)(4,1)}), s8[4194304]{0:T(1024)(128)(4,1)S(1)}, s32[]{:S(2)}) async-start(s8[6291456]{0:T(1024)(128)(4,1)} %bitcast.64), calls=%async_computation.6 | async-start | bytes 8388608
  62.6 3.4 %slice-start.3 = ((s8[6291456]{0:T(1024)(128)(4,1)}), s8[2097152]{0:T(1024)(128)(4,1)S(1)}, s32[]{:S(2)}) async-start(s8[6291456]{0:T(1024)(128)(4,1)} %bitcast.62), calls=%async_computation.5 | async-start | bytes 4194304
  62.6 7.7 %slice-start.5 = ((s8[6291456]{0:T(1024)(128)(4,1)}), s8[2097152]{0:T(1024)(128)(4,1)S(1)}, s32[]{:S(2)}) async-start(s8[6291456]{0:T(1024)(128)(4,1)} %bitcast.64), calls=%async_computation.7 | async-start | bytes 4194304
  75.2 5.0 %copy-start.2 = (f32[128,8]{0,1:T(8,128)S(1)}, f32[128,8]{0,1:T(8,128)}, u32[]{:S(2)}) copy-start(f32[128,8]{0,1:T(8,128)} %param.8) | copy-start | bytes 12292
  75.2 59.0 %all-to-all-start.1 = ((bf16[32,16,4096]{2,1,0:T(8,128)(2,1)}), bf16[32,16,4096]{2,1,0:T(8,128)(2,1)}, u32[]{:S(2)}, u32[]{:S(2)}) async-start(bf16[32,16,4096]{2,1,0:T(8,128)(2,1)} %bitcast.56), calls=%async_computation.1 | async-start | bytes 8388608 | tf_op jit(solution)/shard_map/all_to_all | solution.py:55
  81.2 8.0 %collective-permute-start.3 = (f32[136,128]{1,0:T(8,128)S(1)}, f32[136,128]{1,0:T(8,128)S(1)}, u32[]{:S(2)}, u32[]{:S(2)}) collective-permute-start(f32[136,128]{1,0:T(8,128)S(1)} %concatenate.7), channel_id=1, source_target_pairs={{0,1},{1,2},{2,3},{3,0},{4,5},{5,6},{6,7},{7,4},{8,9},{9,10},{10,1... | collective-permute-start | bytes 208904 | tf_op jit(solution)/shard_map/ppermute | solution.py:78
  83.2 8.3 %collective-permute-start.4 = (f32[136,128]{1,0:T(8,128)S(1)}, f32[136,128]{1,0:T(8,128)S(1)}, u32[]{:S(2)}, u32[]{:S(2)}) collective-permute-start(f32[136,128]{1,0:T(8,128)S(1)} %concatenate.7), channel_id=1, source_target_pairs={{0,2},{1,3},{2,0},{3,1},{4,6},{5,7},{6,4},{7,5},{8,10},{9,11},{10,... | collective-permute-start | bytes 208904 | tf_op jit(solution)/shard_map/ppermute | solution.py:78
  86.8 4.7 %collective-permute-start.5 = (f32[136,128]{1,0:T(8,128)S(1)}, f32[136,128]{1,0:T(8,128)S(1)}, u32[]{:S(2)}, u32[]{:S(2)}) collective-permute-start(f32[136,128]{1,0:T(8,128)S(1)} %concatenate.7), channel_id=1, source_target_pairs={{0,3},{1,0},{2,1},{3,2},{4,7},{5,4},{6,5},{7,6},{8,11},{9,8},{10,9... | collective-permute-start | bytes 208904 | tf_op jit(solution)/shard_map/ppermute | solution.py:78
  87.8 37.0 %collective-permute-start = (bf16[512,768]{1,0:T(8,128)(2,1)S(1)}, bf16[512,768]{1,0:T(8,128)(2,1)S(1)}, u32[]{:S(2)}, u32[]{:S(2)}) collective-permute-start(bf16[512,768]{1,0:T(8,128)(2,1)S(1)} %get-tuple-element.6), channel_id=1, source_target_pairs={{0,1},{1,2},{2,3},{3,0},{4,5},{5,6},{6,7},{7,4},{8,9},{9,10},{10,1... | collective-permute-start | bytes 2359304 | tf_op jit(solution)/shard_map/ppermute | solution.py:85
  88.8 36.0 %collective-permute-start.1 = (bf16[512,768]{1,0:T(8,128)(2,1)S(1)}, bf16[512,768]{1,0:T(8,128)(2,1)S(1)}, u32[]{:S(2)}, u32[]{:S(2)}) collective-permute-start(bf16[512,768]{1,0:T(8,128)(2,1)S(1)} %get-tuple-element.6), channel_id=1, source_target_pairs={{0,2},{1,3},{2,0},{3,1},{4,6},{5,7},{6,4},{7,5},{8,10},{9,11},{10,... | collective-permute-start | bytes 2359304 | tf_op jit(solution)/shard_map/ppermute | solution.py:85
  89.2 36.0 %collective-permute-start.2 = (bf16[512,768]{1,0:T(8,128)(2,1)S(1)}, bf16[512,768]{1,0:T(8,128)(2,1)}, u32[]{:S(2)}, u32[]{:S(2)}) collective-permute-start(bf16[512,768]{1,0:T(8,128)(2,1)S(1)} %get-tuple-element.6), channel_id=1, source_target_pairs={{0,3},{1,0},{2,1},{3,2},{4,7},{5,4},{6,5},{7,6},{8,11},{9,8},{10,9... | collective-permute-start | bytes 2359304 | tf_op jit(solution)/shard_map/ppermute | solution.py:85
  127.7 13.4 %copy-start.1 = (f32[192,768]{1,0:T(8,128)}, f32[192,768]{1,0:T(8,128)S(1)}, u32[]{:S(2)}) copy-start(f32[192,768]{1,0:T(8,128)S(1)} %convolution_multiply_fusion) | copy-start | bytes 1769476

commit v4 on v3

--- a/solution.py
+++ b/solution.py
@@ -2,6 +2,8 @@
 import jax.numpy as jnp
 from jax import lax
 from jax.sharding import PartitionSpec as P
+from jax.experimental import pallas as pl
+from jax.experimental.pallas import tpu as pltpu
 
 EXPERTS = 128
 FF = 768
@@ -20,6 +22,35 @@
 def split_bf16(values):
     rounded = lax.reduce_precision(values, exponent_bits=8, mantissa_bits=7)
     return rounded.astype(jnp.bfloat16), (values - rounded).astype(jnp.bfloat16)
+
+
+def combine_kernel(high_ref, low_ref, rows_ref, out_ref):
+    rows = rows_ref[...]
+    total = jnp.dot(high_ref[...], rows, preferred_element_type=jnp.float32)
+    total = total + jnp.dot(low_ref[...], rows, preferred_element_type=jnp.float32)
+    out_ref[...] = total.astype(out_ref.dtype)
+
+
+def combine_rows(weight_high, weight_low, rows):
+    tok_count, slot_count = weight_high.shape
+    width = rows.shape[1]
+    block = 1024
+    return pl.pallas_call(
+        combine_kernel,
+        out_shape=jax.ShapeDtypeStruct((tok_count, width), jnp.bfloat16),
+        grid=(width // block,),
+        in_specs=[
+            pl.BlockSpec((tok_count, slot_count), lambda j: (0, 0)),
+            pl.BlockSpec((tok_count, slot_count), lambda j: (0, 0)),
+            pl.BlockSpec((slot_count, block), lambda j: (0, j)),
+        ],
+        out_specs=pl.BlockSpec((tok_count, block), lambda j: (0, j)),
+        cost_estimate=pl.CostEstimate(
+            flops=4 * tok_count * slot_count * width,
+            transcendentals=0,
+            bytes_accessed=2 * (slot_count * width + tok_count * width + 2 * tok_count * slot_count),
+        ),
+    )(weight_high, weight_low, rows)
 
 
 def per_device(tokens, expert_ids, route_weight, gate_weight, up_weight, down_weight):
@@ -59,9 +90,7 @@
         slot_marks.astype(jnp.float32) * owner_weight[:, :, None]
     ).reshape(tok_count, owners * CAP)
     weight_high, weight_low = split_bf16(combine_matrix)
-    combined = jnp.dot(weight_high, returned_flat, preferred_element_type=jnp.float32) + jnp.dot(
-        weight_low, returned_flat, preferred_element_type=jnp.float32
-    )
+    combined = combine_rows(weight_high, weight_low, returned_flat)
     hess_scale = 2.0 / (CAP * owners * pair_count)
     row_share = FF // pair_count
     pair_place = lax.axis_index("pair")
@@ -95,7 +124,7 @@
     column_ids = lax.broadcasted_iota(jnp.int32, (row_share, PANEL), 1)
     leading = my_rows[:, :PANEL] + damping * (row_ids == column_ids).astype(jnp.float32)
     panel_rows = jax.scipy.linalg.solve_triangular(lower_factor, leading.T, lower=True).T
-    return (combined.astype(jnp.bfloat16), my_rows[None], panel_rows[None])
+    return (combined, my_rows[None], panel_rows[None])
 
 
 def solution(mesh):

time: 142 us -> 141 us (level)
  matrix products: 23 us -> 16.2 us
  waiting for transfers between devices: 8.64 us -> 14.9 us
  Pallas kernels: 0 us -> 4.88 us
  other arithmetic: 31.2 us -> 28.9 us
    dot_general x2 -> x0, matrix products: 6.91 us -> none  [the longest x1 3.95 us: per_device(): jnp.dot(weight_high, returned_flat, preferred_element_type=jnp.float32)]
    ppermute x3, waiting for transfers between devices: 3.07 us -> 9.73 us  [per_device(): gathered.append(lax.ppermute(hidden, 'pair', ring))]
    pallas_call x0 -> x1, Pallas kernels: none -> 4.88 us  [combine_rows(): pl.pallas_call(combine_kernel, out_shape=jax.ShapeDtypeStruct((tok_count,...]
    all_to_all x1, waiting for transfers between devices: 5.57 us -> 4.02 us  [per_device(): lax.all_to_all(results, 'expert', split_axis=0, concat_axis=0, tiled=True)]
    add x1, local copies, waits for them, and re-layouts: 1.57 us -> 0.09 us  [per_device(): corner + damping * jnp.eye(PANEL, dtype=jnp.float32)]
    another operation x2, other arithmetic: 11.9 us -> 10.5 us  [per_device(): jax.scipy.linalg.solve_triangular(lower_factor, leading.T, lower=True)]
    div x1, other arithmetic: 1.49 us -> 0.02 us  [per_device(): jnp.linalg.cholesky(corner + damping * jnp.eye(PANEL, dtype=jnp.float32))]
  transfers between devices with their start and end apart: 7 -> 7, of which waited for: 3 -> 4; matrix products, arithmetic and copies ran while one was open for 24% -> 21% of each run, Pallas kernels for 0% -> 0%
where the time goes in v4:
time: 141 us
  blocking collectives  58.4 us (41%)
  other arithmetic  28.9 us (20%)
  matrix products  16.2 us (11%)
  waiting for transfers between devices  14.9 us (11%)
  starting transfers between devices  13.9 us (10%)
  Pallas kernels  4.88 us (3%)
  local copies, waits for them, and re-layouts  2.08 us (1%)
  between operations  1.56 us (1%)
    all_to_all x1, blocking collectives, per_device(): lax.all_to_all(outgoing, 'expert', split_axis=0, concat_axis=0, tiled=True)  58.4 us
    another operation x3, other arithmetic, per_device(): jnp.linalg.cholesky(corner + damping * jnp.eye(PANEL, dtype=jnp.float32))  12.4 us
    another operation x2, other arithmetic, per_device(): jax.scipy.linalg.solve_triangular(lower_factor, leading.T, lower=True)  10.5 us
    ppermute x3, waiting for transfers between devices, per_device(): gathered.append(lax.ppermute(hidden, 'pair', ring))  9.73 us
    ppermute x3, starting transfers between devices, per_device(): pack_sum = pack_sum + lax.ppermute(pack, 'pair', ring)  5.98 us
    dot_general x1, matrix products, swiglu_rows(): jnp.dot(hidden, down_matrix, preferred_element_type=jnp.float32)  4.98 us
    pallas_call x1, Pallas kernels, combine_rows(): pl.pallas_call(combine_kernel, out_shape=jax.ShapeDtypeStruct((tok_count,...  4.88 us
    all_to_all x1, starting transfers between devices, per_device(): lax.all_to_all(results, 'expert', split_axis=0, concat_axis=0, tiled=True)  4.87 us
  transfers between devices with their start and end apart: 7, of which 4 were waited for; matrix products, arithmetic and copies ran while one was open for 21% of the time, Pallas kernels for 0%

profile of v4, /device:TPU:0, one launch (start us, length us, event | category | flops | bytes accessed | tf_op | source)
XLA Modules:
  0.0 140.9 jit_solution(1499246225020837701)
XLA Ops:
  0.6 0.8 fusion.27
  1.4 0.7 add_select_fusion
  2.2 0.7 fusion.14
  3.9 0.7 fusion.12
  4.6 1.3 convolution_convert_fusion
  6.0 58.4 %all_to_all.10 = bf16[32,16,4096]{2,1,0:T(8,128)(2,1)S(1)} all-to-all(bf16[32,16,4096]{2,1,0:T(8,128)(2,1)S(1)} %bitcast.40), channel_id=1, replica_groups=mesh['expert'=32,'pair'=4] {'expert'}, dimensions={0} | all-to-all | bytes 8388608 | tf_op jit(solution)/shard_map/all_to_all | solution.py:80
  64.4 3.4 %fusion.4 = f32[512,768]{1,0:T(8,128)S(1)} fusion(bf16[512,4096]{1,0:T(8,128)(2,1)S(1)} %bitcast.42, bf16[1,4096,768]{2,1,0:T(8,128)(2,1)S(1)} %bitcast.49), kind=kOutput, calls=%fused_computation.4 | convolution fusion | flops 3221225472 | bytes 12058624 | tf_op jit(solution)/shard_map/dot_general | solution.py:15
  67.9 4.3 %multiply_reduce_fusion = (f32[]{:T(128)}, bf16[512,768]{1,0:T(8,128)(2,1)S(1)}) fusion(bf16[512,4096]{1,0:T(8,128)(2,1)S(1)} %bitcast.43, bf16[1,4096,768]{2,1,0:T(8,128)(2,1)S(1)} %bitcast.51, f32[512,768]{1,0:T(8,128)S(1)} %fusion.4), kind=kOutput, calls=%fused_computation.9 | convolution fusion | flops 3224764416 | bytes 12845060 | tf_op jit(solution)/shard_map/dot_general | solution.py:16
  72.2 5.0 %fusion.6 = bf16[512,4096]{1,0:T(8,128)(2,1)} fusion(bf16[512,768]{1,0:T(8,128)(2,1)S(1)} %get-tuple-element.8, bf16[1,768,4096]{2,1,0:T(8,128)(2,1)S(1)} %bitcast.53), kind=kOutput, calls=%fused_computation.7 | convolution fusion | flops 3223322624 | bytes 11272192 | tf_op jit(solution)/shard_map/dot_general | solution.py:18
  77.1 4.9 %all-to-all-start.1 = ((bf16[32,16,4096]{2,1,0:T(8,128)(2,1)}), bf16[32,16,4096]{2,1,0:T(8,128)(2,1)}, u32[]{:S(2)}, u32[]{:S(2)}) async-start(bf16[32,16,4096]{2,1,0:T(8,128)(2,1)} %bitcast.41), calls=%async_computation.1 | async-start | bytes 8388608 | tf_op jit(solution)/shard_map/all_to_all | solution.py:86
  83.6 4.0 %collective-permute-start.4 = (f32[136,128]{1,0:T(8,128)S(1)}, f32[136,128]{1,0:T(8,128)S(1)}, u32[]{:S(2)}, u32[]{:S(2)}) collective-permute-start(f32[136,128]{1,0:T(8,128)S(1)} %concatenate.7), channel_id=1, source_target_pairs={{0,2},{1,3},{2,0},{3,1},{4,6},{5,7},{6,4},{7,5},{8,10},{9,11},{10,... | collective-permute-start | bytes 208904 | tf_op jit(solution)/shard_map/ppermute | solution.py:107
  87.6 0.7 collective-permute-start.5
  88.3 1.3 collective-permute-start.3
  89.6 1.9 %collective-permute-start.2 = (bf16[512,768]{1,0:T(8,128)(2,1)S(1)}, bf16[512,768]{1,0:T(8,128)(2,1)S(1)}, u32[]{:S(2)}, u32[]{:S(2)}) collective-permute-start(bf16[512,768]{1,0:T(8,128)(2,1)S(1)} %get-tuple-element.8), channel_id=1, source_target_pairs={{0,3},{1,0},{2,1},{3,2},{4,7},{5,4},{6,5},{7,6},{8,11},{9,8},{10,9... | collective-permute-start | bytes 2359304 | tf_op jit(solution)/shard_map/ppermute | solution.py:114
  91.5 1.2 collective-permute-start.1
  93.0 0.8 collective-permute-done.3
  95.8 11.7 %cholesky.16 = f32[128,128]{1,0:T(8,128)S(1)} custom-call(f32[128,128]{1,0:T(8,128)S(1)} %fusion.23), custom_call_target="Cholesky" | custom-call | tf_op jit(solution)/shard_map/jit(cholesky)/cholesky | solution.py:110
  108.8 9.8 %custom-call.7 = f32[1,128,128]{1,2,0:T(8,128)S(1)} custom-call(f32[1,128,128]{2,1,0:T(8,128)S(1)} %fusion.20), custom_call_target="InvertDiagBlocksLowerTriangular" | custom-call | tf_op jit(solution)/shard_map/jit(_solve_triangular)/triangular_solve | solution.py:126
  118.7 9.7 %collective-permute-done = bf16[512,768]{1,0:T(8,128)(2,1)} collective-permute-done((bf16[512,768]{1,0:T(8,128)(2,1)S(1)}, bf16[512,768]{1,0:T(8,128)(2,1)}, u32[]{:S(2)}, u32[]{:S(2)}) %collective-permute-start) | collective-permute-done | bytes 786464 | tf_op jit(solution)/shard_map/ppermute | solution.py:114
  128.4 1.5 %pad_maximum_fusion = bf16[2048,768]{1,0:T(8,128)(2,1)S(1)} fusion(bf16[512,768]{1,0:T(8,128)(2,1)S(1)} %collective-permute-done.2, bf16[512,768]{1,0:T(8,128)(2,1)} %collective-permute-done.1, bf16[512,768]{1,0:T(8,128)(2,1)} %collective-permute-done, bf16[512,768]{1,0:T(8,128)(2,1)S(1)} %get-tuple-element.8), kind=kLoop, calls=%fused_computation.8 | loop fusion | flops 12582912 | bytes 6291456 | tf_op jit(solution)/shard_map/concatenate | solution.py:115
  129.9 1.1 convolution_multiply_fusion
  131.0 0.9 convolution_bitcast_fusion
  132.0 4.0 %all-to-all-done.1 = bf16[32,16,4096]{2,1,0:T(8,128)(2,1)} async-done(((bf16[32,16,4096]{2,1,0:T(8,128)(2,1)}), bf16[32,16,4096]{2,1,0:T(8,128)(2,1)}, u32[]{:S(2)}, u32[]{:S(2)}) %all-to-all-start.1) | async-done | bytes 4194336 | tf_op jit(solution)/shard_map/all_to_all | solution.py:86
  136.0 4.9 %shard_map.85 = bf16[128,4096]{1,0:T(8,128)(2,1)} custom-call(bf16[128,512]{1,0:T(8,128)(2,1)} %reduce-precision_convert_fusion.high_ref, bf16[128,512]{1,0:T(8,128)(2,1)} %get-tuple-element.3.low_ref, bf16[512,4096]{1,0:T(8,128)(2,1)} %bitcast.9.rows_ref), custom_call_target="tpu_custom_call" | custom-call | flops 1073741824 | bytes 5505024 | tf_op jit(solution)/shard_map/pallas_call | solution.py:38
  (50 shorter events, 5.6 us)
Async XLA Ops:
  0.6 4.0 %copy-start = (bf16[128,4096]{1,0:T(8,128)(2,1)S(1)}, bf16[128,4096]{1,0:T(8,128)(2,1)}, u32[]{:S(2)}) copy-start(bf16[128,4096]{1,0:T(8,128)(2,1)} %param.6) | copy-start | bytes 3145732
  4.6 59.7 %slice-start = ((s8[6291456]{0:T(1024)(128)(4,1)}), s8[4194304]{0:T(1024)(128)(4,1)S(1)}, s32[]{:S(2)}) async-start(s8[6291456]{0:T(1024)(128)(4,1)} %bitcast.48), calls=%async_computation.2 | async-start | bytes 8388608
  5.9 58.5 %slice-start.1 = ((s8[6291456]{0:T(1024)(128)(4,1)}), s8[2097152]{0:T(1024)(128)(4,1)S(1)}, s32[]{:S(2)}) async-start(s8[6291456]{0:T(1024)(128)(4,1)} %bitcast.48), calls=%async_computation.3 | async-start | bytes 4194304
  5.9 61.9 %slice-start.2 = ((s8[6291456]{0:T(1024)(128)(4,1)}), s8[4194304]{0:T(1024)(128)(4,1)S(1)}, s32[]{:S(2)}) async-start(s8[6291456]{0:T(1024)(128)(4,1)} %bitcast.50), calls=%async_computation.4 | async-start | bytes 8388608
  5.9 66.2 %slice-start.4 = ((s8[6291456]{0:T(1024)(128)(4,1)}), s8[4194304]{0:T(1024)(128)(4,1)S(1)}, s32[]{:S(2)}) async-start(s8[6291456]{0:T(1024)(128)(4,1)} %bitcast.52), calls=%async_computation.6 | async-start | bytes 8388608
  64.4 3.5 %slice-start.3 = ((s8[6291456]{0:T(1024)(128)(4,1)}), s8[2097152]{0:T(1024)(128)(4,1)S(1)}, s32[]{:S(2)}) async-start(s8[6291456]{0:T(1024)(128)(4,1)} %bitcast.50), calls=%async_computation.5 | async-start | bytes 4194304
  64.4 7.8 %slice-start.5 = ((s8[6291456]{0:T(1024)(128)(4,1)}), s8[2097152]{0:T(1024)(128)(4,1)S(1)}, s32[]{:S(2)}) async-start(s8[6291456]{0:T(1024)(128)(4,1)} %bitcast.52), calls=%async_computation.7 | async-start | bytes 4194304
  77.1 58.8 %all-to-all-start.1 = ((bf16[32,16,4096]{2,1,0:T(8,128)(2,1)}), bf16[32,16,4096]{2,1,0:T(8,128)(2,1)}, u32[]{:S(2)}, u32[]{:S(2)}) async-start(bf16[32,16,4096]{2,1,0:T(8,128)(2,1)} %bitcast.41), calls=%async_computation.1 | async-start | bytes 8388608 | tf_op jit(solution)/shard_map/all_to_all | solution.py:86
  83.6 9.1 %collective-permute-start.4 = (f32[136,128]{1,0:T(8,128)S(1)}, f32[136,128]{1,0:T(8,128)S(1)}, u32[]{:S(2)}, u32[]{:S(2)}) collective-permute-start(f32[136,128]{1,0:T(8,128)S(1)} %concatenate.7), channel_id=1, source_target_pairs={{0,2},{1,3},{2,0},{3,1},{4,6},{5,7},{6,4},{7,5},{8,10},{9,11},{10,... | collective-permute-start | bytes 208904 | tf_op jit(solution)/shard_map/ppermute | solution.py:107
  87.6 5.4 %collective-permute-start.5 = (f32[136,128]{1,0:T(8,128)S(1)}, f32[136,128]{1,0:T(8,128)S(1)}, u32[]{:S(2)}, u32[]{:S(2)}) collective-permute-start(f32[136,128]{1,0:T(8,128)S(1)} %concatenate.7), channel_id=1, source_target_pairs={{0,3},{1,0},{2,1},{3,2},{4,7},{5,4},{6,5},{7,6},{8,11},{9,8},{10,9... | collective-permute-start | bytes 208904 | tf_op jit(solution)/shard_map/ppermute | solution.py:107
  88.3 5.5 %collective-permute-start.3 = (f32[136,128]{1,0:T(8,128)S(1)}, f32[136,128]{1,0:T(8,128)S(1)}, u32[]{:S(2)}, u32[]{:S(2)}) collective-permute-start(f32[136,128]{1,0:T(8,128)S(1)} %concatenate.7), channel_id=1, source_target_pairs={{0,1},{1,2},{2,3},{3,0},{4,5},{5,6},{6,7},{7,4},{8,9},{9,10},{10,1... | collective-permute-start | bytes 208904 | tf_op jit(solution)/shard_map/ppermute | solution.py:107
  89.6 29.1 %collective-permute-start.2 = (bf16[512,768]{1,0:T(8,128)(2,1)S(1)}, bf16[512,768]{1,0:T(8,128)(2,1)S(1)}, u32[]{:S(2)}, u32[]{:S(2)}) collective-permute-start(bf16[512,768]{1,0:T(8,128)(2,1)S(1)} %get-tuple-element.8), channel_id=1, source_target_pairs={{0,3},{1,0},{2,1},{3,2},{4,7},{5,4},{6,5},{7,6},{8,11},{9,8},{10,9... | collective-permute-start | bytes 2359304 | tf_op jit(solution)/shard_map/ppermute | solution.py:114
  91.5 27.1 %collective-permute-start.1 = (bf16[512,768]{1,0:T(8,128)(2,1)S(1)}, bf16[512,768]{1,0:T(8,128)(2,1)}, u32[]{:S(2)}, u32[]{:S(2)}) collective-permute-start(bf16[512,768]{1,0:T(8,128)(2,1)S(1)} %get-tuple-element.8), channel_id=1, source_target_pairs={{0,2},{1,3},{2,0},{3,1},{4,6},{5,7},{6,4},{7,5},{8,10},{9,11},{10,... | collective-permute-start | bytes 2359304 | tf_op jit(solution)/shard_map/ppermute | solution.py:114
  92.7 35.7 %collective-permute-start = (bf16[512,768]{1,0:T(8,128)(2,1)S(1)}, bf16[512,768]{1,0:T(8,128)(2,1)}, u32[]{:S(2)}, u32[]{:S(2)}) collective-permute-start(bf16[512,768]{1,0:T(8,128)(2,1)S(1)} %get-tuple-element.8), channel_id=1, source_target_pairs={{0,1},{1,2},{2,3},{3,0},{4,5},{5,6},{6,7},{7,4},{8,9},{9,10},{10,1... | collective-permute-start | bytes 2359304 | tf_op jit(solution)/shard_map/ppermute | solution.py:114
  131.0 9.8 %copy-start.1 = (f32[192,768]{1,0:T(8,128)}, f32[192,768]{1,0:T(8,128)S(1)}, u32[]{:S(2)}) copy-start(f32[192,768]{1,0:T(8,128)S(1)} %convolution_multiply_fusion) | copy-start | bytes 1769476

commit v5 on v4

--- a/solution.py
+++ b/solution.py
@@ -78,6 +78,9 @@
     upper_matrix = up_weight[0]
     down_matrix = down_weight[0]
     arrived = lax.all_to_all(outgoing, "expert", split_axis=0, concat_axis=0, tiled=True)
+    arrived, route_hit, route_weight, slot_marks = lax.optimization_barrier(
+        (arrived, route_hit, route_weight, slot_marks)
+    )
     item_count = arrived.shape[1]
     hidden, output = swiglu_rows(
         arrived.reshape(-1, model_width), gate_matrix, upper_matrix, down_matrix

time: 141 us -> 155 us (1.099)
  blocking collectives: 58.4 us -> 0 us
  waiting for transfers between devices: 14.9 us -> 68.5 us
  matrix products: 16.2 us -> 28.6 us
  starting transfers between devices: 13.9 us -> 21.6 us
    all_to_all x1 -> x0, blocking collectives: 58.4 us -> none  [per_device(): lax.all_to_all(outgoing, 'expert', split_axis=0, concat_axis=0, tiled=True)]
    all_to_all x0 -> x1, waiting for transfers between devices: none -> 53.9 us  [per_device(): lax.all_to_all(outgoing, 'expert', split_axis=0, concat_axis=0, tiled=True)]
    all_to_all x0 -> x1, starting transfers between devices: none -> 7.56 us  [per_device(): lax.all_to_all(outgoing, 'expert', split_axis=0, concat_axis=0, tiled=True)]
    dot_general x1, matrix products: 4.3 us -> 8.34 us  [swiglu_rows(): jnp.dot(flat_rows, upper_matrix, preferred_element_type=jnp.float32)]
    dot_general x1, matrix products: 3.43 us -> 7.04 us  [swiglu_rows(): jnp.dot(flat_rows, gate_matrix, preferred_element_type=jnp.float32)]
    dot_general x1, matrix products: 4.98 us -> 7.74 us  [swiglu_rows(): jnp.dot(hidden, down_matrix, preferred_element_type=jnp.float32)]
    dot_general x1, matrix products: 1.28 us -> 3.21 us  [per_device(): lax.dot_general(selector, tokens, (((0,), (0,)), ((), ())), preferred_ele...]
  transfers between devices with their start and end apart: 7 -> 8, of which waited for: 4 -> 4; matrix products, arithmetic and copies ran while one was open for 21% -> 19% of each run, Pallas kernels for 0% -> 0%
where the time goes in v5:
time: 155 us
  waiting for transfers between devices  68.5 us (44%)
  matrix products  28.6 us (18%)
  other arithmetic  27.8 us (18%)
  starting transfers between devices  21.6 us (14%)
  Pallas kernels  4.88 us (3%)
  local copies, waits for them, and re-layouts  1.71 us (1%)
    all_to_all x1, waiting for transfers between devices, per_device(): lax.all_to_all(outgoing, 'expert', split_axis=0, concat_axis=0, tiled=True)  53.9 us
    another operation x3, other arithmetic, per_device(): jnp.linalg.cholesky(corner + damping * jnp.eye(PANEL, dtype=jnp.float32))  12.4 us
    another operation x2, other arithmetic, per_device(): jax.scipy.linalg.solve_triangular(lower_factor, leading.T, lower=True)  10.5 us
    ppermute x3, waiting for transfers between devices, per_device(): gathered.append(lax.ppermute(hidden, 'pair', ring))  9.72 us
    dot_general x1, matrix products, swiglu_rows(): jnp.dot(flat_rows, upper_matrix, preferred_element_type=jnp.float32)  8.34 us
    dot_general x1, matrix products, swiglu_rows(): jnp.dot(hidden, down_matrix, preferred_element_type=jnp.float32)  7.74 us
    all_to_all x1, starting transfers between devices, per_device(): lax.all_to_all(outgoing, 'expert', split_axis=0, concat_axis=0, tiled=True)  7.56 us
    dot_general x1, matrix products, swiglu_rows(): jnp.dot(flat_rows, gate_matrix, preferred_element_type=jnp.float32)  7.04 us
  transfers between devices with their start and end apart: 8, of which 4 were waited for; matrix products, arithmetic and copies ran while one was open for 19% of the time, Pallas kernels for 0%

profile of v5, /device:TPU:0, one launch (start us, length us, event | category | flops | bytes accessed | tf_op | source)
XLA Modules:
  0.0 154.5 jit_solution(9319257445932386030)
XLA Ops:
  0.6 0.8 fusion.28
  1.4 0.7 add_select_fusion
  2.8 3.2 %convolution_convert_fusion = bf16[512,4096]{1,0:T(8,128)(2,1)} fusion(bf16[128,512]{0,1:T(8,128)(2,1)S(1)} %fusion.13, bf16[128,4096]{1,0:T(8,128)(2,1)S(1)} %copy-done), kind=kOutput, calls=%fused_computation.6 | convolution fusion | flops 538968064 | bytes 5373952 | tf_op jit(solution)/shard_map/dot_general | solution.py:73
  6.0 7.6 %all-to-all-start = ((bf16[32,16,4096]{2,1,0:T(8,128)(2,1)}), bf16[32,16,4096]{2,1,0:T(8,128)(2,1)}, u32[]{:S(2)}, u32[]{:S(2)}) async-start(bf16[32,16,4096]{2,1,0:T(8,128)(2,1)} %bitcast.47), calls=%async_computation | async-start | bytes 8388608 | tf_op jit(solution)/shard_map/all_to_all | solution.py:80
  13.7 53.9 %all-to-all-done = bf16[32,16,4096]{2,1,0:T(8,128)(2,1)} async-done(((bf16[32,16,4096]{2,1,0:T(8,128)(2,1)}), bf16[32,16,4096]{2,1,0:T(8,128)(2,1)}, u32[]{:S(2)}, u32[]{:S(2)}) %all-to-all-start) | async-done | bytes 4194336 | tf_op jit(solution)/shard_map/all_to_all | solution.py:80
  67.6 7.0 %fusion.4 = f32[512,768]{1,0:T(8,128)S(1)} fusion(bf16[512,4096]{1,0:T(8,128)(2,1)} %bitcast.4, bf16[1,4096,768]{2,1,0:T(8,128)(2,1)} %param.9), kind=kOutput, calls=%fused_computation.4 | convolution fusion | flops 3221225472 | bytes 12058624 | tf_op jit(solution)/shard_map/dot_general | solution.py:15
  74.6 8.3 %multiply_reduce_fusion = (f32[]{:T(128)}, bf16[512,768]{1,0:T(8,128)(2,1)S(1)}) fusion(bf16[512,4096]{1,0:T(8,128)(2,1)} %bitcast.4, bf16[1,4096,768]{2,1,0:T(8,128)(2,1)} %param.10, f32[512,768]{1,0:T(8,128)S(1)} %fusion.4), kind=kOutput, calls=%fused_computation.9 | convolution fusion | flops 3224764416 | bytes 12845060 | tf_op jit(solution)/shard_map/dot_general | solution.py:16
  83.0 7.7 %fusion.6 = bf16[512,4096]{1,0:T(8,128)(2,1)} fusion(bf16[512,768]{1,0:T(8,128)(2,1)S(1)} %get-tuple-element.16, bf16[1,768,4096]{2,1,0:T(8,128)(2,1)} %param.11), kind=kOutput, calls=%fused_computation.7 | convolution fusion | flops 3223322624 | bytes 11272192 | tf_op jit(solution)/shard_map/dot_general | solution.py:18
  90.7 5.0 %all-to-all-start.1 = ((bf16[32,16,4096]{2,1,0:T(8,128)(2,1)}), bf16[32,16,4096]{2,1,0:T(8,128)(2,1)}, u32[]{:S(2)}, u32[]{:S(2)}) async-start(bf16[32,16,4096]{2,1,0:T(8,128)(2,1)} %bitcast.48), calls=%async_computation.1 | async-start | bytes 8388608 | tf_op jit(solution)/shard_map/all_to_all | solution.py:89
  96.6 4.0 %collective-permute-start.4 = (f32[136,128]{1,0:T(8,128)S(1)}, f32[136,128]{1,0:T(8,128)S(1)}, u32[]{:S(2)}, u32[]{:S(2)}) collective-permute-start(f32[136,128]{1,0:T(8,128)S(1)} %concatenate.7), channel_id=1, source_target_pairs={{0,2},{1,3},{2,0},{3,1},{4,6},{5,7},{6,4},{7,5},{8,10},{9,11},{10,... | collective-permute-start | bytes 208904 | tf_op jit(solution)/shard_map/ppermute | solution.py:110
  100.5 0.7 collective-permute-start.5
  101.3 1.3 collective-permute-start.3
  102.6 1.9 %collective-permute-start.2 = (bf16[512,768]{1,0:T(8,128)(2,1)S(1)}, bf16[512,768]{1,0:T(8,128)(2,1)S(1)}, u32[]{:S(2)}, u32[]{:S(2)}) collective-permute-start(bf16[512,768]{1,0:T(8,128)(2,1)S(1)} %get-tuple-element.16), channel_id=1, source_target_pairs={{0,3},{1,0},{2,1},{3,2},{4,7},{5,4},{6,5},{7,6},{8,11},{9,8},{10,9... | collective-permute-start | bytes 2359304 | tf_op jit(solution)/shard_map/ppermute | solution.py:117
  104.5 1.2 collective-permute-start.1
  105.9 0.7 fusion.12
  106.8 0.7 add_add_fusion
  108.8 11.7 %cholesky.16 = f32[128,128]{1,0:T(8,128)S(1)} custom-call(f32[128,128]{1,0:T(8,128)S(1)} %fusion.23), custom_call_target="Cholesky" | custom-call | tf_op jit(solution)/shard_map/jit(cholesky)/cholesky | solution.py:113
  121.8 9.8 %custom-call.7 = f32[1,128,128]{1,2,0:T(8,128)S(1)} custom-call(f32[1,128,128]{2,1,0:T(8,128)S(1)} %fusion.20), custom_call_target="InvertDiagBlocksLowerTriangular" | custom-call | tf_op jit(solution)/shard_map/jit(_solve_triangular)/triangular_solve | solution.py:129
  131.7 9.7 %collective-permute-done = bf16[512,768]{1,0:T(8,128)(2,1)} collective-permute-done((bf16[512,768]{1,0:T(8,128)(2,1)S(1)}, bf16[512,768]{1,0:T(8,128)(2,1)}, u32[]{:S(2)}, u32[]{:S(2)}) %collective-permute-start) | collective-permute-done | bytes 786464 | tf_op jit(solution)/shard_map/ppermute | solution.py:117
  141.4 1.5 pad_maximum_fusion
  142.9 1.1 convolution_multiply_fusion
  144.0 0.9 convolution_bitcast_fusion
  144.9 4.7 %all-to-all-done.1 = bf16[32,16,4096]{2,1,0:T(8,128)(2,1)} async-done(((bf16[32,16,4096]{2,1,0:T(8,128)(2,1)}), bf16[32,16,4096]{2,1,0:T(8,128)(2,1)}, u32[]{:S(2)}, u32[]{:S(2)}) %all-to-all-start.1) | async-done | bytes 4194336 | tf_op jit(solution)/shard_map/all_to_all | solution.py:89
  149.6 4.9 %shard_map.85 = bf16[128,4096]{1,0:T(8,128)(2,1)} custom-call(bf16[128,512]{1,0:T(8,128)(2,1)} %get-tuple-element.14.high_ref, bf16[128,512]{1,0:T(8,128)(2,1)} %get-tuple-element.13.low_ref, bf16[512,4096]{1,0:T(8,128)(2,1)} %bitcast.9.rows_ref), custom_call_target="tpu_custom_call" | custom-call | flops 1073741824 | bytes 5505024 | tf_op jit(solution)/shard_map/pallas_call | solution.py:38
  (36 shorter events, 4.0 us)
Async XLA Ops:
  0.6 2.2 %copy-start = (bf16[128,4096]{1,0:T(8,128)(2,1)S(1)}, bf16[128,4096]{1,0:T(8,128)(2,1)}, u32[]{:S(2)}) copy-start(bf16[128,4096]{1,0:T(8,128)(2,1)} %param.6) | copy-start | bytes 3145732
  6.0 61.5 %all-to-all-start = ((bf16[32,16,4096]{2,1,0:T(8,128)(2,1)}), bf16[32,16,4096]{2,1,0:T(8,128)(2,1)}, u32[]{:S(2)}, u32[]{:S(2)}) async-start(bf16[32,16,4096]{2,1,0:T(8,128)(2,1)} %bitcast.47), calls=%async_computation | async-start | bytes 8388608 | tf_op jit(solution)/shard_map/all_to_all | solution.py:80
  90.7 15.0 %copy-start.2 = (f32[128,8]{0,1:T(8,128)S(1)}, f32[128,8]{0,1:T(8,128)}, u32[]{:S(2)}) copy-start(f32[128,8]{0,1:T(8,128)} %param.8) | copy-start | bytes 12292
  90.7 58.9 %all-to-all-start.1 = ((bf16[32,16,4096]{2,1,0:T(8,128)(2,1)}), bf16[32,16,4096]{2,1,0:T(8,128)(2,1)}, u32[]{:S(2)}, u32[]{:S(2)}) async-start(bf16[32,16,4096]{2,1,0:T(8,128)(2,1)} %bitcast.48), calls=%async_computation.1 | async-start | bytes 8388608 | tf_op jit(solution)/shard_map/all_to_all | solution.py:89
  96.6 10.0 %collective-permute-start.4 = (f32[136,128]{1,0:T(8,128)S(1)}, f32[136,128]{1,0:T(8,128)S(1)}, u32[]{:S(2)}, u32[]{:S(2)}) collective-permute-start(f32[136,128]{1,0:T(8,128)S(1)} %concatenate.7), channel_id=1, source_target_pairs={{0,2},{1,3},{2,0},{3,1},{4,6},{5,7},{6,4},{7,5},{8,10},{9,11},{10,... | collective-permute-start | bytes 208904 | tf_op jit(solution)/shard_map/ppermute | solution.py:110
  100.5 6.1 %collective-permute-start.5 = (f32[136,128]{1,0:T(8,128)S(1)}, f32[136,128]{1,0:T(8,128)S(1)}, u32[]{:S(2)}, u32[]{:S(2)}) collective-permute-start(f32[136,128]{1,0:T(8,128)S(1)} %concatenate.7), channel_id=1, source_target_pairs={{0,3},{1,0},{2,1},{3,2},{4,7},{5,4},{6,5},{7,6},{8,11},{9,8},{10,9... | collective-permute-start | bytes 208904 | tf_op jit(solution)/shard_map/ppermute | solution.py:110
  101.3 5.5 %collective-permute-start.3 = (f32[136,128]{1,0:T(8,128)S(1)}, f32[136,128]{1,0:T(8,128)S(1)}, u32[]{:S(2)}, u32[]{:S(2)}) collective-permute-start(f32[136,128]{1,0:T(8,128)S(1)} %concatenate.7), channel_id=1, source_target_pairs={{0,1},{1,2},{2,3},{3,0},{4,5},{5,6},{6,7},{7,4},{8,9},{9,10},{10,1... | collective-permute-start | bytes 208904 | tf_op jit(solution)/shard_map/ppermute | solution.py:110
  102.6 29.1 %collective-permute-start.2 = (bf16[512,768]{1,0:T(8,128)(2,1)S(1)}, bf16[512,768]{1,0:T(8,128)(2,1)S(1)}, u32[]{:S(2)}, u32[]{:S(2)}) collective-permute-start(bf16[512,768]{1,0:T(8,128)(2,1)S(1)} %get-tuple-element.16), channel_id=1, source_target_pairs={{0,3},{1,0},{2,1},{3,2},{4,7},{5,4},{6,5},{7,6},{8,11},{9,8},{10,9... | collective-permute-start | bytes 2359304 | tf_op jit(solution)/shard_map/ppermute | solution.py:117
  104.5 27.1 %collective-permute-start.1 = (bf16[512,768]{1,0:T(8,128)(2,1)S(1)}, bf16[512,768]{1,0:T(8,128)(2,1)}, u32[]{:S(2)}, u32[]{:S(2)}) collective-permute-start(bf16[512,768]{1,0:T(8,128)(2,1)S(1)} %get-tuple-element.16), channel_id=1, source_target_pairs={{0,2},{1,3},{2,0},{3,1},{4,6},{5,7},{6,4},{7,5},{8,10},{9,11},{10,... | collective-permute-start | bytes 2359304 | tf_op jit(solution)/shard_map/ppermute | solution.py:117
  106.6 34.8 %collective-permute-start = (bf16[512,768]{1,0:T(8,128)(2,1)S(1)}, bf16[512,768]{1,0:T(8,128)(2,1)}, u32[]{:S(2)}, u32[]{:S(2)}) collective-permute-start(bf16[512,768]{1,0:T(8,128)(2,1)S(1)} %get-tuple-element.16), channel_id=1, source_target_pairs={{0,1},{1,2},{2,3},{3,0},{4,5},{5,6},{6,7},{7,4},{8,9},{9,10},{10,1... | collective-permute-start | bytes 2359304 | tf_op jit(solution)/shard_map/ppermute | solution.py:117
  144.0 10.5 %copy-start.1 = (f32[192,768]{1,0:T(8,128)}, f32[192,768]{1,0:T(8,128)S(1)}, u32[]{:S(2)}) copy-start(f32[192,768]{1,0:T(8,128)S(1)} %convolution_multiply_fusion) | copy-start | bytes 1769476

commit v6 on v4

--- a/solution.py
+++ b/solution.py
@@ -34,7 +34,7 @@
 def combine_rows(weight_high, weight_low, rows):
     tok_count, slot_count = weight_high.shape
     width = rows.shape[1]
-    block = 1024
+    block = 2048
     return pl.pallas_call(
         combine_kernel,
         out_shape=jax.ShapeDtypeStruct((tok_count, width), jnp.bfloat16),
@@ -65,11 +65,12 @@
     route_hit = (in_flight[:, :, None] & (owner_of[:, :, None] == columns)).astype(jnp.int32)
     picked = jnp.sum(route_hit, axis=1)
     before = jnp.cumsum(picked, axis=0) - picked
-    kept_rows = picked * (before < CAP).astype(jnp.int32)
-    slot_ids = lax.broadcasted_iota(jnp.int32, (1, 1, CAP), 2)
-    slot_marks = kept_rows[:, :, None] * (before[:, :, None] == slot_ids).astype(jnp.int32)
-    marks_flat = slot_marks.reshape(tok_count, owners * CAP)
-    selector = marks_flat.astype(jnp.bfloat16)
+    rank_choice = jnp.sum(route_hit * before[:, None, :], axis=2)
+    keep_choice = in_flight & (rank_choice < CAP)
+    target = jnp.where(keep_choice, owner_of * CAP + rank_choice, -1)
+    slot_iota = lax.broadcasted_iota(jnp.int32, (1, 1, owners * CAP), 2)
+    hits = target[:, :, None] == slot_iota
+    selector = jnp.any(hits, axis=1).astype(jnp.bfloat16)
     outgoing = lax.dot_general(
         selector, tokens, (((0,), (0,)), ((), ())), preferred_element_type=jnp.float32
     ).astype(jnp.bfloat16)
@@ -85,10 +86,7 @@
     results = output.reshape(owners, item_count, model_width)
     returned = lax.all_to_all(results, "expert", split_axis=0, concat_axis=0, tiled=True)
     returned_flat = returned.reshape(-1, model_width)
-    owner_weight = jnp.sum(route_hit.astype(jnp.float32) * route_weight[:, :, None], axis=1)
-    combine_matrix = (
-        slot_marks.astype(jnp.float32) * owner_weight[:, :, None]
-    ).reshape(tok_count, owners * CAP)
+    combine_matrix = jnp.sum(jnp.where(hits, route_weight[:, :, None], 0.0), axis=1)
     weight_high, weight_low = split_bf16(combine_matrix)
     combined = combine_rows(weight_high, weight_low, returned_flat)
     hess_scale = 2.0 / (CAP * owners * pair_count)

time: 141 us -> 140 us (level)
  waiting for transfers between devices: 14.9 us -> 10.1 us
  other arithmetic: 28.9 us -> 31.6 us
    ppermute x3, waiting for transfers between devices: 9.73 us -> 6 us  [per_device(): gathered.append(lax.ppermute(hidden, 'pair', ring))]
  transfers between devices with their start and end apart: 7 -> 7, of which waited for: 4 -> 3; matrix products, arithmetic and copies ran while one was open for 21% -> 24% of each run, Pallas kernels for 0% -> 0%
where the time goes in v6:
time: 140 us; the launch traced here: 139 us
  blocking collectives  58.4 us (42%)
  other arithmetic  31.6 us (23%)
  matrix products  16.2 us (12%)
  starting transfers between devices  15.2 us (11%)
  waiting for transfers between devices  10.1 us (7%)
  Pallas kernels  3.86 us (3%)
  local copies, waits for them, and re-layouts  2.51 us (2%)
  between operations  1.52 us (1%)
    all_to_all x1, blocking collectives, per_device(): lax.all_to_all(outgoing, 'expert', split_axis=0, concat_axis=0, tiled=True)  58.4 us
    another operation x3, other arithmetic, per_device(): jnp.linalg.cholesky(corner + damping * jnp.eye(PANEL, dtype=jnp.float32))  13.2 us
    another operation x2, other arithmetic, per_device(): jax.scipy.linalg.solve_triangular(lower_factor, leading.T, lower=True)  10.5 us
    ppermute x3, starting transfers between devices, per_device(): pack_sum = pack_sum + lax.ppermute(pack, 'pair', ring)  6.57 us
    ppermute x3, waiting for transfers between devices, per_device(): gathered.append(lax.ppermute(hidden, 'pair', ring))  6 us
    all_to_all x1, starting transfers between devices, per_device(): lax.all_to_all(results, 'expert', split_axis=0, concat_axis=0, tiled=True)  4.98 us
    dot_general x1, matrix products, swiglu_rows(): jnp.dot(hidden, down_matrix, preferred_element_type=jnp.float32)  4.98 us
    dot_general x1, matrix products, swiglu_rows(): jnp.dot(flat_rows, upper_matrix, preferred_element_type=jnp.float32)  4.27 us
  transfers between devices with their start and end apart: 7, of which 3 were waited for; matrix products, arithmetic and copies ran while one was open for 24% of the time, Pallas kernels for 0%

profile of v6, /device:TPU:0, one launch (start us, length us, event | category | flops | bytes accessed | tf_op | source)
XLA Modules:
  0.0 139.4 jit_solution(14576339081966925991)
XLA Ops:
  0.6 0.8 add_select_fusion
  2.6 0.7 add_select_fusion.2
  3.4 0.7 fusion.9
  4.1 1.3 convolution_convert_fusion
  5.4 58.4 %all_to_all.10 = bf16[32,16,4096]{2,1,0:T(8,128)(2,1)S(1)} all-to-all(bf16[32,16,4096]{2,1,0:T(8,128)(2,1)S(1)} %bitcast.38), channel_id=1, replica_groups=mesh['expert'=32,'pair'=4] {'expert'}, dimensions={0} | all-to-all | bytes 8388608 | tf_op jit(solution)/shard_map/all_to_all | solution.py:81
  63.9 3.4 %fusion.4 = f32[512,768]{1,0:T(8,128)S(1)} fusion(bf16[512,4096]{1,0:T(8,128)(2,1)S(1)} %bitcast.40, bf16[1,4096,768]{2,1,0:T(8,128)(2,1)S(1)} %bitcast.44), kind=kOutput, calls=%fused_computation.4 | convolution fusion | flops 3221225472 | bytes 12058624 | tf_op jit(solution)/shard_map/dot_general | solution.py:15
  67.3 4.3 %multiply_reduce_fusion = (f32[]{:T(128)}, bf16[512,768]{1,0:T(8,128)(2,1)S(1)}) fusion(bf16[512,4096]{1,0:T(8,128)(2,1)S(1)} %bitcast.41, bf16[1,4096,768]{2,1,0:T(8,128)(2,1)S(1)} %bitcast.46, f32[512,768]{1,0:T(8,128)S(1)} %fusion.4), kind=kOutput, calls=%fused_computation.12 | convolution fusion | flops 3224764416 | bytes 12845060 | tf_op jit(solution)/shard_map/dot_general | solution.py:16
  71.6 5.0 %fusion.6 = bf16[512,4096]{1,0:T(8,128)(2,1)} fusion(bf16[512,768]{1,0:T(8,128)(2,1)S(1)} %get-tuple-element.6, bf16[1,768,4096]{2,1,0:T(8,128)(2,1)S(1)} %bitcast.48), kind=kOutput, calls=%fused_computation.7 | convolution fusion | flops 3223322624 | bytes 11272192 | tf_op jit(solution)/shard_map/dot_general | solution.py:18
  76.6 5.0 %all-to-all-start.1 = ((bf16[32,16,4096]{2,1,0:T(8,128)(2,1)}), bf16[32,16,4096]{2,1,0:T(8,128)(2,1)}, u32[]{:S(2)}, u32[]{:S(2)}) async-start(bf16[32,16,4096]{2,1,0:T(8,128)(2,1)} %bitcast.39), calls=%async_computation.1 | async-start | bytes 8388608 | tf_op jit(solution)/shard_map/all_to_all | solution.py:87
  82.4 0.7 fusion.13
  84.0 2.0 %collective-permute-start.3 = (f32[136,128]{1,0:T(8,128)S(1)}, f32[136,128]{1,0:T(8,128)S(1)}, u32[]{:S(2)}, u32[]{:S(2)}) collective-permute-start(f32[136,128]{1,0:T(8,128)S(1)} %concatenate.7), channel_id=1, source_target_pairs={{0,1},{1,2},{2,3},{3,0},{4,5},{5,6},{6,7},{7,4},{8,9},{9,10},{10,1... | collective-permute-start | bytes 208904 | tf_op jit(solution)/shard_map/ppermute | solution.py:105
  86.0 3.6 %collective-permute-start.4 = (f32[136,128]{1,0:T(8,128)S(1)}, f32[136,128]{1,0:T(8,128)S(1)}, u32[]{:S(2)}, u32[]{:S(2)}) collective-permute-start(f32[136,128]{1,0:T(8,128)S(1)} %concatenate.7), channel_id=1, source_target_pairs={{0,2},{1,3},{2,0},{3,1},{4,6},{5,7},{6,4},{7,5},{8,10},{9,11},{10,... | collective-permute-start | bytes 208904 | tf_op jit(solution)/shard_map/ppermute | solution.py:105
  89.6 1.0 collective-permute-start.5
  90.6 1.0 collective-permute-start
  92.0 2.2 %collective-permute-start.2 = (bf16[512,768]{1,0:T(8,128)(2,1)S(1)}, bf16[512,768]{1,0:T(8,128)(2,1)}, u32[]{:S(2)}, u32[]{:S(2)}) collective-permute-start(bf16[512,768]{1,0:T(8,128)(2,1)S(1)} %get-tuple-element.6), channel_id=1, source_target_pairs={{0,3},{1,0},{2,1},{3,2},{4,7},{5,4},{6,5},{7,6},{8,11},{9,8},{10,9... | collective-permute-start | bytes 2359304 | tf_op jit(solution)/shard_map/ppermute | solution.py:112
  96.8 0.9 copy.19
  98.3 12.5 %cholesky.16 = f32[128,128]{1,0:T(8,128)S(1)} custom-call(f32[128,128]{1,0:T(8,128)} %fusion.21), custom_call_target="Cholesky" | custom-call | tf_op jit(solution)/shard_map/jit(cholesky)/cholesky | solution.py:108
  112.2 9.8 %custom-call.7 = f32[1,128,128]{1,2,0:T(8,128)S(1)} custom-call(f32[1,128,128]{2,1,0:T(8,128)S(1)} %fusion.18), custom_call_target="InvertDiagBlocksLowerTriangular" | custom-call | tf_op jit(solution)/shard_map/jit(_solve_triangular)/triangular_solve | solution.py:124
  122.1 5.5 %collective-permute-done = bf16[512,768]{1,0:T(8,128)(2,1)S(1)} collective-permute-done((bf16[512,768]{1,0:T(8,128)(2,1)S(1)}, bf16[512,768]{1,0:T(8,128)(2,1)S(1)}, u32[]{:S(2)}, u32[]{:S(2)}) %collective-permute-start) | collective-permute-done | bytes 786464 | tf_op jit(solution)/shard_map/ppermute | solution.py:112
  128.1 1.3 pad_maximum_fusion
  129.4 1.1 convolution_multiply_fusion
  130.5 0.9 convolution_bitcast_fusion
  131.4 4.1 %all-to-all-done.1 = bf16[32,16,4096]{2,1,0:T(8,128)(2,1)} async-done(((bf16[32,16,4096]{2,1,0:T(8,128)(2,1)}), bf16[32,16,4096]{2,1,0:T(8,128)(2,1)}, u32[]{:S(2)}, u32[]{:S(2)}) %all-to-all-start.1) | async-done | bytes 4194336 | tf_op jit(solution)/shard_map/all_to_all | solution.py:87
  135.5 3.9 %shard_map.85 = bf16[128,4096]{1,0:T(8,128)(2,1)} custom-call(bf16[128,512]{1,0:T(8,128)(2,1)} %get-tuple-element.4.high_ref, bf16[128,512]{1,0:T(8,128)(2,1)} %get-tuple-element.3.low_ref, bf16[512,4096]{1,0:T(8,128)(2,1)} %bitcast.6.rows_ref), custom_call_target="tpu_custom_call" | custom-call | flops 1073741824 | bytes 5505024 | tf_op jit(solution)/shard_map/pallas_call | solution.py:38
  (47 shorter events, 7.7 us)
Async XLA Ops:
  0.6 3.4 %copy-start = (bf16[128,4096]{1,0:T(8,128)(2,1)S(1)}, bf16[128,4096]{1,0:T(8,128)(2,1)}, u32[]{:S(2)}) copy-start(bf16[128,4096]{1,0:T(8,128)(2,1)} %param.6) | copy-start | bytes 3145732
  4.1 59.8 %slice-start = ((s8[6291456]{0:T(1024)(128)(4,1)}), s8[4194304]{0:T(1024)(128)(4,1)S(1)}, s32[]{:S(2)}) async-start(s8[6291456]{0:T(1024)(128)(4,1)} %bitcast.43), calls=%async_computation.2 | async-start | bytes 8388608
  5.4 58.5 %slice-start.1 = ((s8[6291456]{0:T(1024)(128)(4,1)}), s8[2097152]{0:T(1024)(128)(4,1)S(1)}, s32[]{:S(2)}) async-start(s8[6291456]{0:T(1024)(128)(4,1)} %bitcast.43), calls=%async_computation.3 | async-start | bytes 4194304
  5.4 61.9 %slice-start.2 = ((s8[6291456]{0:T(1024)(128)(4,1)}), s8[4194304]{0:T(1024)(128)(4,1)S(1)}, s32[]{:S(2)}) async-start(s8[6291456]{0:T(1024)(128)(4,1)} %bitcast.45), calls=%async_computation.4 | async-start | bytes 8388608
  5.4 66.2 %slice-start.4 = ((s8[6291456]{0:T(1024)(128)(4,1)}), s8[4194304]{0:T(1024)(128)(4,1)S(1)}, s32[]{:S(2)}) async-start(s8[6291456]{0:T(1024)(128)(4,1)} %bitcast.47), calls=%async_computation.6 | async-start | bytes 8388608
  63.9 3.4 %slice-start.3 = ((s8[6291456]{0:T(1024)(128)(4,1)}), s8[2097152]{0:T(1024)(128)(4,1)S(1)}, s32[]{:S(2)}) async-start(s8[6291456]{0:T(1024)(128)(4,1)} %bitcast.45), calls=%async_computation.5 | async-start | bytes 4194304
  63.9 7.7 %slice-start.5 = ((s8[6291456]{0:T(1024)(128)(4,1)}), s8[2097152]{0:T(1024)(128)(4,1)S(1)}, s32[]{:S(2)}) async-start(s8[6291456]{0:T(1024)(128)(4,1)} %bitcast.47), calls=%async_computation.7 | async-start | bytes 4194304
  76.6 5.0 %copy-start.2 = (f32[128,8]{0,1:T(8,128)S(1)}, f32[128,8]{0,1:T(8,128)}, u32[]{:S(2)}) copy-start(f32[128,8]{0,1:T(8,128)} %param.8) | copy-start | bytes 12292
  76.6 58.9 %all-to-all-start.1 = ((bf16[32,16,4096]{2,1,0:T(8,128)(2,1)}), bf16[32,16,4096]{2,1,0:T(8,128)(2,1)}, u32[]{:S(2)}, u32[]{:S(2)}) async-start(bf16[32,16,4096]{2,1,0:T(8,128)(2,1)} %bitcast.39), calls=%async_computation.1 | async-start | bytes 8388608 | tf_op jit(solution)/shard_map/all_to_all | solution.py:87
  84.0 8.0 %collective-permute-start.3 = (f32[136,128]{1,0:T(8,128)S(1)}, f32[136,128]{1,0:T(8,128)S(1)}, u32[]{:S(2)}, u32[]{:S(2)}) collective-permute-start(f32[136,128]{1,0:T(8,128)S(1)} %concatenate.7), channel_id=1, source_target_pairs={{0,1},{1,2},{2,3},{3,0},{4,5},{5,6},{6,7},{7,4},{8,9},{9,10},{10,1... | collective-permute-start | bytes 208904 | tf_op jit(solution)/shard_map/ppermute | solution.py:105
  86.0 8.3 %collective-permute-start.4 = (f32[136,128]{1,0:T(8,128)S(1)}, f32[136,128]{1,0:T(8,128)S(1)}, u32[]{:S(2)}, u32[]{:S(2)}) collective-permute-start(f32[136,128]{1,0:T(8,128)S(1)} %concatenate.7), channel_id=1, source_target_pairs={{0,2},{1,3},{2,0},{3,1},{4,6},{5,7},{6,4},{7,5},{8,10},{9,11},{10,... | collective-permute-start | bytes 208904 | tf_op jit(solution)/shard_map/ppermute | solution.py:105
  89.6 4.7 %collective-permute-start.5 = (f32[136,128]{1,0:T(8,128)S(1)}, f32[136,128]{1,0:T(8,128)S(1)}, u32[]{:S(2)}, u32[]{:S(2)}) collective-permute-start(f32[136,128]{1,0:T(8,128)S(1)} %concatenate.7), channel_id=1, source_target_pairs={{0,3},{1,0},{2,1},{3,2},{4,7},{5,4},{6,5},{7,6},{8,11},{9,8},{10,9... | collective-permute-start | bytes 208904 | tf_op jit(solution)/shard_map/ppermute | solution.py:105
  90.6 37.0 %collective-permute-start = (bf16[512,768]{1,0:T(8,128)(2,1)S(1)}, bf16[512,768]{1,0:T(8,128)(2,1)S(1)}, u32[]{:S(2)}, u32[]{:S(2)}) collective-permute-start(bf16[512,768]{1,0:T(8,128)(2,1)S(1)} %get-tuple-element.6), channel_id=1, source_target_pairs={{0,1},{1,2},{2,3},{3,0},{4,5},{5,6},{6,7},{7,4},{8,9},{9,10},{10,1... | collective-permute-start | bytes 2359304 | tf_op jit(solution)/shard_map/ppermute | solution.py:112
  91.6 36.0 %collective-permute-start.1 = (bf16[512,768]{1,0:T(8,128)(2,1)S(1)}, bf16[512,768]{1,0:T(8,128)(2,1)S(1)}, u32[]{:S(2)}, u32[]{:S(2)}) collective-permute-start(bf16[512,768]{1,0:T(8,128)(2,1)S(1)} %get-tuple-element.6), channel_id=1, source_target_pairs={{0,2},{1,3},{2,0},{3,1},{4,6},{5,7},{6,4},{7,5},{8,10},{9,11},{10,... | collective-permute-start | bytes 2359304 | tf_op jit(solution)/shard_map/ppermute | solution.py:112
  92.0 36.0 %collective-permute-start.2 = (bf16[512,768]{1,0:T(8,128)(2,1)S(1)}, bf16[512,768]{1,0:T(8,128)(2,1)}, u32[]{:S(2)}, u32[]{:S(2)}) collective-permute-start(bf16[512,768]{1,0:T(8,128)(2,1)S(1)} %get-tuple-element.6), channel_id=1, source_target_pairs={{0,3},{1,0},{2,1},{3,2},{4,7},{5,4},{6,5},{7,6},{8,11},{9,8},{10,9... | collective-permute-start | bytes 2359304 | tf_op jit(solution)/shard_map/ppermute | solution.py:112
  130.5 8.9 %copy-start.1 = (f32[192,768]{1,0:T(8,128)}, f32[192,768]{1,0:T(8,128)S(1)}, u32[]{:S(2)}) copy-start(f32[192,768]{1,0:T(8,128)S(1)} %convolution_multiply_fusion) | copy-start | bytes 1769476

commit v7 on v6

--- a/solution.py
+++ b/solution.py
@@ -53,27 +53,78 @@
     )(weight_high, weight_low, rows)
 
 
+def route_kernel(ids_ref, tokens_ref, out_ref, target_ref):
+    tok_count, choices = ids_ref.shape
+    owners = out_ref.shape[0] // CAP
+    per_owner = EXPERTS // owners
+    ids = ids_ref[...]
+    in_flight = (ids % per_owner) == 0
+    owner_of = ids // per_owner
+    owner_iota = lax.broadcasted_iota(jnp.int32, (tok_count, owners), 1)
+    matches = []
+    picked = jnp.zeros((tok_count, owners), jnp.float32)
+    for k in range(choices):
+        hit = (owner_of[:, k : k + 1] == owner_iota) & in_flight[:, k : k + 1]
+        matches.append(hit)
+        picked = picked + hit.astype(jnp.float32)
+    row = lax.broadcasted_iota(jnp.int32, (tok_count, tok_count), 0)
+    col = lax.broadcasted_iota(jnp.int32, (tok_count, tok_count), 1)
+    earlier = (col < row).astype(jnp.bfloat16)
+    before = jnp.dot(earlier, picked.astype(jnp.bfloat16), preferred_element_type=jnp.float32)
+    slot_iota = lax.broadcasted_iota(jnp.int32, (tok_count, owners * CAP), 1)
+    selector = jnp.zeros((tok_count, owners * CAP), jnp.float32)
+    targets = []
+    for k in range(choices):
+        rank = jnp.sum(jnp.where(matches[k], before, 0.0), axis=1, keepdims=True).astype(jnp.int32)
+        keep = in_flight[:, k : k + 1] & (rank < CAP)
+        target = jnp.where(keep, owner_of[:, k : k + 1] * CAP + rank, -1)
+        targets.append(target)
+        selector = selector + (target == slot_iota).astype(jnp.float32)
+    target_ref[...] = jnp.concatenate(targets, axis=1)
+    chosen = selector.T.astype(jnp.bfloat16)
+    width = tokens_ref.shape[1]
+    block = 1024
+    for c in range(width // block):
+        part = jnp.dot(
+            chosen, tokens_ref[:, c * block : (c + 1) * block], preferred_element_type=jnp.float32
+        )
+        out_ref[:, c * block : (c + 1) * block] = part.astype(out_ref.dtype)
+
+
+def route_rows(expert_ids, tokens, owners):
+    tok_count, choices = expert_ids.shape
+    width = tokens.shape[1]
+    slots = owners * CAP
+    return pl.pallas_call(
+        route_kernel,
+        out_shape=(
+            jax.ShapeDtypeStruct((slots, width), tokens.dtype),
+            jax.ShapeDtypeStruct((tok_count, choices), jnp.int32),
+        ),
+        in_specs=[
+            pl.BlockSpec(memory_space=pltpu.VMEM),
+            pl.BlockSpec(memory_space=pltpu.VMEM),
+        ],
+        out_specs=(
+            pl.BlockSpec(memory_space=pltpu.VMEM),
+            pl.BlockSpec(memory_space=pltpu.VMEM),
+        ),
+        compiler_params=pltpu.CompilerParams(vmem_limit_bytes=48 * 1024 * 1024),
+        cost_estimate=pl.CostEstimate(
+            flops=2 * slots * tok_count * width,
+            transcendentals=0,
+            bytes_accessed=2 * (slots * width + tok_count * width),
+        ),
+    )(expert_ids, tokens)
+
+
 def per_device(tokens, expert_ids, route_weight, gate_weight, up_weight, down_weight):
     owners = lax.axis_size("expert")
     pair_count = lax.axis_size("pair")
     tok_count = tokens.shape[0]
     model_width = tokens.shape[1]
     per_owner = EXPERTS // owners
-    in_flight = expert_ids % per_owner == 0
-    owner_of = expert_ids // per_owner
-    columns = lax.broadcasted_iota(jnp.int32, (1, 1, owners), 2)
-    route_hit = (in_flight[:, :, None] & (owner_of[:, :, None] == columns)).astype(jnp.int32)
-    picked = jnp.sum(route_hit, axis=1)
-    before = jnp.cumsum(picked, axis=0) - picked
-    rank_choice = jnp.sum(route_hit * before[:, None, :], axis=2)
-    keep_choice = in_flight & (rank_choice < CAP)
-    target = jnp.where(keep_choice, owner_of * CAP + rank_choice, -1)
-    slot_iota = lax.broadcasted_iota(jnp.int32, (1, 1, owners * CAP), 2)
-    hits = target[:, :, None] == slot_iota
-    selector = jnp.any(hits, axis=1).astype(jnp.bfloat16)
-    outgoing = lax.dot_general(
-        selector, tokens, (((0,), (0,)), ((), ())), preferred_element_type=jnp.float32
-    ).astype(jnp.bfloat16)
+    outgoing, target = route_rows(expert_ids, tokens, owners)
     outgoing = outgoing.reshape(owners, CAP, model_width)
     gate_matrix = gate_weight[0]
     upper_matrix = up_weight[0]
@@ -86,6 +137,8 @@
     results = output.reshape(owners, item_count, model_width)
     returned = lax.all_to_all(results, "expert", split_axis=0, concat_axis=0, tiled=True)
     returned_flat = returned.reshape(-1, model_width)
+    slot_iota = lax.broadcasted_iota(jnp.int32, (1, 1, owners * CAP), 2)
+    hits = target[:, :, None] == slot_iota
     combine_matrix = jnp.sum(jnp.where(hits, route_weight[:, :, None], 0.0), axis=1)
     weight_high, weight_low = split_bf16(combine_matrix)
     combined = combine_rows(weight_high, weight_low, returned_flat)

time: 140 us -> 139 us (level)
  other arithmetic: 31.6 us -> 25.3 us
  waiting for transfers between devices: 10.1 us -> 14 us
  Pallas kernels: 3.86 us -> 6.2 us
    ppermute x3, waiting for transfers between devices: 6 us -> 8.82 us  [per_device(): gathered.append(lax.ppermute(hidden, 'pair', ring))]
    pallas_call x0 -> x1, Pallas kernels: none -> 2.33 us  [route_rows(): pl.pallas_call(route_kernel, out_shape=(jax.ShapeDtypeStruct((slots, widt...]
    unnamed x19 -> x18, local copies, waits for them, and re-layouts: 0.16 us -> 2.15 us
    select_n x2 -> x0, other arithmetic: 1.49 us -> none  [the longest x1 0.78 us: per_device(): owner_of = expert_ids // per_owner]
  transfers between devices with their start and end apart: 7 -> 7, of which waited for: 3 -> 3; matrix products, arithmetic and copies ran while one was open for 24% -> 21% of each run, Pallas kernels for 0% -> 0%
where the time goes in v7:
time: 139 us
  blocking collectives  58.4 us (42%)
  other arithmetic  25.3 us (18%)
  starting transfers between devices  15.2 us (11%)
  matrix products  15 us (11%)
  waiting for transfers between devices  14 us (10%)
  Pallas kernels  6.2 us (4%)
  local copies, waits for them, and re-layouts  3.4 us (2%)
  between operations  1.47 us (1%)
    all_to_all x1, blocking collectives, per_device(): lax.all_to_all(outgoing, 'expert', split_axis=0, concat_axis=0, tiled=True)  58.4 us
    another operation x3, other arithmetic, per_device(): jnp.linalg.cholesky(corner + damping * jnp.eye(PANEL, dtype=jnp.float32))  12.4 us
    another operation x2, other arithmetic, per_device(): jax.scipy.linalg.solve_triangular(lower_factor, leading.T, lower=True)  10.5 us
    ppermute x3, waiting for transfers between devices, per_device(): gathered.append(lax.ppermute(hidden, 'pair', ring))  8.82 us
    ppermute x3, starting transfers between devices, per_device(): pack_sum = pack_sum + lax.ppermute(pack, 'pair', ring)  6.58 us
    all_to_all x1, waiting for transfers between devices, per_device(): lax.all_to_all(results, 'expert', split_axis=0, concat_axis=0, tiled=True)  5.16 us
    dot_general x1, matrix products, swiglu_rows(): jnp.dot(hidden, down_matrix, preferred_element_type=jnp.float32)  4.99 us
    all_to_all x1, starting transfers between devices, per_device(): lax.all_to_all(results, 'expert', split_axis=0, concat_axis=0, tiled=True)  4.98 us
  transfers between devices with their start and end apart: 7, of which 3 were waited for; matrix products, arithmetic and copies ran while one was open for 21% of the time, Pallas kernels for 0%

profile of v7, /device:TPU:0, one launch (start us, length us, event | category | flops | bytes accessed | tf_op | source)
XLA Modules:
  0.0 139.0 jit_solution(11230924825937561807)
XLA Ops:
  0.6 0.8 copy.12.ids_ref
  1.4 1.2 copy-done
  2.6 2.3 %shard_map.85 = (bf16[512,4096]{1,0:T(8,128)(2,1)S(1)}, s32[128,8]{1,0:T(8,128)S(1)}) custom-call(s32[128,8]{1,0:T(8,128)S(1)} %copy.12.ids_ref, bf16[128,4096]{1,0:T(8,128)(2,1)S(1)} %copy-done), custom_call_target="tpu_custom_call" | custom-call | flops 536870912 | bytes 5242880 | tf_op jit(solution)/shard_map/pallas_call | solution.py:98
  5.0 58.4 %all_to_all.10 = bf16[32,16,4096]{2,1,0:T(8,128)(2,1)S(1)} all-to-all(bf16[32,16,4096]{2,1,0:T(8,128)(2,1)S(1)} %bitcast.36), channel_id=1, replica_groups=mesh['expert'=32,'pair'=4] {'expert'}, dimensions={0} | all-to-all | bytes 8388608 | tf_op jit(solution)/shard_map/all_to_all | solution.py:132
  63.4 3.4 %fusion.4 = f32[512,768]{1,0:T(8,128)S(1)} fusion(bf16[512,4096]{1,0:T(8,128)(2,1)S(1)} %bitcast.38, bf16[1,4096,768]{2,1,0:T(8,128)(2,1)S(1)} %copy-done.3), kind=kOutput, calls=%fused_computation.4 | convolution fusion | flops 3221225472 | bytes 12058624 | tf_op jit(solution)/shard_map/dot_general | solution.py:15
  66.9 4.3 %multiply_reduce_fusion = (f32[]{:T(128)}, bf16[512,768]{1,0:T(8,128)(2,1)S(1)}) fusion(bf16[512,4096]{1,0:T(8,128)(2,1)S(1)} %bitcast.39, bf16[1,4096,768]{2,1,0:T(8,128)(2,1)S(1)} %bitcast.42, f32[512,768]{1,0:T(8,128)S(1)} %fusion.4), kind=kOutput, calls=%fused_computation.10 | convolution fusion | flops 3224764416 | bytes 12845060 | tf_op jit(solution)/shard_map/dot_general | solution.py:16
  71.2 5.0 %fusion.6 = bf16[512,4096]{1,0:T(8,128)(2,1)} fusion(bf16[512,768]{1,0:T(8,128)(2,1)S(1)} %get-tuple-element.10, bf16[1,768,4096]{2,1,0:T(8,128)(2,1)S(1)} %bitcast.44), kind=kOutput, calls=%fused_computation.6 | convolution fusion | flops 3223322624 | bytes 11272192 | tf_op jit(solution)/shard_map/dot_general | solution.py:18
  76.2 5.0 %all-to-all-start.1 = ((bf16[32,16,4096]{2,1,0:T(8,128)(2,1)}), bf16[32,16,4096]{2,1,0:T(8,128)(2,1)}, u32[]{:S(2)}, u32[]{:S(2)}) async-start(bf16[32,16,4096]{2,1,0:T(8,128)(2,1)} %bitcast.37), calls=%async_computation.1 | async-start | bytes 8388608 | tf_op jit(solution)/shard_map/all_to_all | solution.py:138
  81.3 0.7 select_reduce_fusion
  82.0 0.8 fusion.12
  83.7 2.0 %collective-permute-start.3 = (f32[136,128]{1,0:T(8,128)S(1)}, f32[136,128]{1,0:T(8,128)S(1)}, u32[]{:S(2)}, u32[]{:S(2)}) collective-permute-start(f32[136,128]{1,0:T(8,128)S(1)} %concatenate.7), channel_id=1, source_target_pairs={{0,1},{1,2},{2,3},{3,0},{4,5},{5,6},{6,7},{7,4},{8,9},{9,10},{10,1... | collective-permute-start | bytes 208904 | tf_op jit(solution)/shard_map/ppermute | solution.py:158
  85.7 3.6 %collective-permute-start.4 = (f32[136,128]{1,0:T(8,128)S(1)}, f32[136,128]{1,0:T(8,128)S(1)}, u32[]{:S(2)}, u32[]{:S(2)}) collective-permute-start(f32[136,128]{1,0:T(8,128)S(1)} %concatenate.7), channel_id=1, source_target_pairs={{0,2},{1,3},{2,0},{3,1},{4,6},{5,7},{6,4},{7,5},{8,10},{9,11},{10,... | collective-permute-start | bytes 208904 | tf_op jit(solution)/shard_map/ppermute | solution.py:158
  89.2 1.0 collective-permute-start.5
  90.3 1.0 collective-permute-start
  91.7 2.2 %collective-permute-start.2 = (bf16[512,768]{1,0:T(8,128)(2,1)S(1)}, bf16[512,768]{1,0:T(8,128)(2,1)S(1)}, u32[]{:S(2)}, u32[]{:S(2)}) collective-permute-start(bf16[512,768]{1,0:T(8,128)(2,1)S(1)} %get-tuple-element.10), channel_id=1, source_target_pairs={{0,3},{1,0},{2,1},{3,2},{4,7},{5,4},{6,5},{7,6},{8,11},{9,8},{10,9... | collective-permute-start | bytes 2359304 | tf_op jit(solution)/shard_map/ppermute | solution.py:165
  94.0 0.7 add_add_fusion
  95.9 11.7 %cholesky.16 = f32[128,128]{1,0:T(8,128)S(1)} custom-call(f32[128,128]{1,0:T(8,128)S(1)} %fusion.19), custom_call_target="Cholesky" | custom-call | tf_op jit(solution)/shard_map/jit(cholesky)/cholesky | solution.py:161
  108.3 0.7 fusion.16
  109.0 9.8 %custom-call.7 = f32[1,128,128]{1,2,0:T(8,128)S(1)} custom-call(f32[1,128,128]{2,1,0:T(8,128)S(1)} %fusion.16), custom_call_target="InvertDiagBlocksLowerTriangular" | custom-call | tf_op jit(solution)/shard_map/jit(_solve_triangular)/triangular_solve | solution.py:177
  118.8 8.4 %collective-permute-done = bf16[512,768]{1,0:T(8,128)(2,1)S(1)} collective-permute-done((bf16[512,768]{1,0:T(8,128)(2,1)S(1)}, bf16[512,768]{1,0:T(8,128)(2,1)S(1)}, u32[]{:S(2)}, u32[]{:S(2)}) %collective-permute-start) | collective-permute-done | bytes 786464 | tf_op jit(solution)/shard_map/ppermute | solution.py:165
  128.0 1.1 convolution_multiply_fusion
  129.1 0.9 convolution_bitcast_fusion
  130.0 5.2 %all-to-all-done.1 = bf16[32,16,4096]{2,1,0:T(8,128)(2,1)} async-done(((bf16[32,16,4096]{2,1,0:T(8,128)(2,1)}), bf16[32,16,4096]{2,1,0:T(8,128)(2,1)}, u32[]{:S(2)}, u32[]{:S(2)}) %all-to-all-start.1) | async-done | bytes 4194336 | tf_op jit(solution)/shard_map/all_to_all | solution.py:138
  135.2 3.9 %shard_map.86 = bf16[128,4096]{1,0:T(8,128)(2,1)} custom-call(bf16[128,512]{1,0:T(8,128)(2,1)} %get-tuple-element.8.high_ref, bf16[128,512]{1,0:T(8,128)(2,1)} %get-tuple-element.7.low_ref, bf16[512,4096]{1,0:T(8,128)(2,1)} %bitcast.6.rows_ref), custom_call_target="tpu_custom_call" | custom-call | flops 1073741824 | bytes 5505024 | tf_op jit(solution)/shard_map/pallas_call | solution.py:38
  (34 shorter events, 3.5 us)
Async XLA Ops:
  1.4 1.2 copy-start
  5.0 58.5 %copy-start.3 = (bf16[1,4096,768]{2,1,0:T(8,128)(2,1)S(1)}, bf16[1,4096,768]{2,1,0:T(8,128)(2,1)}, u32[]{:S(2)}) copy-start(bf16[1,4096,768]{2,1,0:T(8,128)(2,1)} %param.9) | copy-start | bytes 18874372
  5.0 61.9 %slice-start = ((s8[6291456]{0:T(1024)(128)(4,1)}), s8[4194304]{0:T(1024)(128)(4,1)S(1)}, s32[]{:S(2)}) async-start(s8[6291456]{0:T(1024)(128)(4,1)} %bitcast.41), calls=%async_computation.2 | async-start | bytes 8388608
  5.0 66.2 %slice-start.2 = ((s8[6291456]{0:T(1024)(128)(4,1)}), s8[4194304]{0:T(1024)(128)(4,1)S(1)}, s32[]{:S(2)}) async-start(s8[6291456]{0:T(1024)(128)(4,1)} %bitcast.43), calls=%async_computation.4 | async-start | bytes 8388608
  63.4 3.5 %slice-start.1 = ((s8[6291456]{0:T(1024)(128)(4,1)}), s8[2097152]{0:T(1024)(128)(4,1)S(1)}, s32[]{:S(2)}) async-start(s8[6291456]{0:T(1024)(128)(4,1)} %bitcast.41), calls=%async_computation.3 | async-start | bytes 4194304
  63.4 7.8 %slice-start.3 = ((s8[6291456]{0:T(1024)(128)(4,1)}), s8[2097152]{0:T(1024)(128)(4,1)S(1)}, s32[]{:S(2)}) async-start(s8[6291456]{0:T(1024)(128)(4,1)} %bitcast.43), calls=%async_computation.5 | async-start | bytes 4194304
  76.2 5.0 %copy-start.2 = (f32[128,8]{0,1:T(8,128)S(1)}, f32[128,8]{0,1:T(8,128)}, u32[]{:S(2)}) copy-start(f32[128,8]{0,1:T(8,128)} %param.8) | copy-start | bytes 12292
  76.2 58.9 %all-to-all-start.1 = ((bf16[32,16,4096]{2,1,0:T(8,128)(2,1)}), bf16[32,16,4096]{2,1,0:T(8,128)(2,1)}, u32[]{:S(2)}, u32[]{:S(2)}) async-start(bf16[32,16,4096]{2,1,0:T(8,128)(2,1)} %bitcast.37), calls=%async_computation.1 | async-start | bytes 8388608 | tf_op jit(solution)/shard_map/all_to_all | solution.py:138
  83.7 8.1 %collective-permute-start.3 = (f32[136,128]{1,0:T(8,128)S(1)}, f32[136,128]{1,0:T(8,128)S(1)}, u32[]{:S(2)}, u32[]{:S(2)}) collective-permute-start(f32[136,128]{1,0:T(8,128)S(1)} %concatenate.7), channel_id=1, source_target_pairs={{0,1},{1,2},{2,3},{3,0},{4,5},{5,6},{6,7},{7,4},{8,9},{9,10},{10,1... | collective-permute-start | bytes 208904 | tf_op jit(solution)/shard_map/ppermute | solution.py:158
  85.7 8.3 %collective-permute-start.4 = (f32[136,128]{1,0:T(8,128)S(1)}, f32[136,128]{1,0:T(8,128)S(1)}, u32[]{:S(2)}, u32[]{:S(2)}) collective-permute-start(f32[136,128]{1,0:T(8,128)S(1)} %concatenate.7), channel_id=1, source_target_pairs={{0,2},{1,3},{2,0},{3,1},{4,6},{5,7},{6,4},{7,5},{8,10},{9,11},{10,... | collective-permute-start | bytes 208904 | tf_op jit(solution)/shard_map/ppermute | solution.py:158
  89.2 4.7 %collective-permute-start.5 = (f32[136,128]{1,0:T(8,128)S(1)}, f32[136,128]{1,0:T(8,128)S(1)}, u32[]{:S(2)}, u32[]{:S(2)}) collective-permute-start(f32[136,128]{1,0:T(8,128)S(1)} %concatenate.7), channel_id=1, source_target_pairs={{0,3},{1,0},{2,1},{3,2},{4,7},{5,4},{6,5},{7,6},{8,11},{9,8},{10,9... | collective-permute-start | bytes 208904 | tf_op jit(solution)/shard_map/ppermute | solution.py:158
  90.3 37.0 %collective-permute-start = (bf16[512,768]{1,0:T(8,128)(2,1)S(1)}, bf16[512,768]{1,0:T(8,128)(2,1)S(1)}, u32[]{:S(2)}, u32[]{:S(2)}) collective-permute-start(bf16[512,768]{1,0:T(8,128)(2,1)S(1)} %get-tuple-element.10), channel_id=1, source_target_pairs={{0,1},{1,2},{2,3},{3,0},{4,5},{5,6},{6,7},{7,4},{8,9},{9,10},{10,1... | collective-permute-start | bytes 2359304 | tf_op jit(solution)/shard_map/ppermute | solution.py:165
  91.3 36.0 %collective-permute-start.1 = (bf16[512,768]{1,0:T(8,128)(2,1)S(1)}, bf16[512,768]{1,0:T(8,128)(2,1)S(1)}, u32[]{:S(2)}, u32[]{:S(2)}) collective-permute-start(bf16[512,768]{1,0:T(8,128)(2,1)S(1)} %get-tuple-element.10), channel_id=1, source_target_pairs={{0,2},{1,3},{2,0},{3,1},{4,6},{5,7},{6,4},{7,5},{8,10},{9,11},{10,... | collective-permute-start | bytes 2359304 | tf_op jit(solution)/shard_map/ppermute | solution.py:165
  91.7 35.9 %collective-permute-start.2 = (bf16[512,768]{1,0:T(8,128)(2,1)S(1)}, bf16[512,768]{1,0:T(8,128)(2,1)S(1)}, u32[]{:S(2)}, u32[]{:S(2)}) collective-permute-start(bf16[512,768]{1,0:T(8,128)(2,1)S(1)} %get-tuple-element.10), channel_id=1, source_target_pairs={{0,3},{1,0},{2,1},{3,2},{4,7},{5,4},{6,5},{7,6},{8,11},{9,8},{10,9... | collective-permute-start | bytes 2359304 | tf_op jit(solution)/shard_map/ppermute | solution.py:165
  129.1 10.0 %copy-start.1 = (f32[192,768]{1,0:T(8,128)}, f32[192,768]{1,0:T(8,128)S(1)}, u32[]{:S(2)}) copy-start(f32[192,768]{1,0:T(8,128)S(1)} %convolution_multiply_fusion) | copy-start | bytes 1769476

commit v8 on v7

--- a/solution.py
+++ b/solution.py
@@ -53,69 +53,77 @@
     )(weight_high, weight_low, rows)
 
 
-def route_kernel(ids_ref, tokens_ref, out_ref, target_ref):
-    tok_count, choices = ids_ref.shape
-    owners = out_ref.shape[0] // CAP
+def route_kernel(ids_ref, tokens_hbm, out_ref, target_ref, tokens_vmem, copy_sem):
+    fetch = pltpu.make_async_copy(tokens_hbm, tokens_vmem, copy_sem.at[0])
+    fetch.start()
+    choices, tok_count = ids_ref.shape
+    slots = out_ref.shape[0]
+    owners = slots // CAP
     per_owner = EXPERTS // owners
     ids = ids_ref[...]
     in_flight = (ids % per_owner) == 0
     owner_of = ids // per_owner
-    owner_iota = lax.broadcasted_iota(jnp.int32, (tok_count, owners), 1)
+    owner_iota = lax.broadcasted_iota(jnp.int32, (owners, tok_count), 0)
     matches = []
-    picked = jnp.zeros((tok_count, owners), jnp.float32)
+    picked = jnp.zeros((owners, tok_count), jnp.float32)
     for k in range(choices):
-        hit = (owner_of[:, k : k + 1] == owner_iota) & in_flight[:, k : k + 1]
+        hit = (owner_of[k : k + 1, :] == owner_iota) & in_flight[k : k + 1, :]
         matches.append(hit)
         picked = picked + hit.astype(jnp.float32)
     row = lax.broadcasted_iota(jnp.int32, (tok_count, tok_count), 0)
     col = lax.broadcasted_iota(jnp.int32, (tok_count, tok_count), 1)
-    earlier = (col < row).astype(jnp.bfloat16)
-    before = jnp.dot(earlier, picked.astype(jnp.bfloat16), preferred_element_type=jnp.float32)
-    slot_iota = lax.broadcasted_iota(jnp.int32, (tok_count, owners * CAP), 1)
-    selector = jnp.zeros((tok_count, owners * CAP), jnp.float32)
+    later = (row < col).astype(jnp.bfloat16)
+    before = jnp.dot(picked.astype(jnp.bfloat16), later, preferred_element_type=jnp.float32)
+    slot_iota = lax.broadcasted_iota(jnp.int32, (slots, tok_count), 0)
+    chosen = jnp.zeros((slots, tok_count), jnp.float32)
     targets = []
     for k in range(choices):
-        rank = jnp.sum(jnp.where(matches[k], before, 0.0), axis=1, keepdims=True).astype(jnp.int32)
-        keep = in_flight[:, k : k + 1] & (rank < CAP)
-        target = jnp.where(keep, owner_of[:, k : k + 1] * CAP + rank, -1)
+        rank = jnp.sum(jnp.where(matches[k], before, 0.0), axis=0, keepdims=True).astype(jnp.int32)
+        keep = in_flight[k : k + 1, :] & (rank < CAP)
+        target = jnp.where(keep, owner_of[k : k + 1, :] * CAP + rank, -1)
         targets.append(target)
-        selector = selector + (target == slot_iota).astype(jnp.float32)
-    target_ref[...] = jnp.concatenate(targets, axis=1)
-    chosen = selector.T.astype(jnp.bfloat16)
-    width = tokens_ref.shape[1]
+        chosen = chosen + (target == slot_iota).astype(jnp.float32)
+    target_ref[...] = jnp.concatenate(targets, axis=0)
+    chosen = chosen.astype(jnp.bfloat16)
+    fetch.wait()
+    width = tokens_vmem.shape[1]
     block = 1024
     for c in range(width // block):
         part = jnp.dot(
-            chosen, tokens_ref[:, c * block : (c + 1) * block], preferred_element_type=jnp.float32
+            chosen, tokens_vmem[:, c * block : (c + 1) * block], preferred_element_type=jnp.float32
         )
         out_ref[:, c * block : (c + 1) * block] = part.astype(out_ref.dtype)
 
 
-def route_rows(expert_ids, tokens, owners):
-    tok_count, choices = expert_ids.shape
+def route_rows(ids_by_choice, tokens, owners):
+    choices, tok_count = ids_by_choice.shape
     width = tokens.shape[1]
     slots = owners * CAP
     return pl.pallas_call(
         route_kernel,
         out_shape=(
             jax.ShapeDtypeStruct((slots, width), tokens.dtype),
-            jax.ShapeDtypeStruct((tok_count, choices), jnp.int32),
+            jax.ShapeDtypeStruct((choices, tok_count), jnp.int32),
         ),
         in_specs=[
             pl.BlockSpec(memory_space=pltpu.VMEM),
-            pl.BlockSpec(memory_space=pltpu.VMEM),
+            pl.BlockSpec(memory_space=pl.ANY),
         ],
         out_specs=(
             pl.BlockSpec(memory_space=pltpu.VMEM),
             pl.BlockSpec(memory_space=pltpu.VMEM),
         ),
+        scratch_shapes=[
+            pltpu.VMEM((tok_count, width), tokens.dtype),
+            pltpu.SemaphoreType.DMA((1,)),
+        ],
         compiler_params=pltpu.CompilerParams(vmem_limit_bytes=48 * 1024 * 1024),
         cost_estimate=pl.CostEstimate(
             flops=2 * slots * tok_count * width,
             transcendentals=0,
             bytes_accessed=2 * (slots * width + tok_count * width),
         ),
-    )(expert_ids, tokens)
+    )(ids_by_choice, tokens)
 
 
 def per_device(tokens, expert_ids, route_weight, gate_weight, up_weight, down_weight):
@@ -124,7 +132,8 @@
     tok_count = tokens.shape[0]
     model_width = tokens.shape[1]
     per_owner = EXPERTS // owners
-    outgoing, target = route_rows(expert_ids, tokens, owners)
+    outgoing, target_by_choice = route_rows(expert_ids.T, tokens, owners)
+    target = target_by_choice.T
     outgoing = outgoing.reshape(owners, CAP, model_width)
     gate_matrix = gate_weight[0]
     upper_matrix = up_weight[0]

time: 139 us -> 139 us (level)
  no operation moved by 1% of the time
where the time goes in v8:
time: 139 us
  blocking collectives  58.4 us (42%)
  other arithmetic  25.3 us (18%)
  starting transfers between devices  15.3 us (11%)
  matrix products  15.1 us (11%)
  waiting for transfers between devices  13.9 us (10%)
  Pallas kernels  5.82 us (4%)
  local copies, waits for them, and re-layouts  3.4 us (2%)
  between operations  1.47 us (1%)
    all_to_all x1, blocking collectives, per_device(): lax.all_to_all(outgoing, 'expert', split_axis=0, concat_axis=0, tiled=True)  58.4 us
    another operation x3, other arithmetic, per_device(): jnp.linalg.cholesky(corner + damping * jnp.eye(PANEL, dtype=jnp.float32))  12.4 us
    another operation x2, other arithmetic, per_device(): jax.scipy.linalg.solve_triangular(lower_factor, leading.T, lower=True)  10.5 us
    ppermute x3, waiting for transfers between devices, per_device(): gathered.append(lax.ppermute(hidden, 'pair', ring))  8.82 us
    ppermute x3, starting transfers between devices, per_device(): pack_sum = pack_sum + lax.ppermute(pack, 'pair', ring)  6.57 us
    all_to_all x1, waiting for transfers between devices, per_device(): lax.all_to_all(results, 'expert', split_axis=0, concat_axis=0, tiled=True)  5.08 us
    dot_general x1, matrix products, swiglu_rows(): jnp.dot(hidden, down_matrix, preferred_element_type=jnp.float32)  5.06 us
    all_to_all x1, starting transfers between devices, per_device(): lax.all_to_all(results, 'expert', split_axis=0, concat_axis=0, tiled=True)  4.99 us
  transfers between devices with their start and end apart: 7, of which 3 were waited for; matrix products, arithmetic and copies ran while one was open for 21% of the time, Pallas kernels for 0%

profile of v8, /device:TPU:0, one launch (start us, length us, event | category | flops | bytes accessed | tf_op | source)
XLA Modules:
  0.0 138.7 jit_solution(7650667818466344694)
XLA Ops:
  0.6 1.2 copy-done
  1.9 0.7 copy-done.1
  2.5 2.0 %shard_map.85 = (bf16[512,4096]{1,0:T(8,128)(2,1)S(1)}, s32[8,128]{1,0:T(8,128)S(1)}) custom-call(s32[8,128]{1,0:T(8,128)S(1)} %bitcast.40, bf16[128,4096]{1,0:T(8,128)(2,1)S(1)} %copy-done), custom_call_target="tpu_custom_call" | custom-call | flops 536870912 | bytes 5242880 | tf_op jit(solution)/shard_map/pallas_call | solution.py:102
  4.6 58.4 %all_to_all.10 = bf16[32,16,4096]{2,1,0:T(8,128)(2,1)S(1)} all-to-all(bf16[32,16,4096]{2,1,0:T(8,128)(2,1)S(1)} %bitcast.38), channel_id=1, replica_groups=mesh['expert'=32,'pair'=4] {'expert'}, dimensions={0} | all-to-all | bytes 8388608 | tf_op jit(solution)/shard_map/all_to_all | solution.py:141
  63.0 3.4 %fusion.4 = f32[512,768]{1,0:T(8,128)S(1)} fusion(bf16[512,4096]{1,0:T(8,128)(2,1)S(1)} %bitcast.42, bf16[1,4096,768]{2,1,0:T(8,128)(2,1)S(1)} %copy-done.4), kind=kOutput, calls=%fused_computation.4 | convolution fusion | flops 3221225472 | bytes 12058624 | tf_op jit(solution)/shard_map/dot_general | solution.py:15
  66.5 4.3 %multiply_reduce_fusion = (f32[]{:T(128)}, bf16[512,768]{1,0:T(8,128)(2,1)S(1)}) fusion(bf16[512,4096]{1,0:T(8,128)(2,1)S(1)} %bitcast.43, bf16[1,4096,768]{2,1,0:T(8,128)(2,1)S(1)} %bitcast.46, f32[512,768]{1,0:T(8,128)S(1)} %fusion.4), kind=kOutput, calls=%fused_computation.10 | convolution fusion | flops 3224764416 | bytes 12845060 | tf_op jit(solution)/shard_map/dot_general | solution.py:16
  70.8 5.1 %fusion.6 = bf16[512,4096]{1,0:T(8,128)(2,1)} fusion(bf16[512,768]{1,0:T(8,128)(2,1)S(1)} %get-tuple-element.10, bf16[1,768,4096]{2,1,0:T(8,128)(2,1)S(1)} %bitcast.48), kind=kOutput, calls=%fused_computation.6 | convolution fusion | flops 3223322624 | bytes 11272192 | tf_op jit(solution)/shard_map/dot_general | solution.py:18
  75.8 5.0 %all-to-all-start.1 = ((bf16[32,16,4096]{2,1,0:T(8,128)(2,1)}), bf16[32,16,4096]{2,1,0:T(8,128)(2,1)}, u32[]{:S(2)}, u32[]{:S(2)}) async-start(bf16[32,16,4096]{2,1,0:T(8,128)(2,1)} %bitcast.41), calls=%async_computation.1 | async-start | bytes 8388608 | tf_op jit(solution)/shard_map/all_to_all | solution.py:147
  81.1 0.7 select_reduce_fusion
  81.7 0.8 fusion.12
  83.4 2.0 %collective-permute-start.3 = (f32[136,128]{1,0:T(8,128)S(1)}, f32[136,128]{1,0:T(8,128)S(1)}, u32[]{:S(2)}, u32[]{:S(2)}) collective-permute-start(f32[136,128]{1,0:T(8,128)S(1)} %concatenate.7), channel_id=1, source_target_pairs={{0,1},{1,2},{2,3},{3,0},{4,5},{5,6},{6,7},{7,4},{8,9},{9,10},{10,1... | collective-permute-start | bytes 208904 | tf_op jit(solution)/shard_map/ppermute | solution.py:167
  85.4 3.6 %collective-permute-start.4 = (f32[136,128]{1,0:T(8,128)S(1)}, f32[136,128]{1,0:T(8,128)S(1)}, u32[]{:S(2)}, u32[]{:S(2)}) collective-permute-start(f32[136,128]{1,0:T(8,128)S(1)} %concatenate.7), channel_id=1, source_target_pairs={{0,2},{1,3},{2,0},{3,1},{4,6},{5,7},{6,4},{7,5},{8,10},{9,11},{10,... | collective-permute-start | bytes 208904 | tf_op jit(solution)/shard_map/ppermute | solution.py:167
  88.9 1.0 collective-permute-start.5
  90.0 1.0 collective-permute-start
  91.4 2.2 %collective-permute-start.2 = (bf16[512,768]{1,0:T(8,128)(2,1)S(1)}, bf16[512,768]{1,0:T(8,128)(2,1)S(1)}, u32[]{:S(2)}, u32[]{:S(2)}) collective-permute-start(bf16[512,768]{1,0:T(8,128)(2,1)S(1)} %get-tuple-element.10), channel_id=1, source_target_pairs={{0,3},{1,0},{2,1},{3,2},{4,7},{5,4},{6,5},{7,6},{8,11},{9,8},{10,9... | collective-permute-start | bytes 2359304 | tf_op jit(solution)/shard_map/ppermute | solution.py:174
  93.7 0.7 add_add_fusion
  95.7 11.7 %cholesky.16 = f32[128,128]{1,0:T(8,128)S(1)} custom-call(f32[128,128]{1,0:T(8,128)S(1)} %fusion.19), custom_call_target="Cholesky" | custom-call | tf_op jit(solution)/shard_map/jit(cholesky)/cholesky | solution.py:170
  108.0 0.7 fusion.16
  108.7 9.8 %custom-call.7 = f32[1,128,128]{1,2,0:T(8,128)S(1)} custom-call(f32[1,128,128]{2,1,0:T(8,128)S(1)} %fusion.16), custom_call_target="InvertDiagBlocksLowerTriangular" | custom-call | tf_op jit(solution)/shard_map/jit(_solve_triangular)/triangular_solve | solution.py:186
  118.5 8.4 %collective-permute-done = bf16[512,768]{1,0:T(8,128)(2,1)S(1)} collective-permute-done((bf16[512,768]{1,0:T(8,128)(2,1)S(1)}, bf16[512,768]{1,0:T(8,128)(2,1)S(1)}, u32[]{:S(2)}, u32[]{:S(2)}) %collective-permute-start) | collective-permute-done | bytes 786464 | tf_op jit(solution)/shard_map/ppermute | solution.py:174
  127.7 1.1 convolution_multiply_fusion
  128.8 0.9 convolution_bitcast_fusion
  129.7 5.1 %all-to-all-done.1 = bf16[32,16,4096]{2,1,0:T(8,128)(2,1)} async-done(((bf16[32,16,4096]{2,1,0:T(8,128)(2,1)}), bf16[32,16,4096]{2,1,0:T(8,128)(2,1)}, u32[]{:S(2)}, u32[]{:S(2)}) %all-to-all-start.1) | async-done | bytes 4194336 | tf_op jit(solution)/shard_map/all_to_all | solution.py:147
  134.8 3.9 %shard_map.86 = bf16[128,4096]{1,0:T(8,128)(2,1)} custom-call(bf16[128,512]{1,0:T(8,128)(2,1)} %get-tuple-element.8.high_ref, bf16[128,512]{1,0:T(8,128)(2,1)} %get-tuple-element.7.low_ref, bf16[512,4096]{1,0:T(8,128)(2,1)} %bitcast.8.rows_ref), custom_call_target="tpu_custom_call" | custom-call | flops 1073741824 | bytes 5505024 | tf_op jit(solution)/shard_map/pallas_call | solution.py:38
  (36 shorter events, 3.6 us)
Async XLA Ops:
  0.6 1.2 copy-start
  1.9 0.7 copy-start.1
  4.5 58.5 %copy-start.4 = (bf16[1,4096,768]{2,1,0:T(8,128)(2,1)S(1)}, bf16[1,4096,768]{2,1,0:T(8,128)(2,1)}, u32[]{:S(2)}) copy-start(bf16[1,4096,768]{2,1,0:T(8,128)(2,1)} %param.9) | copy-start | bytes 18874372
  4.5 61.9 %slice-start = ((s8[6291456]{0:T(1024)(128)(4,1)}), s8[4194304]{0:T(1024)(128)(4,1)S(1)}, s32[]{:S(2)}) async-start(s8[6291456]{0:T(1024)(128)(4,1)} %bitcast.45), calls=%async_computation.2 | async-start | bytes 8388608
  4.5 66.2 %slice-start.2 = ((s8[6291456]{0:T(1024)(128)(4,1)}), s8[4194304]{0:T(1024)(128)(4,1)S(1)}, s32[]{:S(2)}) async-start(s8[6291456]{0:T(1024)(128)(4,1)} %bitcast.47), calls=%async_computation.4 | async-start | bytes 8388608
  63.0 3.5 %slice-start.1 = ((s8[6291456]{0:T(1024)(128)(4,1)}), s8[2097152]{0:T(1024)(128)(4,1)S(1)}, s32[]{:S(2)}) async-start(s8[6291456]{0:T(1024)(128)(4,1)} %bitcast.45), calls=%async_computation.3 | async-start | bytes 4194304
  63.0 7.8 %slice-start.3 = ((s8[6291456]{0:T(1024)(128)(4,1)}), s8[2097152]{0:T(1024)(128)(4,1)S(1)}, s32[]{:S(2)}) async-start(s8[6291456]{0:T(1024)(128)(4,1)} %bitcast.47), calls=%async_computation.5 | async-start | bytes 4194304
  75.8 5.1 %copy-start.3 = (f32[128,8]{0,1:T(8,128)S(1)}, f32[128,8]{0,1:T(8,128)}, u32[]{:S(2)}) copy-start(f32[128,8]{0,1:T(8,128)} %param.8) | copy-start | bytes 12292
  75.8 59.0 %all-to-all-start.1 = ((bf16[32,16,4096]{2,1,0:T(8,128)(2,1)}), bf16[32,16,4096]{2,1,0:T(8,128)(2,1)}, u32[]{:S(2)}, u32[]{:S(2)}) async-start(bf16[32,16,4096]{2,1,0:T(8,128)(2,1)} %bitcast.41), calls=%async_computation.1 | async-start | bytes 8388608 | tf_op jit(solution)/shard_map/all_to_all | solution.py:147
  83.4 8.0 %collective-permute-start.3 = (f32[136,128]{1,0:T(8,128)S(1)}, f32[136,128]{1,0:T(8,128)S(1)}, u32[]{:S(2)}, u32[]{:S(2)}) collective-permute-start(f32[136,128]{1,0:T(8,128)S(1)} %concatenate.7), channel_id=1, source_target_pairs={{0,1},{1,2},{2,3},{3,0},{4,5},{5,6},{6,7},{7,4},{8,9},{9,10},{10,1... | collective-permute-start | bytes 208904 | tf_op jit(solution)/shard_map/ppermute | solution.py:167
  85.4 8.3 %collective-permute-start.4 = (f32[136,128]{1,0:T(8,128)S(1)}, f32[136,128]{1,0:T(8,128)S(1)}, u32[]{:S(2)}, u32[]{:S(2)}) collective-permute-start(f32[136,128]{1,0:T(8,128)S(1)} %concatenate.7), channel_id=1, source_target_pairs={{0,2},{1,3},{2,0},{3,1},{4,6},{5,7},{6,4},{7,5},{8,10},{9,11},{10,... | collective-permute-start | bytes 208904 | tf_op jit(solution)/shard_map/ppermute | solution.py:167
  88.9 4.7 %collective-permute-start.5 = (f32[136,128]{1,0:T(8,128)S(1)}, f32[136,128]{1,0:T(8,128)S(1)}, u32[]{:S(2)}, u32[]{:S(2)}) collective-permute-start(f32[136,128]{1,0:T(8,128)S(1)} %concatenate.7), channel_id=1, source_target_pairs={{0,3},{1,0},{2,1},{3,2},{4,7},{5,4},{6,5},{7,6},{8,11},{9,8},{10,9... | collective-permute-start | bytes 208904 | tf_op jit(solution)/shard_map/ppermute | solution.py:167
  90.0 37.0 %collective-permute-start = (bf16[512,768]{1,0:T(8,128)(2,1)S(1)}, bf16[512,768]{1,0:T(8,128)(2,1)S(1)}, u32[]{:S(2)}, u32[]{:S(2)}) collective-permute-start(bf16[512,768]{1,0:T(8,128)(2,1)S(1)} %get-tuple-element.10), channel_id=1, source_target_pairs={{0,1},{1,2},{2,3},{3,0},{4,5},{5,6},{6,7},{7,4},{8,9},{9,10},{10,1... | collective-permute-start | bytes 2359304 | tf_op jit(solution)/shard_map/ppermute | solution.py:174
  91.0 36.0 %collective-permute-start.1 = (bf16[512,768]{1,0:T(8,128)(2,1)S(1)}, bf16[512,768]{1,0:T(8,128)(2,1)S(1)}, u32[]{:S(2)}, u32[]{:S(2)}) collective-permute-start(bf16[512,768]{1,0:T(8,128)(2,1)S(1)} %get-tuple-element.10), channel_id=1, source_target_pairs={{0,2},{1,3},{2,0},{3,1},{4,6},{5,7},{6,4},{7,5},{8,10},{9,11},{10,... | collective-permute-start | bytes 2359304 | tf_op jit(solution)/shard_map/ppermute | solution.py:174
  91.4 35.9 %collective-permute-start.2 = (bf16[512,768]{1,0:T(8,128)(2,1)S(1)}, bf16[512,768]{1,0:T(8,128)(2,1)S(1)}, u32[]{:S(2)}, u32[]{:S(2)}) collective-permute-start(bf16[512,768]{1,0:T(8,128)(2,1)S(1)} %get-tuple-element.10), channel_id=1, source_target_pairs={{0,3},{1,0},{2,1},{3,2},{4,7},{5,4},{6,5},{7,6},{8,11},{9,8},{10,9... | collective-permute-start | bytes 2359304 | tf_op jit(solution)/shard_map/ppermute | solution.py:174
  128.8 9.9 %copy-start.2 = (f32[192,768]{1,0:T(8,128)}, f32[192,768]{1,0:T(8,128)S(1)}, u32[]{:S(2)}) copy-start(f32[192,768]{1,0:T(8,128)S(1)} %convolution_multiply_fusion) | copy-start | bytes 1769476

commit v9 on v8

--- a/solution.py
+++ b/solution.py
@@ -53,9 +53,12 @@
     )(weight_high, weight_low, rows)
 
 
-def route_kernel(ids_ref, tokens_hbm, out_ref, target_ref, tokens_vmem, copy_sem):
+def route_kernel(ids_hbm, tokens_hbm, out_ref, target_ref, ids_ref, tokens_vmem, copy_sem):
+    fetch_ids = pltpu.make_async_copy(ids_hbm, ids_ref, copy_sem.at[1])
+    fetch_ids.start()
     fetch = pltpu.make_async_copy(tokens_hbm, tokens_vmem, copy_sem.at[0])
     fetch.start()
+    fetch_ids.wait()
     choices, tok_count = ids_ref.shape
     slots = out_ref.shape[0]
     owners = slots // CAP
@@ -106,7 +109,7 @@
             jax.ShapeDtypeStruct((choices, tok_count), jnp.int32),
         ),
         in_specs=[
-            pl.BlockSpec(memory_space=pltpu.VMEM),
+            pl.BlockSpec(memory_space=pl.ANY),
             pl.BlockSpec(memory_space=pl.ANY),
         ],
         out_specs=(
@@ -114,10 +117,10 @@
             pl.BlockSpec(memory_space=pltpu.VMEM),
         ),
         scratch_shapes=[
+            pltpu.VMEM((choices, tok_count), jnp.int32),
             pltpu.VMEM((tok_count, width), tokens.dtype),
-            pltpu.SemaphoreType.DMA((1,)),
+            pltpu.SemaphoreType.DMA((2,)),
         ],
-        compiler_params=pltpu.CompilerParams(vmem_limit_bytes=48 * 1024 * 1024),
         cost_estimate=pl.CostEstimate(
             flops=2 * slots * tok_count * width,
             transcendentals=0,

time: 139 us -> 140 us (level)
  Pallas kernels: 5.82 us -> 8.4 us
  local copies, waits for them, and re-layouts: 3.4 us -> 1.5 us
    pallas_call x1, Pallas kernels: 1.96 us -> 4.54 us  [route_rows(): pl.pallas_call(route_kernel, out_shape=(jax.ShapeDtypeStruct((slots, widt...]
    unnamed x19 -> x17, local copies, waits for them, and re-layouts: 2.04 us -> 0.14 us
where the time goes in v9:
time: 140 us; the launch traced here: 139 us
  blocking collectives  58.6 us (42%)
  other arithmetic  25.3 us (18%)
  starting transfers between devices  15.3 us (11%)
  matrix products  14.9 us (11%)
  waiting for transfers between devices  13.9 us (10%)
  Pallas kernels  8.4 us (6%)
  local copies, waits for them, and re-layouts  1.5 us (1%)
  between operations  1.47 us (1%)
    all_to_all x1, blocking collectives, per_device(): lax.all_to_all(outgoing, 'expert', split_axis=0, concat_axis=0, tiled=True)  58.6 us
    another operation x3, other arithmetic, per_device(): jnp.linalg.cholesky(corner + damping * jnp.eye(PANEL, dtype=jnp.float32))  12.4 us
    another operation x2, other arithmetic, per_device(): jax.scipy.linalg.solve_triangular(lower_factor, leading.T, lower=True)  10.5 us
    ppermute x3, waiting for transfers between devices, per_device(): gathered.append(lax.ppermute(hidden, 'pair', ring))  8.81 us
    ppermute x3, starting transfers between devices, per_device(): pack_sum = pack_sum + lax.ppermute(pack, 'pair', ring)  6.57 us
    all_to_all x1, waiting for transfers between devices, per_device(): lax.all_to_all(results, 'expert', split_axis=0, concat_axis=0, tiled=True)  5.07 us
    all_to_all x1, starting transfers between devices, per_device(): lax.all_to_all(results, 'expert', split_axis=0, concat_axis=0, tiled=True)  4.98 us
    dot_general x1, matrix products, swiglu_rows(): jnp.dot(hidden, down_matrix, preferred_element_type=jnp.float32)  4.96 us
  transfers between devices with their start and end apart: 7, of which 3 were waited for; matrix products, arithmetic and copies ran while one was open for 21% of the time, Pallas kernels for 0%

profile of v9, /device:TPU:0, one launch (start us, length us, event | category | flops | bytes accessed | tf_op | source)
XLA Modules:
  0.0 139.3 jit_solution(3359687530460836760)
XLA Ops:
  0.6 4.5 %shard_map.85 = (bf16[512,4096]{1,0:T(8,128)(2,1)}, s32[8,128]{1,0:T(8,128)}) custom-call(s32[8,128]{1,0:T(8,128)} %bitcast.48, bf16[128,4096]{1,0:T(8,128)(2,1)} %tokens_hbm.1), custom_call_target="tpu_custom_call" | custom-call | flops 536870912 | bytes 5242880 | tf_op jit(solution)/shard_map/pallas_call | solution.py:105
  5.2 58.6 %all_to_all.10 = bf16[32,16,4096]{2,1,0:T(8,128)(2,1)S(1)} all-to-all(bf16[32,16,4096]{2,1,0:T(8,128)(2,1)} %bitcast.41), channel_id=1, replica_groups=mesh['expert'=32,'pair'=4] {'expert'}, dimensions={0} | all-to-all | bytes 8388608 | tf_op jit(solution)/shard_map/all_to_all | solution.py:144
  63.9 3.4 %fusion.4 = f32[512,768]{1,0:T(8,128)S(1)} fusion(bf16[512,4096]{1,0:T(8,128)(2,1)S(1)} %bitcast.39, bf16[1,4096,768]{2,1,0:T(8,128)(2,1)S(1)} %copy-done.3), kind=kOutput, calls=%fused_computation.4 | convolution fusion | flops 3221225472 | bytes 12058624 | tf_op jit(solution)/shard_map/dot_general | solution.py:15
  67.3 4.3 %multiply_reduce_fusion = (f32[]{:T(128)}, bf16[512,768]{1,0:T(8,128)(2,1)S(1)}) fusion(bf16[512,4096]{1,0:T(8,128)(2,1)S(1)} %bitcast.40, bf16[1,4096,768]{2,1,0:T(8,128)(2,1)S(1)} %bitcast.45, f32[512,768]{1,0:T(8,128)S(1)} %fusion.4), kind=kOutput, calls=%fused_computation.10 | convolution fusion | flops 3224764416 | bytes 12845060 | tf_op jit(solution)/shard_map/dot_general | solution.py:16
  71.6 5.0 %fusion.6 = bf16[512,4096]{1,0:T(8,128)(2,1)} fusion(bf16[512,768]{1,0:T(8,128)(2,1)S(1)} %get-tuple-element.10, bf16[1,768,4096]{2,1,0:T(8,128)(2,1)S(1)} %bitcast.47), kind=kOutput, calls=%fused_computation.6 | convolution fusion | flops 3223322624 | bytes 11272192 | tf_op jit(solution)/shard_map/dot_general | solution.py:18
  76.5 5.0 %all-to-all-start.1 = ((bf16[32,16,4096]{2,1,0:T(8,128)(2,1)}), bf16[32,16,4096]{2,1,0:T(8,128)(2,1)}, u32[]{:S(2)}, u32[]{:S(2)}) async-start(bf16[32,16,4096]{2,1,0:T(8,128)(2,1)} %bitcast.38), calls=%async_computation.1 | async-start | bytes 8388608 | tf_op jit(solution)/shard_map/all_to_all | solution.py:150
  81.7 0.7 select_reduce_fusion
  82.4 0.8 fusion.12
  83.4 0.7 concatenate.7
  84.1 2.0 %collective-permute-start.3 = (f32[136,128]{1,0:T(8,128)S(1)}, f32[136,128]{1,0:T(8,128)S(1)}, u32[]{:S(2)}, u32[]{:S(2)}) collective-permute-start(f32[136,128]{1,0:T(8,128)S(1)} %concatenate.7), channel_id=1, source_target_pairs={{0,1},{1,2},{2,3},{3,0},{4,5},{5,6},{6,7},{7,4},{8,9},{9,10},{10,1... | collective-permute-start | bytes 208904 | tf_op jit(solution)/shard_map/ppermute | solution.py:170
  86.1 3.6 %collective-permute-start.4 = (f32[136,128]{1,0:T(8,128)S(1)}, f32[136,128]{1,0:T(8,128)S(1)}, u32[]{:S(2)}, u32[]{:S(2)}) collective-permute-start(f32[136,128]{1,0:T(8,128)S(1)} %concatenate.7), channel_id=1, source_target_pairs={{0,2},{1,3},{2,0},{3,1},{4,6},{5,7},{6,4},{7,5},{8,10},{9,11},{10,... | collective-permute-start | bytes 208904 | tf_op jit(solution)/shard_map/ppermute | solution.py:170
  89.6 1.0 collective-permute-start.5
  90.6 1.0 collective-permute-start
  92.1 2.2 %collective-permute-start.2 = (bf16[512,768]{1,0:T(8,128)(2,1)S(1)}, bf16[512,768]{1,0:T(8,128)(2,1)S(1)}, u32[]{:S(2)}, u32[]{:S(2)}) collective-permute-start(bf16[512,768]{1,0:T(8,128)(2,1)S(1)} %get-tuple-element.10), channel_id=1, source_target_pairs={{0,3},{1,0},{2,1},{3,2},{4,7},{5,4},{6,5},{7,6},{8,11},{9,8},{10,9... | collective-permute-start | bytes 2359304 | tf_op jit(solution)/shard_map/ppermute | solution.py:177
  94.4 0.7 add_add_fusion
  96.3 11.7 %cholesky.16 = f32[128,128]{1,0:T(8,128)S(1)} custom-call(f32[128,128]{1,0:T(8,128)S(1)} %fusion.19), custom_call_target="Cholesky" | custom-call | tf_op jit(solution)/shard_map/jit(cholesky)/cholesky | solution.py:173
  108.1 0.6 compare_reduce_fusion
  108.7 0.7 fusion.16
  109.4 9.8 %custom-call.7 = f32[1,128,128]{1,2,0:T(8,128)S(1)} custom-call(f32[1,128,128]{2,1,0:T(8,128)S(1)} %fusion.16), custom_call_target="InvertDiagBlocksLowerTriangular" | custom-call | tf_op jit(solution)/shard_map/jit(_solve_triangular)/triangular_solve | solution.py:189
  119.2 8.4 %collective-permute-done = bf16[512,768]{1,0:T(8,128)(2,1)S(1)} collective-permute-done((bf16[512,768]{1,0:T(8,128)(2,1)S(1)}, bf16[512,768]{1,0:T(8,128)(2,1)S(1)}, u32[]{:S(2)}, u32[]{:S(2)}) %collective-permute-start) | collective-permute-done | bytes 786464 | tf_op jit(solution)/shard_map/ppermute | solution.py:177
  128.4 1.1 convolution_multiply_fusion
  129.5 0.9 convolution_bitcast_fusion
  130.4 5.1 %all-to-all-done.1 = bf16[32,16,4096]{2,1,0:T(8,128)(2,1)} async-done(((bf16[32,16,4096]{2,1,0:T(8,128)(2,1)}), bf16[32,16,4096]{2,1,0:T(8,128)(2,1)}, u32[]{:S(2)}, u32[]{:S(2)}) %all-to-all-start.1) | async-done | bytes 4194336 | tf_op jit(solution)/shard_map/all_to_all | solution.py:150
  135.5 3.9 %shard_map.86 = bf16[128,4096]{1,0:T(8,128)(2,1)} custom-call(bf16[128,512]{1,0:T(8,128)(2,1)} %get-tuple-element.8.high_ref, bf16[128,512]{1,0:T(8,128)(2,1)} %get-tuple-element.7.low_ref, bf16[512,4096]{1,0:T(8,128)(2,1)} %bitcast.8.rows_ref), custom_call_target="tpu_custom_call" | custom-call | flops 1073741824 | bytes 5505024 | tf_op jit(solution)/shard_map/pallas_call | solution.py:38
  (34 shorter events, 2.3 us)
Async XLA Ops:
  5.2 58.7 %copy-start.3 = (bf16[1,4096,768]{2,1,0:T(8,128)(2,1)S(1)}, bf16[1,4096,768]{2,1,0:T(8,128)(2,1)}, u32[]{:S(2)}) copy-start(bf16[1,4096,768]{2,1,0:T(8,128)(2,1)} %param.9) | copy-start | bytes 18874372
  5.2 62.1 %slice-start = ((s8[6291456]{0:T(1024)(128)(4,1)}), s8[4194304]{0:T(1024)(128)(4,1)S(1)}, s32[]{:S(2)}) async-start(s8[6291456]{0:T(1024)(128)(4,1)} %bitcast.44), calls=%async_computation.2 | async-start | bytes 8388608
  5.2 66.3 %slice-start.2 = ((s8[6291456]{0:T(1024)(128)(4,1)}), s8[4194304]{0:T(1024)(128)(4,1)S(1)}, s32[]{:S(2)}) async-start(s8[6291456]{0:T(1024)(128)(4,1)} %bitcast.46), calls=%async_computation.4 | async-start | bytes 8388608
  63.8 3.4 %slice-start.1 = ((s8[6291456]{0:T(1024)(128)(4,1)}), s8[2097152]{0:T(1024)(128)(4,1)S(1)}, s32[]{:S(2)}) async-start(s8[6291456]{0:T(1024)(128)(4,1)} %bitcast.44), calls=%async_computation.3 | async-start | bytes 4194304
  63.9 7.7 %slice-start.3 = ((s8[6291456]{0:T(1024)(128)(4,1)}), s8[2097152]{0:T(1024)(128)(4,1)S(1)}, s32[]{:S(2)}) async-start(s8[6291456]{0:T(1024)(128)(4,1)} %bitcast.46), calls=%async_computation.5 | async-start | bytes 4194304
  76.5 5.0 %copy-start.2 = (s32[8,128]{1,0:T(8,128)S(1)}, s32[8,128]{1,0:T(8,128)}, u32[]{:S(2)}) copy-start(s32[8,128]{1,0:T(8,128)} %get-tuple-element.5) | copy-start | bytes 12292
  76.5 5.1 %copy-start.1 = (f32[128,8]{0,1:T(8,128)S(1)}, f32[128,8]{0,1:T(8,128)}, u32[]{:S(2)}) copy-start(f32[128,8]{0,1:T(8,128)} %param.8) | copy-start | bytes 12292
  76.5 58.9 %all-to-all-start.1 = ((bf16[32,16,4096]{2,1,0:T(8,128)(2,1)}), bf16[32,16,4096]{2,1,0:T(8,128)(2,1)}, u32[]{:S(2)}, u32[]{:S(2)}) async-start(bf16[32,16,4096]{2,1,0:T(8,128)(2,1)} %bitcast.38), calls=%async_computation.1 | async-start | bytes 8388608 | tf_op jit(solution)/shard_map/all_to_all | solution.py:150
  84.1 8.0 %collective-permute-start.3 = (f32[136,128]{1,0:T(8,128)S(1)}, f32[136,128]{1,0:T(8,128)S(1)}, u32[]{:S(2)}, u32[]{:S(2)}) collective-permute-start(f32[136,128]{1,0:T(8,128)S(1)} %concatenate.7), channel_id=1, source_target_pairs={{0,1},{1,2},{2,3},{3,0},{4,5},{5,6},{6,7},{7,4},{8,9},{9,10},{10,1... | collective-permute-start | bytes 208904 | tf_op jit(solution)/shard_map/ppermute | solution.py:170
  86.1 8.3 %collective-permute-start.4 = (f32[136,128]{1,0:T(8,128)S(1)}, f32[136,128]{1,0:T(8,128)S(1)}, u32[]{:S(2)}, u32[]{:S(2)}) collective-permute-start(f32[136,128]{1,0:T(8,128)S(1)} %concatenate.7), channel_id=1, source_target_pairs={{0,2},{1,3},{2,0},{3,1},{4,6},{5,7},{6,4},{7,5},{8,10},{9,11},{10,... | collective-permute-start | bytes 208904 | tf_op jit(solution)/shard_map/ppermute | solution.py:170
  89.6 4.7 %collective-permute-start.5 = (f32[136,128]{1,0:T(8,128)S(1)}, f32[136,128]{1,0:T(8,128)S(1)}, u32[]{:S(2)}, u32[]{:S(2)}) collective-permute-start(f32[136,128]{1,0:T(8,128)S(1)} %concatenate.7), channel_id=1, source_target_pairs={{0,3},{1,0},{2,1},{3,2},{4,7},{5,4},{6,5},{7,6},{8,11},{9,8},{10,9... | collective-permute-start | bytes 208904 | tf_op jit(solution)/shard_map/ppermute | solution.py:170
  90.6 37.0 %collective-permute-start = (bf16[512,768]{1,0:T(8,128)(2,1)S(1)}, bf16[512,768]{1,0:T(8,128)(2,1)S(1)}, u32[]{:S(2)}, u32[]{:S(2)}) collective-permute-start(bf16[512,768]{1,0:T(8,128)(2,1)S(1)} %get-tuple-element.10), channel_id=1, source_target_pairs={{0,1},{1,2},{2,3},{3,0},{4,5},{5,6},{6,7},{7,4},{8,9},{9,10},{10,1... | collective-permute-start | bytes 2359304 | tf_op jit(solution)/shard_map/ppermute | solution.py:177
  91.7 36.0 %collective-permute-start.1 = (bf16[512,768]{1,0:T(8,128)(2,1)S(1)}, bf16[512,768]{1,0:T(8,128)(2,1)S(1)}, u32[]{:S(2)}, u32[]{:S(2)}) collective-permute-start(bf16[512,768]{1,0:T(8,128)(2,1)S(1)} %get-tuple-element.10), channel_id=1, source_target_pairs={{0,2},{1,3},{2,0},{3,1},{4,6},{5,7},{6,4},{7,5},{8,10},{9,11},{10,... | collective-permute-start | bytes 2359304 | tf_op jit(solution)/shard_map/ppermute | solution.py:177
  92.1 35.9 %collective-permute-start.2 = (bf16[512,768]{1,0:T(8,128)(2,1)S(1)}, bf16[512,768]{1,0:T(8,128)(2,1)S(1)}, u32[]{:S(2)}, u32[]{:S(2)}) collective-permute-start(bf16[512,768]{1,0:T(8,128)(2,1)S(1)} %get-tuple-element.10), channel_id=1, source_target_pairs={{0,3},{1,0},{2,1},{3,2},{4,7},{5,4},{6,5},{7,6},{8,11},{9,8},{10,9... | collective-permute-start | bytes 2359304 | tf_op jit(solution)/shard_map/ppermute | solution.py:177
  129.5 9.9 %copy-start = (f32[192,768]{1,0:T(8,128)}, f32[192,768]{1,0:T(8,128)S(1)}, u32[]{:S(2)}) copy-start(f32[192,768]{1,0:T(8,128)S(1)} %convolution_multiply_fusion) | copy-start | bytes 1769476

commit v10 on v8

--- a/solution.py
+++ b/solution.py
@@ -53,11 +53,9 @@
     )(weight_high, weight_low, rows)
 
 
-def route_kernel(ids_ref, tokens_hbm, out_ref, target_ref, tokens_vmem, copy_sem):
-    fetch = pltpu.make_async_copy(tokens_hbm, tokens_vmem, copy_sem.at[0])
-    fetch.start()
+def route_kernel(ids_ref, chosen_ref, target_ref):
     choices, tok_count = ids_ref.shape
-    slots = out_ref.shape[0]
+    slots = chosen_ref.shape[0]
     owners = slots // CAP
     per_owner = EXPERTS // owners
     ids = ids_ref[...]
@@ -84,46 +82,29 @@
         targets.append(target)
         chosen = chosen + (target == slot_iota).astype(jnp.float32)
     target_ref[...] = jnp.concatenate(targets, axis=0)
-    chosen = chosen.astype(jnp.bfloat16)
-    fetch.wait()
-    width = tokens_vmem.shape[1]
-    block = 1024
-    for c in range(width // block):
-        part = jnp.dot(
-            chosen, tokens_vmem[:, c * block : (c + 1) * block], preferred_element_type=jnp.float32
-        )
-        out_ref[:, c * block : (c + 1) * block] = part.astype(out_ref.dtype)
+    chosen_ref[...] = chosen.astype(chosen_ref.dtype)
 
 
 def route_rows(ids_by_choice, tokens, owners):
     choices, tok_count = ids_by_choice.shape
-    width = tokens.shape[1]
     slots = owners * CAP
-    return pl.pallas_call(
+    chosen, target = pl.pallas_call(
         route_kernel,
         out_shape=(
-            jax.ShapeDtypeStruct((slots, width), tokens.dtype),
+            jax.ShapeDtypeStruct((slots, tok_count), jnp.bfloat16),
             jax.ShapeDtypeStruct((choices, tok_count), jnp.int32),
         ),
-        in_specs=[
-            pl.BlockSpec(memory_space=pltpu.VMEM),
-            pl.BlockSpec(memory_space=pl.ANY),
-        ],
+        in_specs=[pl.BlockSpec(memory_space=pltpu.VMEM)],
         out_specs=(
             pl.BlockSpec(memory_space=pltpu.VMEM),
             pl.BlockSpec(memory_space=pltpu.VMEM),
         ),
-        scratch_shapes=[
-            pltpu.VMEM((tok_count, width), tokens.dtype),
-            pltpu.SemaphoreType.DMA((1,)),
-        ],
-        compiler_params=pltpu.CompilerParams(vmem_limit_bytes=48 * 1024 * 1024),
         cost_estimate=pl.CostEstimate(
-            flops=2 * slots * tok_count * width,
-            transcendentals=0,
-            bytes_accessed=2 * (slots * width + tok_count * width),
+            flops=2 * owners * tok_count * tok_count, transcendentals=0, bytes_accessed=4 * slots * tok_count
         ),
-    )(ids_by_choice, tokens)
+    )(ids_by_choice)
+    outgoing = jnp.dot(chosen, tokens, preferred_element_type=jnp.float32).astype(tokens.dtype)
+    return outgoing, target
 
 
 def per_device(tokens, expert_ids, route_weight, gate_weight, up_weight, down_weight):

time: 139 us -> 139 us (level)
  waiting for transfers between devices: 13.9 us -> 9.98 us
  other arithmetic: 25.3 us -> 28.4 us
  matrix products: 15.1 us -> 17.2 us
    ppermute x3, waiting for transfers between devices: 8.82 us -> 6 us  [per_device(): gathered.append(lax.ppermute(hidden, 'pair', ring))]
    dot_general x0 -> x1, matrix products: none -> 2.29 us  [route_rows(): jnp.dot(chosen, tokens, preferred_element_type=jnp.float32)]
    unnamed x19 -> x21, local copies, waits for them, and re-layouts: 2.04 us -> 0.16 us
  transfers between devices with their start and end apart: 7 -> 7, of which waited for: 3 -> 3; matrix products, arithmetic and copies ran while one was open for 21% -> 24% of each run, Pallas kernels for 0% -> 0%
where the time goes in v10:
time: 139 us
  blocking collectives  58.4 us (42%)
  other arithmetic  28.4 us (20%)
  matrix products  17.2 us (12%)
  starting transfers between devices  15.3 us (11%)
  waiting for transfers between devices  9.98 us (7%)
  Pallas kernels  5.94 us (4%)
  local copies, waits for them, and re-layouts  2.36 us (2%)
  between operations  1.48 us (1%)
    all_to_all x1, blocking collectives, per_device(): lax.all_to_all(outgoing, 'expert', split_axis=0, concat_axis=0, tiled=True)  58.4 us
    another operation x3, other arithmetic, per_device(): jnp.linalg.cholesky(corner + damping * jnp.eye(PANEL, dtype=jnp.float32))  13.2 us
    another operation x2, other arithmetic, per_device(): jax.scipy.linalg.solve_triangular(lower_factor, leading.T, lower=True)  10.5 us
    ppermute x3, starting transfers between devices, per_device(): pack_sum = pack_sum + lax.ppermute(pack, 'pair', ring)  6.57 us
    ppermute x3, waiting for transfers between devices, per_device(): gathered.append(lax.ppermute(hidden, 'pair', ring))  6 us
    all_to_all x1, starting transfers between devices, per_device(): lax.all_to_all(results, 'expert', split_axis=0, concat_axis=0, tiled=True)  5 us
    dot_general x1, matrix products, swiglu_rows(): jnp.dot(hidden, down_matrix, preferred_element_type=jnp.float32)  4.97 us
    dot_general x1, matrix products, swiglu_rows(): jnp.dot(flat_rows, upper_matrix, preferred_element_type=jnp.float32)  4.26 us
  transfers between devices with their start and end apart: 7, of which 3 were waited for; matrix products, arithmetic and copies ran while one was open for 24% of the time, Pallas kernels for 0%

profile of v10, /device:TPU:0, one launch (start us, length us, event | category | flops | bytes accessed | tf_op | source)
XLA Modules:
  0.0 139.0 jit_solution(7269929637448325452)
XLA Ops:
  0.6 2.1 %shard_map.85 = (bf16[512,128]{1,0:T(8,128)(2,1)}, s32[8,128]{1,0:T(8,128)}) custom-call(s32[8,128]{1,0:T(8,128)} %bitcast.46), custom_call_target="tpu_custom_call" | custom-call | flops 1048576 | bytes 262144 | tf_op jit(solution)/shard_map/pallas_call | solution.py:91
  2.7 2.3 %convolution_convert_fusion = bf16[512,4096]{1,0:T(8,128)(2,1)S(1)} fusion(bf16[512,128]{1,0:T(8,128)(2,1)} %get-tuple-element.6, bf16[128,4096]{1,0:T(8,128)(2,1)S(1)} %copy-done), kind=kOutput, calls=%fused_computation.6 | convolution fusion | flops 538968064 | bytes 5373952 | tf_op jit(solution)/shard_map/dot_general | solution.py:106
  5.1 58.4 %all_to_all.10 = bf16[32,16,4096]{2,1,0:T(8,128)(2,1)S(1)} all-to-all(bf16[32,16,4096]{2,1,0:T(8,128)(2,1)S(1)} %bitcast.40), channel_id=1, replica_groups=mesh['expert'=32,'pair'=4] {'expert'}, dimensions={0} | all-to-all | bytes 8388608 | tf_op jit(solution)/shard_map/all_to_all | solution.py:122
  63.5 3.4 %fusion.4 = f32[512,768]{1,0:T(8,128)S(1)} fusion(bf16[512,4096]{1,0:T(8,128)(2,1)S(1)} %bitcast.42, bf16[1,4096,768]{2,1,0:T(8,128)(2,1)S(1)} %bitcast.48), kind=kOutput, calls=%fused_computation.4 | convolution fusion | flops 3221225472 | bytes 12058624 | tf_op jit(solution)/shard_map/dot_general | solution.py:15
  66.9 4.3 %multiply_reduce_fusion = (f32[]{:T(128)}, bf16[512,768]{1,0:T(8,128)(2,1)S(1)}) fusion(bf16[512,4096]{1,0:T(8,128)(2,1)S(1)} %bitcast.43, bf16[1,4096,768]{2,1,0:T(8,128)(2,1)S(1)} %bitcast.50, f32[512,768]{1,0:T(8,128)S(1)} %fusion.4), kind=kOutput, calls=%fused_computation.11 | convolution fusion | flops 3224764416 | bytes 12845060 | tf_op jit(solution)/shard_map/dot_general | solution.py:16
  71.2 5.0 %fusion.6 = bf16[512,4096]{1,0:T(8,128)(2,1)} fusion(bf16[512,768]{1,0:T(8,128)(2,1)S(1)} %get-tuple-element.10, bf16[1,768,4096]{2,1,0:T(8,128)(2,1)S(1)} %bitcast.52), kind=kOutput, calls=%fused_computation.7 | convolution fusion | flops 3223322624 | bytes 11272192 | tf_op jit(solution)/shard_map/dot_general | solution.py:18
  76.2 5.0 %all-to-all-start.1 = ((bf16[32,16,4096]{2,1,0:T(8,128)(2,1)}), bf16[32,16,4096]{2,1,0:T(8,128)(2,1)}, u32[]{:S(2)}, u32[]{:S(2)}) async-start(bf16[32,16,4096]{2,1,0:T(8,128)(2,1)} %bitcast.41), calls=%async_computation.1 | async-start | bytes 8388608 | tf_op jit(solution)/shard_map/all_to_all | solution.py:128
  81.4 0.7 select_reduce_fusion
  82.1 0.7 fusion.12
  83.7 2.0 %collective-permute-start.3 = (f32[136,128]{1,0:T(8,128)S(1)}, f32[136,128]{1,0:T(8,128)S(1)}, u32[]{:S(2)}, u32[]{:S(2)}) collective-permute-start(f32[136,128]{1,0:T(8,128)S(1)} %concatenate.7), channel_id=1, source_target_pairs={{0,1},{1,2},{2,3},{3,0},{4,5},{5,6},{6,7},{7,4},{8,9},{9,10},{10,1... | collective-permute-start | bytes 208904 | tf_op jit(solution)/shard_map/ppermute | solution.py:148
  85.7 3.6 %collective-permute-start.4 = (f32[136,128]{1,0:T(8,128)S(1)}, f32[136,128]{1,0:T(8,128)S(1)}, u32[]{:S(2)}, u32[]{:S(2)}) collective-permute-start(f32[136,128]{1,0:T(8,128)S(1)} %concatenate.7), channel_id=1, source_target_pairs={{0,2},{1,3},{2,0},{3,1},{4,6},{5,7},{6,4},{7,5},{8,10},{9,11},{10,... | collective-permute-start | bytes 208904 | tf_op jit(solution)/shard_map/ppermute | solution.py:148
  89.3 1.0 collective-permute-start.5
  90.3 1.0 collective-permute-start
  91.8 2.2 %collective-permute-start.2 = (bf16[512,768]{1,0:T(8,128)(2,1)S(1)}, bf16[512,768]{1,0:T(8,128)(2,1)}, u32[]{:S(2)}, u32[]{:S(2)}) collective-permute-start(bf16[512,768]{1,0:T(8,128)(2,1)S(1)} %get-tuple-element.10), channel_id=1, source_target_pairs={{0,3},{1,0},{2,1},{3,2},{4,7},{5,4},{6,5},{7,6},{8,11},{9,8},{10,9... | collective-permute-start | bytes 2359304 | tf_op jit(solution)/shard_map/ppermute | solution.py:155
  94.0 0.7 add_add_fusion
  96.5 0.9 copy.14
  98.1 12.5 %cholesky.16 = f32[128,128]{1,0:T(8,128)S(1)} custom-call(f32[128,128]{1,0:T(8,128)} %fusion.19), custom_call_target="Cholesky" | custom-call | tf_op jit(solution)/shard_map/jit(cholesky)/cholesky | solution.py:151
  112.0 9.8 %custom-call.7 = f32[1,128,128]{1,2,0:T(8,128)S(1)} custom-call(f32[1,128,128]{2,1,0:T(8,128)S(1)} %fusion.16), custom_call_target="InvertDiagBlocksLowerTriangular" | custom-call | tf_op jit(solution)/shard_map/jit(_solve_triangular)/triangular_solve | solution.py:167
  121.8 5.5 %collective-permute-done = bf16[512,768]{1,0:T(8,128)(2,1)S(1)} collective-permute-done((bf16[512,768]{1,0:T(8,128)(2,1)S(1)}, bf16[512,768]{1,0:T(8,128)(2,1)S(1)}, u32[]{:S(2)}, u32[]{:S(2)}) %collective-permute-start) | collective-permute-done | bytes 786464 | tf_op jit(solution)/shard_map/ppermute | solution.py:155
  127.8 1.3 pad_maximum_fusion
  129.1 1.1 convolution_multiply_fusion
  130.2 0.9 convolution_bitcast_fusion
  131.2 4.0 %all-to-all-done.1 = bf16[32,16,4096]{2,1,0:T(8,128)(2,1)} async-done(((bf16[32,16,4096]{2,1,0:T(8,128)(2,1)}), bf16[32,16,4096]{2,1,0:T(8,128)(2,1)}, u32[]{:S(2)}, u32[]{:S(2)}) %all-to-all-start.1) | async-done | bytes 4194336 | tf_op jit(solution)/shard_map/all_to_all | solution.py:128
  135.1 3.9 %shard_map.86 = bf16[128,4096]{1,0:T(8,128)(2,1)} custom-call(bf16[128,512]{1,0:T(8,128)(2,1)} %get-tuple-element.8.high_ref, bf16[128,512]{1,0:T(8,128)(2,1)} %get-tuple-element.7.low_ref, bf16[512,4096]{1,0:T(8,128)(2,1)} %bitcast.8.rows_ref), custom_call_target="tpu_custom_call" | custom-call | flops 1073741824 | bytes 5505024 | tf_op jit(solution)/shard_map/pallas_call | solution.py:38
  (40 shorter events, 5.2 us)
Async XLA Ops:
  0.6 2.1 %copy-start = (bf16[128,4096]{1,0:T(8,128)(2,1)S(1)}, bf16[128,4096]{1,0:T(8,128)(2,1)}, u32[]{:S(2)}) copy-start(bf16[128,4096]{1,0:T(8,128)(2,1)} %param.6) | copy-start | bytes 3145732
  2.7 60.8 %slice-start = ((s8[6291456]{0:T(1024)(128)(4,1)}), s8[4194304]{0:T(1024)(128)(4,1)S(1)}, s32[]{:S(2)}) async-start(s8[6291456]{0:T(1024)(128)(4,1)} %bitcast.47), calls=%async_computation.2 | async-start | bytes 8388608
  5.0 58.5 %slice-start.1 = ((s8[6291456]{0:T(1024)(128)(4,1)}), s8[2097152]{0:T(1024)(128)(4,1)S(1)}, s32[]{:S(2)}) async-start(s8[6291456]{0:T(1024)(128)(4,1)} %bitcast.47), calls=%async_computation.3 | async-start | bytes 4194304
  5.0 61.9 %slice-start.2 = ((s8[6291456]{0:T(1024)(128)(4,1)}), s8[4194304]{0:T(1024)(128)(4,1)S(1)}, s32[]{:S(2)}) async-start(s8[6291456]{0:T(1024)(128)(4,1)} %bitcast.49), calls=%async_computation.4 | async-start | bytes 8388608
  5.0 66.2 %slice-start.4 = ((s8[6291456]{0:T(1024)(128)(4,1)}), s8[4194304]{0:T(1024)(128)(4,1)S(1)}, s32[]{:S(2)}) async-start(s8[6291456]{0:T(1024)(128)(4,1)} %bitcast.51), calls=%async_computation.6 | async-start | bytes 8388608
  63.5 3.4 %slice-start.3 = ((s8[6291456]{0:T(1024)(128)(4,1)}), s8[2097152]{0:T(1024)(128)(4,1)S(1)}, s32[]{:S(2)}) async-start(s8[6291456]{0:T(1024)(128)(4,1)} %bitcast.49), calls=%async_computation.5 | async-start | bytes 4194304
  63.5 7.7 %slice-start.5 = ((s8[6291456]{0:T(1024)(128)(4,1)}), s8[2097152]{0:T(1024)(128)(4,1)S(1)}, s32[]{:S(2)}) async-start(s8[6291456]{0:T(1024)(128)(4,1)} %bitcast.51), calls=%async_computation.7 | async-start | bytes 4194304
  76.2 5.0 %copy-start.3 = (s32[8,128]{1,0:T(8,128)S(1)}, s32[8,128]{1,0:T(8,128)}, u32[]{:S(2)}) copy-start(s32[8,128]{1,0:T(8,128)} %get-tuple-element.5) | copy-start | bytes 12292
  76.2 5.1 %copy-start.2 = (f32[128,8]{0,1:T(8,128)S(1)}, f32[128,8]{0,1:T(8,128)}, u32[]{:S(2)}) copy-start(f32[128,8]{0,1:T(8,128)} %param.8) | copy-start | bytes 12292
  76.2 59.0 %all-to-all-start.1 = ((bf16[32,16,4096]{2,1,0:T(8,128)(2,1)}), bf16[32,16,4096]{2,1,0:T(8,128)(2,1)}, u32[]{:S(2)}, u32[]{:S(2)}) async-start(bf16[32,16,4096]{2,1,0:T(8,128)(2,1)} %bitcast.41), calls=%async_computation.1 | async-start | bytes 8388608 | tf_op jit(solution)/shard_map/all_to_all | solution.py:128
  83.7 8.0 %collective-permute-start.3 = (f32[136,128]{1,0:T(8,128)S(1)}, f32[136,128]{1,0:T(8,128)S(1)}, u32[]{:S(2)}, u32[]{:S(2)}) collective-permute-start(f32[136,128]{1,0:T(8,128)S(1)} %concatenate.7), channel_id=1, source_target_pairs={{0,1},{1,2},{2,3},{3,0},{4,5},{5,6},{6,7},{7,4},{8,9},{9,10},{10,1... | collective-permute-start | bytes 208904 | tf_op jit(solution)/shard_map/ppermute | solution.py:148
  85.7 8.3 %collective-permute-start.4 = (f32[136,128]{1,0:T(8,128)S(1)}, f32[136,128]{1,0:T(8,128)S(1)}, u32[]{:S(2)}, u32[]{:S(2)}) collective-permute-start(f32[136,128]{1,0:T(8,128)S(1)} %concatenate.7), channel_id=1, source_target_pairs={{0,2},{1,3},{2,0},{3,1},{4,6},{5,7},{6,4},{7,5},{8,10},{9,11},{10,... | collective-permute-start | bytes 208904 | tf_op jit(solution)/shard_map/ppermute | solution.py:148
  89.3 4.7 %collective-permute-start.5 = (f32[136,128]{1,0:T(8,128)S(1)}, f32[136,128]{1,0:T(8,128)S(1)}, u32[]{:S(2)}, u32[]{:S(2)}) collective-permute-start(f32[136,128]{1,0:T(8,128)S(1)} %concatenate.7), channel_id=1, source_target_pairs={{0,3},{1,0},{2,1},{3,2},{4,7},{5,4},{6,5},{7,6},{8,11},{9,8},{10,9... | collective-permute-start | bytes 208904 | tf_op jit(solution)/shard_map/ppermute | solution.py:148
  90.3 37.0 %collective-permute-start = (bf16[512,768]{1,0:T(8,128)(2,1)S(1)}, bf16[512,768]{1,0:T(8,128)(2,1)S(1)}, u32[]{:S(2)}, u32[]{:S(2)}) collective-permute-start(bf16[512,768]{1,0:T(8,128)(2,1)S(1)} %get-tuple-element.10), channel_id=1, source_target_pairs={{0,1},{1,2},{2,3},{3,0},{4,5},{5,6},{6,7},{7,4},{8,9},{9,10},{10,1... | collective-permute-start | bytes 2359304 | tf_op jit(solution)/shard_map/ppermute | solution.py:155
  91.3 36.0 %collective-permute-start.1 = (bf16[512,768]{1,0:T(8,128)(2,1)S(1)}, bf16[512,768]{1,0:T(8,128)(2,1)S(1)}, u32[]{:S(2)}, u32[]{:S(2)}) collective-permute-start(bf16[512,768]{1,0:T(8,128)(2,1)S(1)} %get-tuple-element.10), channel_id=1, source_target_pairs={{0,2},{1,3},{2,0},{3,1},{4,6},{5,7},{6,4},{7,5},{8,10},{9,11},{10,... | collective-permute-start | bytes 2359304 | tf_op jit(solution)/shard_map/ppermute | solution.py:155
  91.8 36.0 %collective-permute-start.2 = (bf16[512,768]{1,0:T(8,128)(2,1)S(1)}, bf16[512,768]{1,0:T(8,128)(2,1)}, u32[]{:S(2)}, u32[]{:S(2)}) collective-permute-start(bf16[512,768]{1,0:T(8,128)(2,1)S(1)} %get-tuple-element.10), channel_id=1, source_target_pairs={{0,3},{1,0},{2,1},{3,2},{4,7},{5,4},{6,5},{7,6},{8,11},{9,8},{10,9... | collective-permute-start | bytes 2359304 | tf_op jit(solution)/shard_map/ppermute | solution.py:155
  130.2 8.8 %copy-start.1 = (f32[192,768]{1,0:T(8,128)}, f32[192,768]{1,0:T(8,128)S(1)}, u32[]{:S(2)}) copy-start(f32[192,768]{1,0:T(8,128)S(1)} %convolution_multiply_fusion) | copy-start | bytes 1769476

commit v11 on v8

--- a/solution.py
+++ b/solution.py
@@ -74,17 +74,17 @@
     col = lax.broadcasted_iota(jnp.int32, (tok_count, tok_count), 1)
     later = (row < col).astype(jnp.bfloat16)
     before = jnp.dot(picked.astype(jnp.bfloat16), later, preferred_element_type=jnp.float32)
-    slot_iota = lax.broadcasted_iota(jnp.int32, (slots, tok_count), 0)
-    chosen = jnp.zeros((slots, tok_count), jnp.float32)
     targets = []
     for k in range(choices):
         rank = jnp.sum(jnp.where(matches[k], before, 0.0), axis=0, keepdims=True).astype(jnp.int32)
         keep = in_flight[k : k + 1, :] & (rank < CAP)
         target = jnp.where(keep, owner_of[k : k + 1, :] * CAP + rank, -1)
         targets.append(target)
-        chosen = chosen + (target == slot_iota).astype(jnp.float32)
     target_ref[...] = jnp.concatenate(targets, axis=0)
-    chosen = chosen.astype(jnp.bfloat16)
+    owner_rank = jnp.where((picked > 0.0) & (before < CAP), before, -1.0)
+    slot_iota = lax.broadcasted_iota(jnp.int32, (owners, CAP, tok_count), 1).astype(jnp.float32)
+    chosen = (owner_rank[:, None, :] == slot_iota).astype(jnp.float32)
+    chosen = chosen.reshape(slots, tok_count).astype(jnp.bfloat16)
     fetch.wait()
     width = tokens_vmem.shape[1]
     block = 1024

time: 139 us -> 139 us (level)
  no operation moved by 1% of the time
where the time goes in v11:
time: 139 us; the launch traced here: 138 us
  blocking collectives  58.4 us (42%)
  other arithmetic  25.3 us (18%)
  starting transfers between devices  15.3 us (11%)
  matrix products  15 us (11%)
  waiting for transfers between devices  13.9 us (10%)
  Pallas kernels  5.4 us (4%)
  local copies, waits for them, and re-layouts  3.4 us (2%)
  between operations  1.47 us (1%)
    all_to_all x1, blocking collectives, per_device(): lax.all_to_all(outgoing, 'expert', split_axis=0, concat_axis=0, tiled=True)  58.4 us
    another operation x3, other arithmetic, per_device(): jnp.linalg.cholesky(corner + damping * jnp.eye(PANEL, dtype=jnp.float32))  12.4 us
    another operation x2, other arithmetic, per_device(): jax.scipy.linalg.solve_triangular(lower_factor, leading.T, lower=True)  10.5 us
    ppermute x3, waiting for transfers between devices, per_device(): gathered.append(lax.ppermute(hidden, 'pair', ring))  8.81 us
    ppermute x3, starting transfers between devices, per_device(): pack_sum = pack_sum + lax.ppermute(pack, 'pair', ring)  6.58 us
    all_to_all x1, waiting for transfers between devices, per_device(): lax.all_to_all(results, 'expert', split_axis=0, concat_axis=0, tiled=True)  5.07 us
    dot_general x1, matrix products, swiglu_rows(): jnp.dot(hidden, down_matrix, preferred_element_type=jnp.float32)  5.06 us
    all_to_all x1, starting transfers between devices, per_device(): lax.all_to_all(results, 'expert', split_axis=0, concat_axis=0, tiled=True)  4.99 us
  transfers between devices with their start and end apart: 7, of which 3 were waited for; matrix products, arithmetic and copies ran while one was open for 21% of the time, Pallas kernels for 0%

profile of v11, /device:TPU:0, one launch (start us, length us, event | category | flops | bytes accessed | tf_op | source)
XLA Modules:
  0.0 138.2 jit_solution(10424660207963621241)
XLA Ops:
  0.6 1.2 copy-done
  1.9 0.7 copy-done.1
  2.5 1.5 %shard_map.85 = (bf16[512,4096]{1,0:T(8,128)(2,1)S(1)}, s32[8,128]{1,0:T(8,128)S(1)}) custom-call(s32[8,128]{1,0:T(8,128)S(1)} %bitcast.40, bf16[128,4096]{1,0:T(8,128)(2,1)S(1)} %copy-done), custom_call_target="tpu_custom_call" | custom-call | flops 536870912 | bytes 5242880 | tf_op jit(solution)/shard_map/pallas_call | solution.py:102
  4.1 58.4 %all_to_all.10 = bf16[32,16,4096]{2,1,0:T(8,128)(2,1)S(1)} all-to-all(bf16[32,16,4096]{2,1,0:T(8,128)(2,1)S(1)} %bitcast.38), channel_id=1, replica_groups=mesh['expert'=32,'pair'=4] {'expert'}, dimensions={0} | all-to-all | bytes 8388608 | tf_op jit(solution)/shard_map/all_to_all | solution.py:141
  62.5 3.4 %fusion.4 = f32[512,768]{1,0:T(8,128)S(1)} fusion(bf16[512,4096]{1,0:T(8,128)(2,1)S(1)} %bitcast.42, bf16[1,4096,768]{2,1,0:T(8,128)(2,1)S(1)} %copy-done.4), kind=kOutput, calls=%fused_computation.4 | convolution fusion | flops 3221225472 | bytes 12058624 | tf_op jit(solution)/shard_map/dot_general | solution.py:15
  66.0 4.3 %multiply_reduce_fusion = (f32[]{:T(128)}, bf16[512,768]{1,0:T(8,128)(2,1)S(1)}) fusion(bf16[512,4096]{1,0:T(8,128)(2,1)S(1)} %bitcast.43, bf16[1,4096,768]{2,1,0:T(8,128)(2,1)S(1)} %bitcast.46, f32[512,768]{1,0:T(8,128)S(1)} %fusion.4), kind=kOutput, calls=%fused_computation.10 | convolution fusion | flops 3224764416 | bytes 12845060 | tf_op jit(solution)/shard_map/dot_general | solution.py:16
  70.3 5.1 %fusion.6 = bf16[512,4096]{1,0:T(8,128)(2,1)} fusion(bf16[512,768]{1,0:T(8,128)(2,1)S(1)} %get-tuple-element.10, bf16[1,768,4096]{2,1,0:T(8,128)(2,1)S(1)} %bitcast.48), kind=kOutput, calls=%fused_computation.6 | convolution fusion | flops 3223322624 | bytes 11272192 | tf_op jit(solution)/shard_map/dot_general | solution.py:18
  75.4 5.0 %all-to-all-start.1 = ((bf16[32,16,4096]{2,1,0:T(8,128)(2,1)}), bf16[32,16,4096]{2,1,0:T(8,128)(2,1)}, u32[]{:S(2)}, u32[]{:S(2)}) async-start(bf16[32,16,4096]{2,1,0:T(8,128)(2,1)} %bitcast.41), calls=%async_computation.1 | async-start | bytes 8388608 | tf_op jit(solution)/shard_map/all_to_all | solution.py:147
  80.6 0.7 select_reduce_fusion
  81.3 0.8 fusion.12
  82.9 2.0 %collective-permute-start.3 = (f32[136,128]{1,0:T(8,128)S(1)}, f32[136,128]{1,0:T(8,128)S(1)}, u32[]{:S(2)}, u32[]{:S(2)}) collective-permute-start(f32[136,128]{1,0:T(8,128)S(1)} %concatenate.7), channel_id=1, source_target_pairs={{0,1},{1,2},{2,3},{3,0},{4,5},{5,6},{6,7},{7,4},{8,9},{9,10},{10,1... | collective-permute-start | bytes 208904 | tf_op jit(solution)/shard_map/ppermute | solution.py:167
  84.9 3.6 %collective-permute-start.4 = (f32[136,128]{1,0:T(8,128)S(1)}, f32[136,128]{1,0:T(8,128)S(1)}, u32[]{:S(2)}, u32[]{:S(2)}) collective-permute-start(f32[136,128]{1,0:T(8,128)S(1)} %concatenate.7), channel_id=1, source_target_pairs={{0,2},{1,3},{2,0},{3,1},{4,6},{5,7},{6,4},{7,5},{8,10},{9,11},{10,... | collective-permute-start | bytes 208904 | tf_op jit(solution)/shard_map/ppermute | solution.py:167
  88.5 1.0 collective-permute-start.5
  89.5 1.0 collective-permute-start
  91.0 2.2 %collective-permute-start.2 = (bf16[512,768]{1,0:T(8,128)(2,1)S(1)}, bf16[512,768]{1,0:T(8,128)(2,1)S(1)}, u32[]{:S(2)}, u32[]{:S(2)}) collective-permute-start(bf16[512,768]{1,0:T(8,128)(2,1)S(1)} %get-tuple-element.10), channel_id=1, source_target_pairs={{0,3},{1,0},{2,1},{3,2},{4,7},{5,4},{6,5},{7,6},{8,11},{9,8},{10,9... | collective-permute-start | bytes 2359304 | tf_op jit(solution)/shard_map/ppermute | solution.py:174
  93.2 0.7 add_add_fusion
  95.2 11.7 %cholesky.16 = f32[128,128]{1,0:T(8,128)S(1)} custom-call(f32[128,128]{1,0:T(8,128)S(1)} %fusion.19), custom_call_target="Cholesky" | custom-call | tf_op jit(solution)/shard_map/jit(cholesky)/cholesky | solution.py:170
  107.6 0.7 fusion.16
  108.3 9.8 %custom-call.7 = f32[1,128,128]{1,2,0:T(8,128)S(1)} custom-call(f32[1,128,128]{2,1,0:T(8,128)S(1)} %fusion.16), custom_call_target="InvertDiagBlocksLowerTriangular" | custom-call | tf_op jit(solution)/shard_map/jit(_solve_triangular)/triangular_solve | solution.py:186
  118.1 8.4 %collective-permute-done = bf16[512,768]{1,0:T(8,128)(2,1)S(1)} collective-permute-done((bf16[512,768]{1,0:T(8,128)(2,1)S(1)}, bf16[512,768]{1,0:T(8,128)(2,1)S(1)}, u32[]{:S(2)}, u32[]{:S(2)}) %collective-permute-start) | collective-permute-done | bytes 786464 | tf_op jit(solution)/shard_map/ppermute | solution.py:174
  127.2 1.1 convolution_multiply_fusion
  128.3 0.9 convolution_bitcast_fusion
  129.3 5.1 %all-to-all-done.1 = bf16[32,16,4096]{2,1,0:T(8,128)(2,1)} async-done(((bf16[32,16,4096]{2,1,0:T(8,128)(2,1)}), bf16[32,16,4096]{2,1,0:T(8,128)(2,1)}, u32[]{:S(2)}, u32[]{:S(2)}) %all-to-all-start.1) | async-done | bytes 4194336 | tf_op jit(solution)/shard_map/all_to_all | solution.py:147
  134.4 3.9 %shard_map.86 = bf16[128,4096]{1,0:T(8,128)(2,1)} custom-call(bf16[128,512]{1,0:T(8,128)(2,1)} %get-tuple-element.8.high_ref, bf16[128,512]{1,0:T(8,128)(2,1)} %get-tuple-element.7.low_ref, bf16[512,4096]{1,0:T(8,128)(2,1)} %bitcast.8.rows_ref), custom_call_target="tpu_custom_call" | custom-call | flops 1073741824 | bytes 5505024 | tf_op jit(solution)/shard_map/pallas_call | solution.py:38
  (36 shorter events, 3.6 us)
Async XLA Ops:
  0.6 1.2 copy-start
  1.9 0.7 copy-start.1
  4.1 58.4 %copy-start.4 = (bf16[1,4096,768]{2,1,0:T(8,128)(2,1)S(1)}, bf16[1,4096,768]{2,1,0:T(8,128)(2,1)}, u32[]{:S(2)}) copy-start(bf16[1,4096,768]{2,1,0:T(8,128)(2,1)} %param.9) | copy-start | bytes 18874372
  4.1 61.9 %slice-start = ((s8[6291456]{0:T(1024)(128)(4,1)}), s8[4194304]{0:T(1024)(128)(4,1)S(1)}, s32[]{:S(2)}) async-start(s8[6291456]{0:T(1024)(128)(4,1)} %bitcast.45), calls=%async_computation.2 | async-start | bytes 8388608
  4.1 66.2 %slice-start.2 = ((s8[6291456]{0:T(1024)(128)(4,1)}), s8[4194304]{0:T(1024)(128)(4,1)S(1)}, s32[]{:S(2)}) async-start(s8[6291456]{0:T(1024)(128)(4,1)} %bitcast.47), calls=%async_computation.4 | async-start | bytes 8388608
  62.5 3.5 %slice-start.1 = ((s8[6291456]{0:T(1024)(128)(4,1)}), s8[2097152]{0:T(1024)(128)(4,1)S(1)}, s32[]{:S(2)}) async-start(s8[6291456]{0:T(1024)(128)(4,1)} %bitcast.45), calls=%async_computation.3 | async-start | bytes 4194304
  62.5 7.8 %slice-start.3 = ((s8[6291456]{0:T(1024)(128)(4,1)}), s8[2097152]{0:T(1024)(128)(4,1)S(1)}, s32[]{:S(2)}) async-start(s8[6291456]{0:T(1024)(128)(4,1)} %bitcast.47), calls=%async_computation.5 | async-start | bytes 4194304
  75.4 5.1 %copy-start.3 = (f32[128,8]{0,1:T(8,128)S(1)}, f32[128,8]{0,1:T(8,128)}, u32[]{:S(2)}) copy-start(f32[128,8]{0,1:T(8,128)} %param.8) | copy-start | bytes 12292
  75.4 59.0 %all-to-all-start.1 = ((bf16[32,16,4096]{2,1,0:T(8,128)(2,1)}), bf16[32,16,4096]{2,1,0:T(8,128)(2,1)}, u32[]{:S(2)}, u32[]{:S(2)}) async-start(bf16[32,16,4096]{2,1,0:T(8,128)(2,1)} %bitcast.41), calls=%async_computation.1 | async-start | bytes 8388608 | tf_op jit(solution)/shard_map/all_to_all | solution.py:147
  82.9 8.1 %collective-permute-start.3 = (f32[136,128]{1,0:T(8,128)S(1)}, f32[136,128]{1,0:T(8,128)S(1)}, u32[]{:S(2)}, u32[]{:S(2)}) collective-permute-start(f32[136,128]{1,0:T(8,128)S(1)} %concatenate.7), channel_id=1, source_target_pairs={{0,1},{1,2},{2,3},{3,0},{4,5},{5,6},{6,7},{7,4},{8,9},{9,10},{10,1... | collective-permute-start | bytes 208904 | tf_op jit(solution)/shard_map/ppermute | solution.py:167
  84.9 8.3 %collective-permute-start.4 = (f32[136,128]{1,0:T(8,128)S(1)}, f32[136,128]{1,0:T(8,128)S(1)}, u32[]{:S(2)}, u32[]{:S(2)}) collective-permute-start(f32[136,128]{1,0:T(8,128)S(1)} %concatenate.7), channel_id=1, source_target_pairs={{0,2},{1,3},{2,0},{3,1},{4,6},{5,7},{6,4},{7,5},{8,10},{9,11},{10,... | collective-permute-start | bytes 208904 | tf_op jit(solution)/shard_map/ppermute | solution.py:167
  88.5 4.7 %collective-permute-start.5 = (f32[136,128]{1,0:T(8,128)S(1)}, f32[136,128]{1,0:T(8,128)S(1)}, u32[]{:S(2)}, u32[]{:S(2)}) collective-permute-start(f32[136,128]{1,0:T(8,128)S(1)} %concatenate.7), channel_id=1, source_target_pairs={{0,3},{1,0},{2,1},{3,2},{4,7},{5,4},{6,5},{7,6},{8,11},{9,8},{10,9... | collective-permute-start | bytes 208904 | tf_op jit(solution)/shard_map/ppermute | solution.py:167
  89.5 37.0 %collective-permute-start = (bf16[512,768]{1,0:T(8,128)(2,1)S(1)}, bf16[512,768]{1,0:T(8,128)(2,1)S(1)}, u32[]{:S(2)}, u32[]{:S(2)}) collective-permute-start(bf16[512,768]{1,0:T(8,128)(2,1)S(1)} %get-tuple-element.10), channel_id=1, source_target_pairs={{0,1},{1,2},{2,3},{3,0},{4,5},{5,6},{6,7},{7,4},{8,9},{9,10},{10,1... | collective-permute-start | bytes 2359304 | tf_op jit(solution)/shard_map/ppermute | solution.py:174
  90.6 36.0 %collective-permute-start.1 = (bf16[512,768]{1,0:T(8,128)(2,1)S(1)}, bf16[512,768]{1,0:T(8,128)(2,1)S(1)}, u32[]{:S(2)}, u32[]{:S(2)}) collective-permute-start(bf16[512,768]{1,0:T(8,128)(2,1)S(1)} %get-tuple-element.10), channel_id=1, source_target_pairs={{0,2},{1,3},{2,0},{3,1},{4,6},{5,7},{6,4},{7,5},{8,10},{9,11},{10,... | collective-permute-start | bytes 2359304 | tf_op jit(solution)/shard_map/ppermute | solution.py:174
  91.0 35.9 %collective-permute-start.2 = (bf16[512,768]{1,0:T(8,128)(2,1)S(1)}, bf16[512,768]{1,0:T(8,128)(2,1)S(1)}, u32[]{:S(2)}, u32[]{:S(2)}) collective-permute-start(bf16[512,768]{1,0:T(8,128)(2,1)S(1)} %get-tuple-element.10), channel_id=1, source_target_pairs={{0,3},{1,0},{2,1},{3,2},{4,7},{5,4},{6,5},{7,6},{8,11},{9,8},{10,9... | collective-permute-start | bytes 2359304 | tf_op jit(solution)/shard_map/ppermute | solution.py:174
  128.3 9.9 %copy-start.2 = (f32[192,768]{1,0:T(8,128)}, f32[192,768]{1,0:T(8,128)S(1)}, u32[]{:S(2)}) copy-start(f32[192,768]{1,0:T(8,128)S(1)} %convolution_multiply_fusion) | copy-start | bytes 1769476

commit v12 on v11

--- a/solution.py
+++ b/solution.py
@@ -117,7 +117,6 @@
             pltpu.VMEM((tok_count, width), tokens.dtype),
             pltpu.SemaphoreType.DMA((1,)),
         ],
-        compiler_params=pltpu.CompilerParams(vmem_limit_bytes=48 * 1024 * 1024),
         cost_estimate=pl.CostEstimate(
             flops=2 * slots * tok_count * width,
             transcendentals=0,

time: 139 us -> 140 us (level)
  Pallas kernels: 5.4 us -> 8.98 us
  local copies, waits for them, and re-layouts: 3.4 us -> 1.5 us
    pallas_call x1, Pallas kernels: 1.53 us -> 5.12 us  [route_rows(): pl.pallas_call(route_kernel, out_shape=(jax.ShapeDtypeStruct((slots, widt...]
    unnamed x19 -> x17, local copies, waits for them, and re-layouts: 2.04 us -> 0.14 us
where the time goes in v12:
time: 140 us
  blocking collectives  58.6 us (42%)
  other arithmetic  25.3 us (18%)
  starting transfers between devices  15.3 us (11%)
  matrix products  14.9 us (11%)
  waiting for transfers between devices  13.9 us (10%)
  Pallas kernels  8.98 us (6%)
  local copies, waits for them, and re-layouts  1.5 us (1%)
  between operations  1.47 us (1%)
    all_to_all x1, blocking collectives, per_device(): lax.all_to_all(outgoing, 'expert', split_axis=0, concat_axis=0, tiled=True)  58.6 us
    another operation x3, other arithmetic, per_device(): jnp.linalg.cholesky(corner + damping * jnp.eye(PANEL, dtype=jnp.float32))  12.4 us
    another operation x2, other arithmetic, per_device(): jax.scipy.linalg.solve_triangular(lower_factor, leading.T, lower=True)  10.5 us
    ppermute x3, waiting for transfers between devices, per_device(): gathered.append(lax.ppermute(hidden, 'pair', ring))  8.81 us
    ppermute x3, starting transfers between devices, per_device(): pack_sum = pack_sum + lax.ppermute(pack, 'pair', ring)  6.57 us
    pallas_call x1, Pallas kernels, route_rows(): pl.pallas_call(route_kernel, out_shape=(jax.ShapeDtypeStruct((slots, widt...  5.12 us
    all_to_all x1, waiting for transfers between devices, per_device(): lax.all_to_all(results, 'expert', split_axis=0, concat_axis=0, tiled=True)  5.07 us
    all_to_all x1, starting transfers between devices, per_device(): lax.all_to_all(results, 'expert', split_axis=0, concat_axis=0, tiled=True)  4.98 us
  transfers between devices with their start and end apart: 7, of which 3 were waited for; matrix products, arithmetic and copies ran while one was open for 21% of the time, Pallas kernels for 0%

profile of v12, /device:TPU:0, one launch (start us, length us, event | category | flops | bytes accessed | tf_op | source)
XLA Modules:
  0.0 139.9 jit_solution(9577070788336100955)
XLA Ops:
  0.6 5.1 %shard_map.85 = (bf16[512,4096]{1,0:T(8,128)(2,1)}, s32[8,128]{1,0:T(8,128)}) custom-call(s32[8,128]{1,0:T(8,128)} %bitcast.48, bf16[128,4096]{1,0:T(8,128)(2,1)} %tokens_hbm.1), custom_call_target="tpu_custom_call" | custom-call | flops 536870912 | bytes 5242880 | tf_op jit(solution)/shard_map/pallas_call | solution.py:102
  5.8 58.6 %all_to_all.10 = bf16[32,16,4096]{2,1,0:T(8,128)(2,1)S(1)} all-to-all(bf16[32,16,4096]{2,1,0:T(8,128)(2,1)} %bitcast.41), channel_id=1, replica_groups=mesh['expert'=32,'pair'=4] {'expert'}, dimensions={0} | all-to-all | bytes 8388608 | tf_op jit(solution)/shard_map/all_to_all | solution.py:140
  64.4 3.4 %fusion.4 = f32[512,768]{1,0:T(8,128)S(1)} fusion(bf16[512,4096]{1,0:T(8,128)(2,1)S(1)} %bitcast.39, bf16[1,4096,768]{2,1,0:T(8,128)(2,1)S(1)} %copy-done.3), kind=kOutput, calls=%fused_computation.4 | convolution fusion | flops 3221225472 | bytes 12058624 | tf_op jit(solution)/shard_map/dot_general | solution.py:15
  67.9 4.3 %multiply_reduce_fusion = (f32[]{:T(128)}, bf16[512,768]{1,0:T(8,128)(2,1)S(1)}) fusion(bf16[512,4096]{1,0:T(8,128)(2,1)S(1)} %bitcast.40, bf16[1,4096,768]{2,1,0:T(8,128)(2,1)S(1)} %bitcast.45, f32[512,768]{1,0:T(8,128)S(1)} %fusion.4), kind=kOutput, calls=%fused_computation.10 | convolution fusion | flops 3224764416 | bytes 12845060 | tf_op jit(solution)/shard_map/dot_general | solution.py:16
  72.1 5.0 %fusion.6 = bf16[512,4096]{1,0:T(8,128)(2,1)} fusion(bf16[512,768]{1,0:T(8,128)(2,1)S(1)} %get-tuple-element.10, bf16[1,768,4096]{2,1,0:T(8,128)(2,1)S(1)} %bitcast.47), kind=kOutput, calls=%fused_computation.6 | convolution fusion | flops 3223322624 | bytes 11272192 | tf_op jit(solution)/shard_map/dot_general | solution.py:18
  77.1 5.0 %all-to-all-start.1 = ((bf16[32,16,4096]{2,1,0:T(8,128)(2,1)}), bf16[32,16,4096]{2,1,0:T(8,128)(2,1)}, u32[]{:S(2)}, u32[]{:S(2)}) async-start(bf16[32,16,4096]{2,1,0:T(8,128)(2,1)} %bitcast.38), calls=%async_computation.1 | async-start | bytes 8388608 | tf_op jit(solution)/shard_map/all_to_all | solution.py:146
  82.3 0.7 select_reduce_fusion
  83.0 0.8 fusion.12
  84.0 0.7 concatenate.7
  84.7 2.0 %collective-permute-start.3 = (f32[136,128]{1,0:T(8,128)S(1)}, f32[136,128]{1,0:T(8,128)S(1)}, u32[]{:S(2)}, u32[]{:S(2)}) collective-permute-start(f32[136,128]{1,0:T(8,128)S(1)} %concatenate.7), channel_id=1, source_target_pairs={{0,1},{1,2},{2,3},{3,0},{4,5},{5,6},{6,7},{7,4},{8,9},{9,10},{10,1... | collective-permute-start | bytes 208904 | tf_op jit(solution)/shard_map/ppermute | solution.py:166
  86.6 3.6 %collective-permute-start.4 = (f32[136,128]{1,0:T(8,128)S(1)}, f32[136,128]{1,0:T(8,128)S(1)}, u32[]{:S(2)}, u32[]{:S(2)}) collective-permute-start(f32[136,128]{1,0:T(8,128)S(1)} %concatenate.7), channel_id=1, source_target_pairs={{0,2},{1,3},{2,0},{3,1},{4,6},{5,7},{6,4},{7,5},{8,10},{9,11},{10,... | collective-permute-start | bytes 208904 | tf_op jit(solution)/shard_map/ppermute | solution.py:166
  90.2 1.0 collective-permute-start.5
  91.2 1.0 collective-permute-start
  92.7 2.2 %collective-permute-start.2 = (bf16[512,768]{1,0:T(8,128)(2,1)S(1)}, bf16[512,768]{1,0:T(8,128)(2,1)S(1)}, u32[]{:S(2)}, u32[]{:S(2)}) collective-permute-start(bf16[512,768]{1,0:T(8,128)(2,1)S(1)} %get-tuple-element.10), channel_id=1, source_target_pairs={{0,3},{1,0},{2,1},{3,2},{4,7},{5,4},{6,5},{7,6},{8,11},{9,8},{10,9... | collective-permute-start | bytes 2359304 | tf_op jit(solution)/shard_map/ppermute | solution.py:173
  94.9 0.7 add_add_fusion
  96.9 11.7 %cholesky.16 = f32[128,128]{1,0:T(8,128)S(1)} custom-call(f32[128,128]{1,0:T(8,128)S(1)} %fusion.19), custom_call_target="Cholesky" | custom-call | tf_op jit(solution)/shard_map/jit(cholesky)/cholesky | solution.py:169
  108.7 0.6 compare_reduce_fusion
  109.3 0.7 fusion.16
  110.0 9.8 %custom-call.7 = f32[1,128,128]{1,2,0:T(8,128)S(1)} custom-call(f32[1,128,128]{2,1,0:T(8,128)S(1)} %fusion.16), custom_call_target="InvertDiagBlocksLowerTriangular" | custom-call | tf_op jit(solution)/shard_map/jit(_solve_triangular)/triangular_solve | solution.py:185
  119.8 8.4 %collective-permute-done = bf16[512,768]{1,0:T(8,128)(2,1)S(1)} collective-permute-done((bf16[512,768]{1,0:T(8,128)(2,1)S(1)}, bf16[512,768]{1,0:T(8,128)(2,1)S(1)}, u32[]{:S(2)}, u32[]{:S(2)}) %collective-permute-start) | collective-permute-done | bytes 786464 | tf_op jit(solution)/shard_map/ppermute | solution.py:173
  128.9 1.1 convolution_multiply_fusion
  130.0 0.9 convolution_bitcast_fusion
  131.0 5.1 %all-to-all-done.1 = bf16[32,16,4096]{2,1,0:T(8,128)(2,1)} async-done(((bf16[32,16,4096]{2,1,0:T(8,128)(2,1)}), bf16[32,16,4096]{2,1,0:T(8,128)(2,1)}, u32[]{:S(2)}, u32[]{:S(2)}) %all-to-all-start.1) | async-done | bytes 4194336 | tf_op jit(solution)/shard_map/all_to_all | solution.py:146
  136.0 3.9 %shard_map.86 = bf16[128,4096]{1,0:T(8,128)(2,1)} custom-call(bf16[128,512]{1,0:T(8,128)(2,1)} %get-tuple-element.8.high_ref, bf16[128,512]{1,0:T(8,128)(2,1)} %get-tuple-element.7.low_ref, bf16[512,4096]{1,0:T(8,128)(2,1)} %bitcast.8.rows_ref), custom_call_target="tpu_custom_call" | custom-call | flops 1073741824 | bytes 5505024 | tf_op jit(solution)/shard_map/pallas_call | solution.py:38
  (34 shorter events, 2.3 us)
Async XLA Ops:
  5.8 58.7 %copy-start.3 = (bf16[1,4096,768]{2,1,0:T(8,128)(2,1)S(1)}, bf16[1,4096,768]{2,1,0:T(8,128)(2,1)}, u32[]{:S(2)}) copy-start(bf16[1,4096,768]{2,1,0:T(8,128)(2,1)} %param.9) | copy-start | bytes 18874372
  5.8 62.1 %slice-start = ((s8[6291456]{0:T(1024)(128)(4,1)}), s8[4194304]{0:T(1024)(128)(4,1)S(1)}, s32[]{:S(2)}) async-start(s8[6291456]{0:T(1024)(128)(4,1)} %bitcast.44), calls=%async_computation.2 | async-start | bytes 8388608
  5.8 66.3 %slice-start.2 = ((s8[6291456]{0:T(1024)(128)(4,1)}), s8[4194304]{0:T(1024)(128)(4,1)S(1)}, s32[]{:S(2)}) async-start(s8[6291456]{0:T(1024)(128)(4,1)} %bitcast.46), calls=%async_computation.4 | async-start | bytes 8388608
  64.4 3.4 %slice-start.1 = ((s8[6291456]{0:T(1024)(128)(4,1)}), s8[2097152]{0:T(1024)(128)(4,1)S(1)}, s32[]{:S(2)}) async-start(s8[6291456]{0:T(1024)(128)(4,1)} %bitcast.44), calls=%async_computation.3 | async-start | bytes 4194304
  64.4 7.7 %slice-start.3 = ((s8[6291456]{0:T(1024)(128)(4,1)}), s8[2097152]{0:T(1024)(128)(4,1)S(1)}, s32[]{:S(2)}) async-start(s8[6291456]{0:T(1024)(128)(4,1)} %bitcast.46), calls=%async_computation.5 | async-start | bytes 4194304
  77.1 5.0 %copy-start.2 = (s32[8,128]{1,0:T(8,128)S(1)}, s32[8,128]{1,0:T(8,128)}, u32[]{:S(2)}) copy-start(s32[8,128]{1,0:T(8,128)} %get-tuple-element.5) | copy-start | bytes 12292
  77.1 5.1 %copy-start.1 = (f32[128,8]{0,1:T(8,128)S(1)}, f32[128,8]{0,1:T(8,128)}, u32[]{:S(2)}) copy-start(f32[128,8]{0,1:T(8,128)} %param.8) | copy-start | bytes 12292
  77.1 58.9 %all-to-all-start.1 = ((bf16[32,16,4096]{2,1,0:T(8,128)(2,1)}), bf16[32,16,4096]{2,1,0:T(8,128)(2,1)}, u32[]{:S(2)}, u32[]{:S(2)}) async-start(bf16[32,16,4096]{2,1,0:T(8,128)(2,1)} %bitcast.38), calls=%async_computation.1 | async-start | bytes 8388608 | tf_op jit(solution)/shard_map/all_to_all | solution.py:146
  84.7 8.0 %collective-permute-start.3 = (f32[136,128]{1,0:T(8,128)S(1)}, f32[136,128]{1,0:T(8,128)S(1)}, u32[]{:S(2)}, u32[]{:S(2)}) collective-permute-start(f32[136,128]{1,0:T(8,128)S(1)} %concatenate.7), channel_id=1, source_target_pairs={{0,1},{1,2},{2,3},{3,0},{4,5},{5,6},{6,7},{7,4},{8,9},{9,10},{10,1... | collective-permute-start | bytes 208904 | tf_op jit(solution)/shard_map/ppermute | solution.py:166
  86.6 8.3 %collective-permute-start.4 = (f32[136,128]{1,0:T(8,128)S(1)}, f32[136,128]{1,0:T(8,128)S(1)}, u32[]{:S(2)}, u32[]{:S(2)}) collective-permute-start(f32[136,128]{1,0:T(8,128)S(1)} %concatenate.7), channel_id=1, source_target_pairs={{0,2},{1,3},{2,0},{3,1},{4,6},{5,7},{6,4},{7,5},{8,10},{9,11},{10,... | collective-permute-start | bytes 208904 | tf_op jit(solution)/shard_map/ppermute | solution.py:166
  90.2 4.7 %collective-permute-start.5 = (f32[136,128]{1,0:T(8,128)S(1)}, f32[136,128]{1,0:T(8,128)S(1)}, u32[]{:S(2)}, u32[]{:S(2)}) collective-permute-start(f32[136,128]{1,0:T(8,128)S(1)} %concatenate.7), channel_id=1, source_target_pairs={{0,3},{1,0},{2,1},{3,2},{4,7},{5,4},{6,5},{7,6},{8,11},{9,8},{10,9... | collective-permute-start | bytes 208904 | tf_op jit(solution)/shard_map/ppermute | solution.py:166
  91.2 37.0 %collective-permute-start = (bf16[512,768]{1,0:T(8,128)(2,1)S(1)}, bf16[512,768]{1,0:T(8,128)(2,1)S(1)}, u32[]{:S(2)}, u32[]{:S(2)}) collective-permute-start(bf16[512,768]{1,0:T(8,128)(2,1)S(1)} %get-tuple-element.10), channel_id=1, source_target_pairs={{0,1},{1,2},{2,3},{3,0},{4,5},{5,6},{6,7},{7,4},{8,9},{9,10},{10,1... | collective-permute-start | bytes 2359304 | tf_op jit(solution)/shard_map/ppermute | solution.py:173
  92.3 36.0 %collective-permute-start.1 = (bf16[512,768]{1,0:T(8,128)(2,1)S(1)}, bf16[512,768]{1,0:T(8,128)(2,1)S(1)}, u32[]{:S(2)}, u32[]{:S(2)}) collective-permute-start(bf16[512,768]{1,0:T(8,128)(2,1)S(1)} %get-tuple-element.10), channel_id=1, source_target_pairs={{0,2},{1,3},{2,0},{3,1},{4,6},{5,7},{6,4},{7,5},{8,10},{9,11},{10,... | collective-permute-start | bytes 2359304 | tf_op jit(solution)/shard_map/ppermute | solution.py:173
  92.7 35.9 %collective-permute-start.2 = (bf16[512,768]{1,0:T(8,128)(2,1)S(1)}, bf16[512,768]{1,0:T(8,128)(2,1)S(1)}, u32[]{:S(2)}, u32[]{:S(2)}) collective-permute-start(bf16[512,768]{1,0:T(8,128)(2,1)S(1)} %get-tuple-element.10), channel_id=1, source_target_pairs={{0,3},{1,0},{2,1},{3,2},{4,7},{5,4},{6,5},{7,6},{8,11},{9,8},{10,9... | collective-permute-start | bytes 2359304 | tf_op jit(solution)/shard_map/ppermute | solution.py:173
  130.0 9.9 %copy-start = (f32[192,768]{1,0:T(8,128)}, f32[192,768]{1,0:T(8,128)S(1)}, u32[]{:S(2)}) copy-start(f32[192,768]{1,0:T(8,128)S(1)} %convolution_multiply_fusion) | copy-start | bytes 1769476

commit v13 on v11

--- a/solution.py
+++ b/solution.py
@@ -154,12 +154,13 @@
     hess_scale = 2.0 / (CAP * owners * pair_count)
     row_share = FF // pair_count
     pair_place = lax.axis_index("pair")
-    hidden_wide = hidden.astype(jnp.float32)
     corner_part = lax.dot_general(
         hidden[:, :PANEL], hidden[:, :PANEL], (((0,), (0,)), ((), ())),
         preferred_element_type=jnp.float32,
     )
-    square_part = jnp.broadcast_to(jnp.sum(hidden_wide * hidden_wide), (8, PANEL))
+    held = lax.optimization_barrier(hidden).astype(jnp.float32)
+    square_sum = jnp.sum(held * held)
+    square_part = jnp.broadcast_to(square_sum, (8, PANEL))
     pack = jnp.concatenate([corner_part, square_part], axis=0)
     pack_sum = pack
     for shift in range(1, pair_count):

time: 139 us -> 138 us (level)
  transfers between devices with their start and end apart: 7 -> 7, of which waited for: 3 -> 3; matrix products, arithmetic and copies ran while one was open for 21% -> 22% of each run, Pallas kernels for 0% -> 0%
where the time goes in v13:
time: 138 us; the launch traced here: 137 us
  blocking collectives  58.4 us (42%)
  other arithmetic  26.3 us (19%)
  starting transfers between devices  15.3 us (11%)
  matrix products  14.2 us (10%)
  waiting for transfers between devices  12.9 us (9%)
  Pallas kernels  5.4 us (4%)
  local copies, waits for them, and re-layouts  3.4 us (2%)
  between operations  1.5 us (1%)
    all_to_all x1, blocking collectives, per_device(): lax.all_to_all(outgoing, 'expert', split_axis=0, concat_axis=0, tiled=True)  58.4 us
    another operation x3, other arithmetic, per_device(): jnp.linalg.cholesky(corner + damping * jnp.eye(PANEL, dtype=jnp.float32))  12.4 us
    another operation x2, other arithmetic, per_device(): jax.scipy.linalg.solve_triangular(lower_factor, leading.T, lower=True)  10.5 us
    ppermute x3, waiting for transfers between devices, per_device(): gathered.append(lax.ppermute(hidden, 'pair', ring))  8.82 us
    ppermute x3, starting transfers between devices, per_device(): pack_sum = pack_sum + lax.ppermute(pack, 'pair', ring)  6.58 us
    all_to_all x1, starting transfers between devices, per_device(): lax.all_to_all(results, 'expert', split_axis=0, concat_axis=0, tiled=True)  4.98 us
    dot_general x1, matrix products, swiglu_rows(): jnp.dot(hidden, down_matrix, preferred_element_type=jnp.float32)  4.98 us
    all_to_all x1, waiting for transfers between devices, per_device(): lax.all_to_all(results, 'expert', split_axis=0, concat_axis=0, tiled=True)  4.06 us
  transfers between devices with their start and end apart: 7, of which 3 were waited for; matrix products, arithmetic and copies ran while one was open for 22% of the time, Pallas kernels for 0%

profile of v13, /device:TPU:0, one launch (start us, length us, event | category | flops | bytes accessed | tf_op | source)
XLA Modules:
  0.0 137.4 jit_solution(185346152648955121)
XLA Ops:
  0.6 1.2 copy-done
  1.9 0.7 copy-done.1
  2.5 1.5 %shard_map.85 = (bf16[512,4096]{1,0:T(8,128)(2,1)S(1)}, s32[8,128]{1,0:T(8,128)S(1)}) custom-call(s32[8,128]{1,0:T(8,128)S(1)} %bitcast.38, bf16[128,4096]{1,0:T(8,128)(2,1)S(1)} %copy-done), custom_call_target="tpu_custom_call" | custom-call | flops 536870912 | bytes 5242880 | tf_op jit(solution)/shard_map/pallas_call | solution.py:102
  4.1 58.4 %all_to_all.10 = bf16[32,16,4096]{2,1,0:T(8,128)(2,1)S(1)} all-to-all(bf16[32,16,4096]{2,1,0:T(8,128)(2,1)S(1)} %bitcast.36), channel_id=1, replica_groups=mesh['expert'=32,'pair'=4] {'expert'}, dimensions={0} | all-to-all | bytes 8388608 | tf_op jit(solution)/shard_map/all_to_all | solution.py:141
  62.5 3.4 %fusion.4 = f32[512,768]{1,0:T(8,128)S(1)} fusion(bf16[512,4096]{1,0:T(8,128)(2,1)S(1)} %bitcast.40, bf16[1,4096,768]{2,1,0:T(8,128)(2,1)S(1)} %copy-done.4), kind=kOutput, calls=%fused_computation.4 | convolution fusion | flops 3221225472 | bytes 12058624 | tf_op jit(solution)/shard_map/dot_general | solution.py:15
  66.0 3.5 %multiply_convert_fusion = bf16[512,768]{1,0:T(8,128)(2,1)S(1)} fusion(f32[512,768]{1,0:T(8,128)S(1)} %fusion.4, bf16[512,4096]{1,0:T(8,128)(2,1)S(1)} %bitcast.41, bf16[1,4096,768]{2,1,0:T(8,128)(2,1)S(1)} %bitcast.44), kind=kOutput, calls=%fused_computation.11 | convolution fusion | flops 3223584768 | bytes 12845056 | tf_op jit(solution)/shard_map/dot_general | solution.py:16
  69.6 5.0 %fusion.6 = bf16[512,4096]{1,0:T(8,128)(2,1)} fusion(bf16[512,768]{1,0:T(8,128)(2,1)S(1)} %multiply_convert_fusion, bf16[1,768,4096]{2,1,0:T(8,128)(2,1)S(1)} %bitcast.46), kind=kOutput, calls=%fused_computation.6 | convolution fusion | flops 3223322624 | bytes 11272192 | tf_op jit(solution)/shard_map/dot_general | solution.py:18
  74.5 5.0 %all-to-all-start.1 = ((bf16[32,16,4096]{2,1,0:T(8,128)(2,1)}), bf16[32,16,4096]{2,1,0:T(8,128)(2,1)}, u32[]{:S(2)}, u32[]{:S(2)}) async-start(bf16[32,16,4096]{2,1,0:T(8,128)(2,1)} %bitcast.39), calls=%async_computation.1 | async-start | bytes 8388608 | tf_op jit(solution)/shard_map/all_to_all | solution.py:147
  79.7 0.7 select_reduce_fusion
  80.4 0.8 fusion.12
  81.2 1.0 multiply_reduce_fusion
  83.1 2.0 %collective-permute-start.3 = (f32[136,128]{1,0:T(8,128)S(1)}, f32[136,128]{1,0:T(8,128)S(1)}, u32[]{:S(2)}, u32[]{:S(2)}) collective-permute-start(f32[136,128]{1,0:T(8,128)S(1)} %concatenate.7), channel_id=1, source_target_pairs={{0,1},{1,2},{2,3},{3,0},{4,5},{5,6},{6,7},{7,4},{8,9},{9,10},{10,1... | collective-permute-start | bytes 208904 | tf_op jit(solution)/shard_map/ppermute | solution.py:168
  85.1 3.6 %collective-permute-start.4 = (f32[136,128]{1,0:T(8,128)S(1)}, f32[136,128]{1,0:T(8,128)S(1)}, u32[]{:S(2)}, u32[]{:S(2)}) collective-permute-start(f32[136,128]{1,0:T(8,128)S(1)} %concatenate.7), channel_id=1, source_target_pairs={{0,2},{1,3},{2,0},{3,1},{4,6},{5,7},{6,4},{7,5},{8,10},{9,11},{10,... | collective-permute-start | bytes 208904 | tf_op jit(solution)/shard_map/ppermute | solution.py:168
  88.7 1.0 collective-permute-start.5
  89.7 1.0 collective-permute-start
  91.1 2.2 %collective-permute-start.2 = (bf16[512,768]{1,0:T(8,128)(2,1)S(1)}, bf16[512,768]{1,0:T(8,128)(2,1)S(1)}, u32[]{:S(2)}, u32[]{:S(2)}) collective-permute-start(bf16[512,768]{1,0:T(8,128)(2,1)S(1)} %multiply_convert_fusion), channel_id=1, source_target_pairs={{0,3},{1,0},{2,1},{3,2},{4,7},{5,4},{6,5},{7,6},{8,11},{9,8},{10,9... | collective-permute-start | bytes 2359304 | tf_op jit(solution)/shard_map/ppermute | solution.py:175
  93.4 0.7 add_add_fusion
  95.4 11.7 %cholesky.16 = f32[128,128]{1,0:T(8,128)S(1)} custom-call(f32[128,128]{1,0:T(8,128)S(1)} %fusion.19), custom_call_target="Cholesky" | custom-call | tf_op jit(solution)/shard_map/jit(cholesky)/cholesky | solution.py:171
  108.4 9.8 %custom-call.7 = f32[1,128,128]{1,2,0:T(8,128)S(1)} custom-call(f32[1,128,128]{2,1,0:T(8,128)S(1)} %fusion.16), custom_call_target="InvertDiagBlocksLowerTriangular" | custom-call | tf_op jit(solution)/shard_map/jit(_solve_triangular)/triangular_solve | solution.py:187
  118.2 8.4 %collective-permute-done = bf16[512,768]{1,0:T(8,128)(2,1)S(1)} collective-permute-done((bf16[512,768]{1,0:T(8,128)(2,1)S(1)}, bf16[512,768]{1,0:T(8,128)(2,1)S(1)}, u32[]{:S(2)}, u32[]{:S(2)}) %collective-permute-start) | collective-permute-done | bytes 786464 | tf_op jit(solution)/shard_map/ppermute | solution.py:175
  127.4 1.1 convolution_multiply_fusion
  128.5 0.9 convolution_bitcast_fusion
  129.4 4.1 %all-to-all-done.1 = bf16[32,16,4096]{2,1,0:T(8,128)(2,1)} async-done(((bf16[32,16,4096]{2,1,0:T(8,128)(2,1)}), bf16[32,16,4096]{2,1,0:T(8,128)(2,1)}, u32[]{:S(2)}, u32[]{:S(2)}) %all-to-all-start.1) | async-done | bytes 4194336 | tf_op jit(solution)/shard_map/all_to_all | solution.py:147
  133.5 3.9 %shard_map.86 = bf16[128,4096]{1,0:T(8,128)(2,1)} custom-call(bf16[128,512]{1,0:T(8,128)(2,1)} %get-tuple-element.8.high_ref, bf16[128,512]{1,0:T(8,128)(2,1)} %get-tuple-element.7.low_ref, bf16[512,4096]{1,0:T(8,128)(2,1)} %bitcast.8.rows_ref), custom_call_target="tpu_custom_call" | custom-call | flops 1073741824 | bytes 5505024 | tf_op jit(solution)/shard_map/pallas_call | solution.py:38
  (37 shorter events, 4.3 us)
Async XLA Ops:
  0.6 1.2 copy-start
  1.9 0.7 copy-start.1
  4.1 58.4 %copy-start.4 = (bf16[1,4096,768]{2,1,0:T(8,128)(2,1)S(1)}, bf16[1,4096,768]{2,1,0:T(8,128)(2,1)}, u32[]{:S(2)}) copy-start(bf16[1,4096,768]{2,1,0:T(8,128)(2,1)} %param.9) | copy-start | bytes 18874372
  4.1 61.9 %slice-start = ((s8[6291456]{0:T(1024)(128)(4,1)}), s8[4194304]{0:T(1024)(128)(4,1)S(1)}, s32[]{:S(2)}) async-start(s8[6291456]{0:T(1024)(128)(4,1)} %bitcast.43), calls=%async_computation.2 | async-start | bytes 8388608
  4.1 65.4 %slice-start.2 = ((s8[6291456]{0:T(1024)(128)(4,1)}), s8[4194304]{0:T(1024)(128)(4,1)S(1)}, s32[]{:S(2)}) async-start(s8[6291456]{0:T(1024)(128)(4,1)} %bitcast.45), calls=%async_computation.4 | async-start | bytes 8388608
  62.5 3.5 %slice-start.1 = ((s8[6291456]{0:T(1024)(128)(4,1)}), s8[2097152]{0:T(1024)(128)(4,1)S(1)}, s32[]{:S(2)}) async-start(s8[6291456]{0:T(1024)(128)(4,1)} %bitcast.43), calls=%async_computation.3 | async-start | bytes 4194304
  62.5 7.0 %slice-start.3 = ((s8[6291456]{0:T(1024)(128)(4,1)}), s8[2097152]{0:T(1024)(128)(4,1)S(1)}, s32[]{:S(2)}) async-start(s8[6291456]{0:T(1024)(128)(4,1)} %bitcast.45), calls=%async_computation.5 | async-start | bytes 4194304
  74.5 5.1 %copy-start.3 = (f32[128,8]{0,1:T(8,128)S(1)}, f32[128,8]{0,1:T(8,128)}, u32[]{:S(2)}) copy-start(f32[128,8]{0,1:T(8,128)} %param.8) | copy-start | bytes 12292
  74.5 58.9 %all-to-all-start.1 = ((bf16[32,16,4096]{2,1,0:T(8,128)(2,1)}), bf16[32,16,4096]{2,1,0:T(8,128)(2,1)}, u32[]{:S(2)}, u32[]{:S(2)}) async-start(bf16[32,16,4096]{2,1,0:T(8,128)(2,1)} %bitcast.39), calls=%async_computation.1 | async-start | bytes 8388608 | tf_op jit(solution)/shard_map/all_to_all | solution.py:147
  83.1 8.1 %collective-permute-start.3 = (f32[136,128]{1,0:T(8,128)S(1)}, f32[136,128]{1,0:T(8,128)S(1)}, u32[]{:S(2)}, u32[]{:S(2)}) collective-permute-start(f32[136,128]{1,0:T(8,128)S(1)} %concatenate.7), channel_id=1, source_target_pairs={{0,1},{1,2},{2,3},{3,0},{4,5},{5,6},{6,7},{7,4},{8,9},{9,10},{10,1... | collective-permute-start | bytes 208904 | tf_op jit(solution)/shard_map/ppermute | solution.py:168
  85.1 8.3 %collective-permute-start.4 = (f32[136,128]{1,0:T(8,128)S(1)}, f32[136,128]{1,0:T(8,128)S(1)}, u32[]{:S(2)}, u32[]{:S(2)}) collective-permute-start(f32[136,128]{1,0:T(8,128)S(1)} %concatenate.7), channel_id=1, source_target_pairs={{0,2},{1,3},{2,0},{3,1},{4,6},{5,7},{6,4},{7,5},{8,10},{9,11},{10,... | collective-permute-start | bytes 208904 | tf_op jit(solution)/shard_map/ppermute | solution.py:168
  88.7 4.7 %collective-permute-start.5 = (f32[136,128]{1,0:T(8,128)S(1)}, f32[136,128]{1,0:T(8,128)S(1)}, u32[]{:S(2)}, u32[]{:S(2)}) collective-permute-start(f32[136,128]{1,0:T(8,128)S(1)} %concatenate.7), channel_id=1, source_target_pairs={{0,3},{1,0},{2,1},{3,2},{4,7},{5,4},{6,5},{7,6},{8,11},{9,8},{10,9... | collective-permute-start | bytes 208904 | tf_op jit(solution)/shard_map/ppermute | solution.py:168
  89.7 37.0 %collective-permute-start = (bf16[512,768]{1,0:T(8,128)(2,1)S(1)}, bf16[512,768]{1,0:T(8,128)(2,1)S(1)}, u32[]{:S(2)}, u32[]{:S(2)}) collective-permute-start(bf16[512,768]{1,0:T(8,128)(2,1)S(1)} %multiply_convert_fusion), channel_id=1, source_target_pairs={{0,1},{1,2},{2,3},{3,0},{4,5},{5,6},{6,7},{7,4},{8,9},{9,10},{10,1... | collective-permute-start | bytes 2359304 | tf_op jit(solution)/shard_map/ppermute | solution.py:175
  90.7 36.0 %collective-permute-start.1 = (bf16[512,768]{1,0:T(8,128)(2,1)S(1)}, bf16[512,768]{1,0:T(8,128)(2,1)S(1)}, u32[]{:S(2)}, u32[]{:S(2)}) collective-permute-start(bf16[512,768]{1,0:T(8,128)(2,1)S(1)} %multiply_convert_fusion), channel_id=1, source_target_pairs={{0,2},{1,3},{2,0},{3,1},{4,6},{5,7},{6,4},{7,5},{8,10},{9,11},{10,... | collective-permute-start | bytes 2359304 | tf_op jit(solution)/shard_map/ppermute | solution.py:175
  91.1 35.9 %collective-permute-start.2 = (bf16[512,768]{1,0:T(8,128)(2,1)S(1)}, bf16[512,768]{1,0:T(8,128)(2,1)S(1)}, u32[]{:S(2)}, u32[]{:S(2)}) collective-permute-start(bf16[512,768]{1,0:T(8,128)(2,1)S(1)} %multiply_convert_fusion), channel_id=1, source_target_pairs={{0,3},{1,0},{2,1},{3,2},{4,7},{5,4},{6,5},{7,6},{8,11},{9,8},{10,9... | collective-permute-start | bytes 2359304 | tf_op jit(solution)/shard_map/ppermute | solution.py:175
  128.5 8.9 %copy-start.2 = (f32[192,768]{1,0:T(8,128)}, f32[192,768]{1,0:T(8,128)S(1)}, u32[]{:S(2)}) copy-start(f32[192,768]{1,0:T(8,128)S(1)} %convolution_multiply_fusion) | copy-start | bytes 1769476

commit v14 on v10

--- a/solution.py
+++ b/solution.py
@@ -55,7 +55,7 @@
 
 def route_kernel(ids_ref, chosen_ref, target_ref):
     choices, tok_count = ids_ref.shape
-    slots = chosen_ref.shape[0]
+    slots = chosen_ref.shape[1]
     owners = slots // CAP
     per_owner = EXPERTS // owners
     ids = ids_ref[...]
@@ -72,17 +72,17 @@
     col = lax.broadcasted_iota(jnp.int32, (tok_count, tok_count), 1)
     later = (row < col).astype(jnp.bfloat16)
     before = jnp.dot(picked.astype(jnp.bfloat16), later, preferred_element_type=jnp.float32)
-    slot_iota = lax.broadcasted_iota(jnp.int32, (slots, tok_count), 0)
-    chosen = jnp.zeros((slots, tok_count), jnp.float32)
     targets = []
     for k in range(choices):
         rank = jnp.sum(jnp.where(matches[k], before, 0.0), axis=0, keepdims=True).astype(jnp.int32)
         keep = in_flight[k : k + 1, :] & (rank < CAP)
         target = jnp.where(keep, owner_of[k : k + 1, :] * CAP + rank, -1)
         targets.append(target)
-        chosen = chosen + (target == slot_iota).astype(jnp.float32)
     target_ref[...] = jnp.concatenate(targets, axis=0)
-    chosen_ref[...] = chosen.astype(chosen_ref.dtype)
+    owner_rank = jnp.where((picked > 0.0) & (before < CAP), before, -1.0)
+    slot_iota = lax.broadcasted_iota(jnp.int32, (owners, CAP, tok_count), 1).astype(jnp.float32)
+    chosen = (owner_rank[:, None, :] == slot_iota).astype(jnp.float32)
+    chosen_ref[...] = chosen.reshape(slots, tok_count).T.astype(chosen_ref.dtype)
 
 
 def route_rows(ids_by_choice, tokens, owners):
@@ -91,7 +91,7 @@
     chosen, target = pl.pallas_call(
         route_kernel,
         out_shape=(
-            jax.ShapeDtypeStruct((slots, tok_count), jnp.bfloat16),
+            jax.ShapeDtypeStruct((tok_count, slots), jnp.bfloat16),
             jax.ShapeDtypeStruct((choices, tok_count), jnp.int32),
         ),
         in_specs=[pl.BlockSpec(memory_space=pltpu.VMEM)],
@@ -103,7 +103,9 @@
             flops=2 * owners * tok_count * tok_count, transcendentals=0, bytes_accessed=4 * slots * tok_count
         ),
     )(ids_by_choice)
-    outgoing = jnp.dot(chosen, tokens, preferred_element_type=jnp.float32).astype(tokens.dtype)
+    outgoing = lax.dot_general(
+        chosen, tokens, (((0,), (0,)), ((), ())), preferred_element_type=jnp.float32
+    ).astype(tokens.dtype)
     return outgoing, target
 
 
@@ -135,12 +137,13 @@
     hess_scale = 2.0 / (CAP * owners * pair_count)
     row_share = FF // pair_count
     pair_place = lax.axis_index("pair")
-    hidden_wide = hidden.astype(jnp.float32)
     corner_part = lax.dot_general(
         hidden[:, :PANEL], hidden[:, :PANEL], (((0,), (0,)), ((), ())),
         preferred_element_type=jnp.float32,
     )
-    square_part = jnp.broadcast_to(jnp.sum(hidden_wide * hidden_wide), (8, PANEL))
+    held = lax.optimization_barrier(hidden).astype(jnp.float32)
+    square_sum = jnp.sum(held * held)
+    square_part = jnp.broadcast_to(square_sum, (8, PANEL))
     pack = jnp.concatenate([corner_part, square_part], axis=0)
     pack_sum = pack
     for shift in range(1, pair_count):

time: 139 us -> 138 us (level)
  transfers between devices with their start and end apart: 7 -> 7, of which waited for: 3 -> 3; matrix products, arithmetic and copies ran while one was open for 24% -> 25% of each run, Pallas kernels for 0% -> 0%
where the time goes in v14:
time: 138 us
  blocking collectives  58.4 us (42%)
  other arithmetic  29.4 us (21%)
  matrix products  16.6 us (12%)
  starting transfers between devices  15.3 us (11%)
  waiting for transfers between devices  8.97 us (7%)
  Pallas kernels  5.55 us (4%)
  local copies, waits for them, and re-layouts  2.36 us (2%)
  between operations  1.51 us (1%)
    all_to_all x1, blocking collectives, per_device(): lax.all_to_all(outgoing, 'expert', split_axis=0, concat_axis=0, tiled=True)  58.4 us
    another operation x3, other arithmetic, per_device(): jnp.linalg.cholesky(corner + damping * jnp.eye(PANEL, dtype=jnp.float32))  13.2 us
    another operation x2, other arithmetic, per_device(): jax.scipy.linalg.solve_triangular(lower_factor, leading.T, lower=True)  10.5 us
    ppermute x3, starting transfers between devices, per_device(): pack_sum = pack_sum + lax.ppermute(pack, 'pair', ring)  6.57 us
    ppermute x3, waiting for transfers between devices, per_device(): gathered.append(lax.ppermute(hidden, 'pair', ring))  5.99 us
    dot_general x1, matrix products, swiglu_rows(): jnp.dot(hidden, down_matrix, preferred_element_type=jnp.float32)  5.11 us
    all_to_all x1, starting transfers between devices, per_device(): lax.all_to_all(results, 'expert', split_axis=0, concat_axis=0, tiled=True)  4.99 us
    pallas_call x1, Pallas kernels, combine_rows(): pl.pallas_call(combine_kernel, out_shape=jax.ShapeDtypeStruct((tok_count,...  3.86 us
  transfers between devices with their start and end apart: 7, of which 3 were waited for; matrix products, arithmetic and copies ran while one was open for 25% of the time, Pallas kernels for 0%

profile of v14, /device:TPU:0, one launch (start us, length us, event | category | flops | bytes accessed | tf_op | source)
XLA Modules:
  0.0 138.0 jit_solution(10447986826924163045)
XLA Ops:
  0.6 1.7 %shard_map.85 = (bf16[128,512]{1,0:T(8,128)(2,1)}, s32[8,128]{1,0:T(8,128)}) custom-call(s32[8,128]{1,0:T(8,128)} %bitcast.44), custom_call_target="tpu_custom_call" | custom-call | flops 1048576 | bytes 262144 | tf_op jit(solution)/shard_map/pallas_call | solution.py:91
  2.3 2.3 %convolution_convert_fusion = bf16[512,4096]{1,0:T(8,128)(2,1)S(1)} fusion(bf16[128,512]{1,0:T(8,128)(2,1)} %get-tuple-element.6, bf16[128,4096]{1,0:T(8,128)(2,1)S(1)} %copy-done), kind=kOutput, calls=%fused_computation.6 | convolution fusion | flops 538968064 | bytes 5373952 | tf_op jit(solution)/shard_map/dot_general | solution.py:106
  4.7 58.4 %all_to_all.10 = bf16[32,16,4096]{2,1,0:T(8,128)(2,1)S(1)} all-to-all(bf16[32,16,4096]{2,1,0:T(8,128)(2,1)S(1)} %bitcast.38), channel_id=1, replica_groups=mesh['expert'=32,'pair'=4] {'expert'}, dimensions={0} | all-to-all | bytes 8388608 | tf_op jit(solution)/shard_map/all_to_all | solution.py:124
  63.2 3.4 %fusion.4 = f32[512,768]{1,0:T(8,128)S(1)} fusion(bf16[512,4096]{1,0:T(8,128)(2,1)S(1)} %bitcast.40, bf16[1,4096,768]{2,1,0:T(8,128)(2,1)S(1)} %bitcast.46), kind=kOutput, calls=%fused_computation.4 | convolution fusion | flops 3221225472 | bytes 12058624 | tf_op jit(solution)/shard_map/dot_general | solution.py:15
  66.6 3.5 %multiply_convert_fusion = bf16[512,768]{1,0:T(8,128)(2,1)S(1)} fusion(f32[512,768]{1,0:T(8,128)S(1)} %fusion.4, bf16[512,4096]{1,0:T(8,128)(2,1)S(1)} %bitcast.41, bf16[1,4096,768]{2,1,0:T(8,128)(2,1)S(1)} %bitcast.48), kind=kOutput, calls=%fused_computation.12 | convolution fusion | flops 3223584768 | bytes 12845056 | tf_op jit(solution)/shard_map/dot_general | solution.py:16
  70.1 5.1 %fusion.6 = bf16[512,4096]{1,0:T(8,128)(2,1)} fusion(bf16[512,768]{1,0:T(8,128)(2,1)S(1)} %multiply_convert_fusion, bf16[1,768,4096]{2,1,0:T(8,128)(2,1)S(1)} %bitcast.50), kind=kOutput, calls=%fused_computation.7 | convolution fusion | flops 3223322624 | bytes 11272192 | tf_op jit(solution)/shard_map/dot_general | solution.py:18
  75.2 5.0 %all-to-all-start.1 = ((bf16[32,16,4096]{2,1,0:T(8,128)(2,1)}), bf16[32,16,4096]{2,1,0:T(8,128)(2,1)}, u32[]{:S(2)}, u32[]{:S(2)}) async-start(bf16[32,16,4096]{2,1,0:T(8,128)(2,1)} %bitcast.39), calls=%async_computation.1 | async-start | bytes 8388608 | tf_op jit(solution)/shard_map/all_to_all | solution.py:130
  80.5 0.7 select_reduce_fusion
  81.1 0.7 fusion.12
  81.9 1.0 multiply_reduce_fusion
  83.8 2.0 %collective-permute-start.3 = (f32[136,128]{1,0:T(8,128)S(1)}, f32[136,128]{1,0:T(8,128)S(1)}, u32[]{:S(2)}, u32[]{:S(2)}) collective-permute-start(f32[136,128]{1,0:T(8,128)S(1)} %concatenate.7), channel_id=1, source_target_pairs={{0,1},{1,2},{2,3},{3,0},{4,5},{5,6},{6,7},{7,4},{8,9},{9,10},{10,1... | collective-permute-start | bytes 208904 | tf_op jit(solution)/shard_map/ppermute | solution.py:151
  85.8 3.6 %collective-permute-start.4 = (f32[136,128]{1,0:T(8,128)S(1)}, f32[136,128]{1,0:T(8,128)S(1)}, u32[]{:S(2)}, u32[]{:S(2)}) collective-permute-start(f32[136,128]{1,0:T(8,128)S(1)} %concatenate.7), channel_id=1, source_target_pairs={{0,2},{1,3},{2,0},{3,1},{4,6},{5,7},{6,4},{7,5},{8,10},{9,11},{10,... | collective-permute-start | bytes 208904 | tf_op jit(solution)/shard_map/ppermute | solution.py:151
  89.3 1.0 collective-permute-start.5
  90.4 1.0 collective-permute-start
  91.8 2.2 %collective-permute-start.2 = (bf16[512,768]{1,0:T(8,128)(2,1)S(1)}, bf16[512,768]{1,0:T(8,128)(2,1)}, u32[]{:S(2)}, u32[]{:S(2)}) collective-permute-start(bf16[512,768]{1,0:T(8,128)(2,1)S(1)} %multiply_convert_fusion), channel_id=1, source_target_pairs={{0,3},{1,0},{2,1},{3,2},{4,7},{5,4},{6,5},{7,6},{8,11},{9,8},{10,9... | collective-permute-start | bytes 2359304 | tf_op jit(solution)/shard_map/ppermute | solution.py:158
  96.5 0.9 copy.14
  98.1 12.5 %cholesky.16 = f32[128,128]{1,0:T(8,128)S(1)} custom-call(f32[128,128]{1,0:T(8,128)} %fusion.19), custom_call_target="Cholesky" | custom-call | tf_op jit(solution)/shard_map/jit(cholesky)/cholesky | solution.py:154
  112.0 9.8 %custom-call.7 = f32[1,128,128]{1,2,0:T(8,128)S(1)} custom-call(f32[1,128,128]{2,1,0:T(8,128)S(1)} %fusion.16), custom_call_target="InvertDiagBlocksLowerTriangular" | custom-call | tf_op jit(solution)/shard_map/jit(_solve_triangular)/triangular_solve | solution.py:170
  121.8 5.5 %collective-permute-done = bf16[512,768]{1,0:T(8,128)(2,1)S(1)} collective-permute-done((bf16[512,768]{1,0:T(8,128)(2,1)S(1)}, bf16[512,768]{1,0:T(8,128)(2,1)S(1)}, u32[]{:S(2)}, u32[]{:S(2)}) %collective-permute-start) | collective-permute-done | bytes 786464 | tf_op jit(solution)/shard_map/ppermute | solution.py:158
  127.8 1.3 pad_maximum_fusion
  129.2 1.1 convolution_multiply_fusion
  130.3 0.9 convolution_bitcast_fusion
  131.2 3.0 %all-to-all-done.1 = bf16[32,16,4096]{2,1,0:T(8,128)(2,1)} async-done(((bf16[32,16,4096]{2,1,0:T(8,128)(2,1)}), bf16[32,16,4096]{2,1,0:T(8,128)(2,1)}, u32[]{:S(2)}, u32[]{:S(2)}) %all-to-all-start.1) | async-done | bytes 4194336 | tf_op jit(solution)/shard_map/all_to_all | solution.py:130
  134.2 3.9 %shard_map.86 = bf16[128,4096]{1,0:T(8,128)(2,1)} custom-call(bf16[128,512]{1,0:T(8,128)(2,1)} %get-tuple-element.8.high_ref, bf16[128,512]{1,0:T(8,128)(2,1)} %get-tuple-element.7.low_ref, bf16[512,4096]{1,0:T(8,128)(2,1)} %bitcast.8.rows_ref), custom_call_target="tpu_custom_call" | custom-call | flops 1073741824 | bytes 5505024 | tf_op jit(solution)/shard_map/pallas_call | solution.py:38
  (41 shorter events, 5.9 us)
Async XLA Ops:
  0.6 1.7 %copy-start = (bf16[128,4096]{1,0:T(8,128)(2,1)S(1)}, bf16[128,4096]{1,0:T(8,128)(2,1)}, u32[]{:S(2)}) copy-start(bf16[128,4096]{1,0:T(8,128)(2,1)} %param.6) | copy-start | bytes 3145732
  2.3 60.8 %slice-start = ((s8[6291456]{0:T(1024)(128)(4,1)}), s8[4194304]{0:T(1024)(128)(4,1)S(1)}, s32[]{:S(2)}) async-start(s8[6291456]{0:T(1024)(128)(4,1)} %bitcast.45), calls=%async_computation.2 | async-start | bytes 8388608
  4.7 58.5 %slice-start.1 = ((s8[6291456]{0:T(1024)(128)(4,1)}), s8[2097152]{0:T(1024)(128)(4,1)S(1)}, s32[]{:S(2)}) async-start(s8[6291456]{0:T(1024)(128)(4,1)} %bitcast.45), calls=%async_computation.3 | async-start | bytes 4194304
  4.7 61.9 %slice-start.2 = ((s8[6291456]{0:T(1024)(128)(4,1)}), s8[4194304]{0:T(1024)(128)(4,1)S(1)}, s32[]{:S(2)}) async-start(s8[6291456]{0:T(1024)(128)(4,1)} %bitcast.47), calls=%async_computation.4 | async-start | bytes 8388608
  4.7 65.4 %slice-start.4 = ((s8[6291456]{0:T(1024)(128)(4,1)}), s8[4194304]{0:T(1024)(128)(4,1)S(1)}, s32[]{:S(2)}) async-start(s8[6291456]{0:T(1024)(128)(4,1)} %bitcast.49), calls=%async_computation.6 | async-start | bytes 8388608
  63.1 3.4 %slice-start.3 = ((s8[6291456]{0:T(1024)(128)(4,1)}), s8[2097152]{0:T(1024)(128)(4,1)S(1)}, s32[]{:S(2)}) async-start(s8[6291456]{0:T(1024)(128)(4,1)} %bitcast.47), calls=%async_computation.5 | async-start | bytes 4194304
  63.1 7.0 %slice-start.5 = ((s8[6291456]{0:T(1024)(128)(4,1)}), s8[2097152]{0:T(1024)(128)(4,1)S(1)}, s32[]{:S(2)}) async-start(s8[6291456]{0:T(1024)(128)(4,1)} %bitcast.49), calls=%async_computation.7 | async-start | bytes 4194304
  75.2 5.0 %copy-start.3 = (s32[8,128]{1,0:T(8,128)S(1)}, s32[8,128]{1,0:T(8,128)}, u32[]{:S(2)}) copy-start(s32[8,128]{1,0:T(8,128)} %get-tuple-element.5) | copy-start | bytes 12292
  75.2 5.1 %copy-start.2 = (f32[128,8]{0,1:T(8,128)S(1)}, f32[128,8]{0,1:T(8,128)}, u32[]{:S(2)}) copy-start(f32[128,8]{0,1:T(8,128)} %param.8) | copy-start | bytes 12292
  75.2 59.0 %all-to-all-start.1 = ((bf16[32,16,4096]{2,1,0:T(8,128)(2,1)}), bf16[32,16,4096]{2,1,0:T(8,128)(2,1)}, u32[]{:S(2)}, u32[]{:S(2)}) async-start(bf16[32,16,4096]{2,1,0:T(8,128)(2,1)} %bitcast.39), calls=%async_computation.1 | async-start | bytes 8388608 | tf_op jit(solution)/shard_map/all_to_all | solution.py:130
  83.8 8.0 %collective-permute-start.3 = (f32[136,128]{1,0:T(8,128)S(1)}, f32[136,128]{1,0:T(8,128)S(1)}, u32[]{:S(2)}, u32[]{:S(2)}) collective-permute-start(f32[136,128]{1,0:T(8,128)S(1)} %concatenate.7), channel_id=1, source_target_pairs={{0,1},{1,2},{2,3},{3,0},{4,5},{5,6},{6,7},{7,4},{8,9},{9,10},{10,1... | collective-permute-start | bytes 208904 | tf_op jit(solution)/shard_map/ppermute | solution.py:151
  85.8 8.3 %collective-permute-start.4 = (f32[136,128]{1,0:T(8,128)S(1)}, f32[136,128]{1,0:T(8,128)S(1)}, u32[]{:S(2)}, u32[]{:S(2)}) collective-permute-start(f32[136,128]{1,0:T(8,128)S(1)} %concatenate.7), channel_id=1, source_target_pairs={{0,2},{1,3},{2,0},{3,1},{4,6},{5,7},{6,4},{7,5},{8,10},{9,11},{10,... | collective-permute-start | bytes 208904 | tf_op jit(solution)/shard_map/ppermute | solution.py:151
  89.3 4.7 %collective-permute-start.5 = (f32[136,128]{1,0:T(8,128)S(1)}, f32[136,128]{1,0:T(8,128)S(1)}, u32[]{:S(2)}, u32[]{:S(2)}) collective-permute-start(f32[136,128]{1,0:T(8,128)S(1)} %concatenate.7), channel_id=1, source_target_pairs={{0,3},{1,0},{2,1},{3,2},{4,7},{5,4},{6,5},{7,6},{8,11},{9,8},{10,9... | collective-permute-start | bytes 208904 | tf_op jit(solution)/shard_map/ppermute | solution.py:151
  90.4 37.0 %collective-permute-start = (bf16[512,768]{1,0:T(8,128)(2,1)S(1)}, bf16[512,768]{1,0:T(8,128)(2,1)S(1)}, u32[]{:S(2)}, u32[]{:S(2)}) collective-permute-start(bf16[512,768]{1,0:T(8,128)(2,1)S(1)} %multiply_convert_fusion), channel_id=1, source_target_pairs={{0,1},{1,2},{2,3},{3,0},{4,5},{5,6},{6,7},{7,4},{8,9},{9,10},{10,1... | collective-permute-start | bytes 2359304 | tf_op jit(solution)/shard_map/ppermute | solution.py:158
  91.4 36.0 %collective-permute-start.1 = (bf16[512,768]{1,0:T(8,128)(2,1)S(1)}, bf16[512,768]{1,0:T(8,128)(2,1)S(1)}, u32[]{:S(2)}, u32[]{:S(2)}) collective-permute-start(bf16[512,768]{1,0:T(8,128)(2,1)S(1)} %multiply_convert_fusion), channel_id=1, source_target_pairs={{0,2},{1,3},{2,0},{3,1},{4,6},{5,7},{6,4},{7,5},{8,10},{9,11},{10,... | collective-permute-start | bytes 2359304 | tf_op jit(solution)/shard_map/ppermute | solution.py:158
  91.8 36.0 %collective-permute-start.2 = (bf16[512,768]{1,0:T(8,128)(2,1)S(1)}, bf16[512,768]{1,0:T(8,128)(2,1)}, u32[]{:S(2)}, u32[]{:S(2)}) collective-permute-start(bf16[512,768]{1,0:T(8,128)(2,1)S(1)} %multiply_convert_fusion), channel_id=1, source_target_pairs={{0,3},{1,0},{2,1},{3,2},{4,7},{5,4},{6,5},{7,6},{8,11},{9,8},{10,9... | collective-permute-start | bytes 2359304 | tf_op jit(solution)/shard_map/ppermute | solution.py:158
  130.3 7.8 %copy-start.1 = (f32[192,768]{1,0:T(8,128)}, f32[192,768]{1,0:T(8,128)S(1)}, u32[]{:S(2)}) copy-start(f32[192,768]{1,0:T(8,128)S(1)} %convolution_multiply_fusion) | copy-start | bytes 1769476

commit v15 on v6

--- a/solution.py
+++ b/solution.py
@@ -53,27 +53,81 @@
     )(weight_high, weight_low, rows)
 
 
+def route_kernel(ids_ref, tokens_ref, out_ref, target_ref, chosen_ref):
+    @pl.when(pl.program_id(0) == 0)
+    def _():
+        choices, tok_count = ids_ref.shape
+        slots = out_ref.shape[0]
+        owners = slots // CAP
+        per_owner = EXPERTS // owners
+        ids = ids_ref[...]
+        in_flight = (ids % per_owner) == 0
+        owner_of = ids // per_owner
+        owner_iota = lax.broadcasted_iota(jnp.int32, (owners, tok_count), 0)
+        matches = []
+        picked = jnp.zeros((owners, tok_count), jnp.float32)
+        for k in range(choices):
+            hit = (owner_of[k : k + 1, :] == owner_iota) & in_flight[k : k + 1, :]
+            matches.append(hit)
+            picked = picked + hit.astype(jnp.float32)
+        row = lax.broadcasted_iota(jnp.int32, (tok_count, tok_count), 0)
+        col = lax.broadcasted_iota(jnp.int32, (tok_count, tok_count), 1)
+        later = (row < col).astype(jnp.bfloat16)
+        before = jnp.dot(picked.astype(jnp.bfloat16), later, preferred_element_type=jnp.float32)
+        targets = []
+        for k in range(choices):
+            rank = jnp.sum(jnp.where(matches[k], before, 0.0), axis=0, keepdims=True)
+            rank = rank.astype(jnp.int32)
+            keep = in_flight[k : k + 1, :] & (rank < CAP)
+            target = jnp.where(keep, owner_of[k : k + 1, :] * CAP + rank, -1)
+            targets.append(target)
+        target_ref[...] = jnp.concatenate(targets, axis=0)
+        owner_rank = jnp.where((picked > 0.0) & (before < CAP), before, -1.0)
+        slot_iota = lax.broadcasted_iota(jnp.int32, (owners, CAP, tok_count), 1).astype(jnp.float32)
+        chosen = (owner_rank[:, None, :] == slot_iota).astype(jnp.float32)
+        chosen_ref[...] = chosen.reshape(slots, tok_count).astype(chosen_ref.dtype)
+
+    part = jnp.dot(chosen_ref[...], tokens_ref[...], preferred_element_type=jnp.float32)
+    out_ref[...] = part.astype(out_ref.dtype)
+
+
+def route_rows(ids_by_choice, tokens, owners):
+    choices, tok_count = ids_by_choice.shape
+    width = tokens.shape[1]
+    slots = owners * CAP
+    block = width // 2
+    return pl.pallas_call(
+        route_kernel,
+        out_shape=(
+            jax.ShapeDtypeStruct((slots, width), tokens.dtype),
+            jax.ShapeDtypeStruct((choices, tok_count), jnp.int32),
+        ),
+        grid=(width // block,),
+        in_specs=[
+            pl.BlockSpec((choices, tok_count), lambda j: (0, 0)),
+            pl.BlockSpec((tok_count, block), lambda j: (0, j)),
+        ],
+        out_specs=(
+            pl.BlockSpec((slots, block), lambda j: (0, j)),
+            pl.BlockSpec((choices, tok_count), lambda j: (0, 0)),
+        ),
+        scratch_shapes=[pltpu.VMEM((slots, tok_count), jnp.bfloat16)],
+        cost_estimate=pl.CostEstimate(
+            flops=2 * slots * tok_count * width,
+            transcendentals=0,
+            bytes_accessed=2 * (slots * width + tok_count * width),
+        ),
+    )(ids_by_choice, tokens)
+
+
 def per_device(tokens, expert_ids, route_weight, gate_weight, up_weight, down_weight):
     owners = lax.axis_size("expert")
     pair_count = lax.axis_size("pair")
     tok_count = tokens.shape[0]
     model_width = tokens.shape[1]
     per_owner = EXPERTS // owners
-    in_flight = expert_ids % per_owner == 0
-    owner_of = expert_ids // per_owner
-    columns = lax.broadcasted_iota(jnp.int32, (1, 1, owners), 2)
-    route_hit = (in_flight[:, :, None] & (owner_of[:, :, None] == columns)).astype(jnp.int32)
-    picked = jnp.sum(route_hit, axis=1)
-    before = jnp.cumsum(picked, axis=0) - picked
-    rank_choice = jnp.sum(route_hit * before[:, None, :], axis=2)
-    keep_choice = in_flight & (rank_choice < CAP)
-    target = jnp.where(keep_choice, owner_of * CAP + rank_choice, -1)
-    slot_iota = lax.broadcasted_iota(jnp.int32, (1, 1, owners * CAP), 2)
-    hits = target[:, :, None] == slot_iota
-    selector = jnp.any(hits, axis=1).astype(jnp.bfloat16)
-    outgoing = lax.dot_general(
-        selector, tokens, (((0,), (0,)), ((), ())), preferred_element_type=jnp.float32
-    ).astype(jnp.bfloat16)
+    outgoing, target_by_choice = route_rows(expert_ids.T, tokens, owners)
+    target = target_by_choice.T
     outgoing = outgoing.reshape(owners, CAP, model_width)
     gate_matrix = gate_weight[0]
     upper_matrix = up_weight[0]
@@ -86,18 +140,21 @@
     results = output.reshape(owners, item_count, model_width)
     returned = lax.all_to_all(results, "expert", split_axis=0, concat_axis=0, tiled=True)
     returned_flat = returned.reshape(-1, model_width)
+    slot_iota = lax.broadcasted_iota(jnp.int32, (1, 1, owners * CAP), 2)
+    hits = target[:, :, None] == slot_iota
     combine_matrix = jnp.sum(jnp.where(hits, route_weight[:, :, None], 0.0), axis=1)
     weight_high, weight_low = split_bf16(combine_matrix)
     combined = combine_rows(weight_high, weight_low, returned_flat)
     hess_scale = 2.0 / (CAP * owners * pair_count)
     row_share = FF // pair_count
     pair_place = lax.axis_index("pair")
-    hidden_wide = hidden.astype(jnp.float32)
     corner_part = lax.dot_general(
         hidden[:, :PANEL], hidden[:, :PANEL], (((0,), (0,)), ((), ())),
         preferred_element_type=jnp.float32,
     )
-    square_part = jnp.broadcast_to(jnp.sum(hidden_wide * hidden_wide), (8, PANEL))
+    held = lax.optimization_barrier(hidden).astype(jnp.float32)
+    square_sum = jnp.sum(held * held)
+    square_part = jnp.broadcast_to(square_sum, (8, PANEL))
     pack = jnp.concatenate([corner_part, square_part], axis=0)
     pack_sum = pack
     for shift in range(1, pair_count):

time: 140 us -> 138 us (0.986)
  other arithmetic: 31.6 us -> 26.4 us
  Pallas kernels: 3.86 us -> 7.95 us
  waiting for transfers between devices: 10.1 us -> 12.9 us
  matrix products: 16.2 us -> 14.2 us
    pallas_call x0 -> x1, Pallas kernels: none -> 4.1 us  [route_rows(): pl.pallas_call(route_kernel, out_shape=(jax.ShapeDtypeStruct((slots, widt...]
    ppermute x3, waiting for transfers between devices: 6 us -> 8.81 us  [per_device(): gathered.append(lax.ppermute(hidden, 'pair', ring))]
    select_n x2 -> x0, other arithmetic: 1.49 us -> none  [the longest x1 0.78 us: per_device(): owner_of = expert_ids // per_owner]
  transfers between devices with their start and end apart: 7 -> 7, of which waited for: 3 -> 3; matrix products, arithmetic and copies ran while one was open for 24% -> 22% of each run, Pallas kernels for 0% -> 0%
where the time goes in v15:
time: 138 us
  blocking collectives  58.6 us (42%)
  other arithmetic  26.4 us (19%)
  starting transfers between devices  15.3 us (11%)
  matrix products  14.2 us (10%)
  waiting for transfers between devices  12.9 us (9%)
  Pallas kernels  7.95 us (6%)
  local copies, waits for them, and re-layouts  1.49 us (1%)
  between operations  1.47 us (1%)
    all_to_all x1, blocking collectives, per_device(): lax.all_to_all(outgoing, 'expert', split_axis=0, concat_axis=0, tiled=True)  58.6 us
    another operation x3, other arithmetic, per_device(): jnp.linalg.cholesky(corner + damping * jnp.eye(PANEL, dtype=jnp.float32))  12.4 us
    another operation x2, other arithmetic, per_device(): jax.scipy.linalg.solve_triangular(lower_factor, leading.T, lower=True)  10.5 us
    ppermute x3, waiting for transfers between devices, per_device(): gathered.append(lax.ppermute(hidden, 'pair', ring))  8.81 us
    ppermute x3, starting transfers between devices, per_device(): pack_sum = pack_sum + lax.ppermute(pack, 'pair', ring)  6.58 us
    dot_general x1, matrix products, swiglu_rows(): jnp.dot(hidden, down_matrix, preferred_element_type=jnp.float32)  5.1 us
    all_to_all x1, starting transfers between devices, per_device(): lax.all_to_all(results, 'expert', split_axis=0, concat_axis=0, tiled=True)  4.99 us
    pallas_call x1, Pallas kernels, route_rows(): pl.pallas_call(route_kernel, out_shape=(jax.ShapeDtypeStruct((slots, widt...  4.1 us
  transfers between devices with their start and end apart: 7, of which 3 were waited for; matrix products, arithmetic and copies ran while one was open for 22% of the time, Pallas kernels for 0%

profile of v15, /device:TPU:0, one launch (start us, length us, event | category | flops | bytes accessed | tf_op | source)
XLA Modules:
  0.0 138.2 jit_solution(3950662954698455870)
XLA Ops:
  0.6 4.1 %shard_map.85 = (bf16[512,4096]{1,0:T(8,128)(2,1)}, s32[8,128]{1,0:T(8,128)}) custom-call(s32[8,128]{1,0:T(8,128)} %bitcast.46, bf16[128,4096]{1,0:T(8,128)(2,1)} %tokens_ref.1), custom_call_target="tpu_custom_call" | custom-call | flops 536870912 | bytes 5242880 | tf_op jit(solution)/shard_map/pallas_call | solution.py:99
  4.7 58.6 %all_to_all.10 = bf16[32,16,4096]{2,1,0:T(8,128)(2,1)S(1)} all-to-all(bf16[32,16,4096]{2,1,0:T(8,128)(2,1)} %bitcast.37), channel_id=1, replica_groups=mesh['expert'=32,'pair'=4] {'expert'}, dimensions={0} | all-to-all | bytes 8388608 | tf_op jit(solution)/shard_map/all_to_all | solution.py:135
  63.4 3.4 %fusion.4 = f32[512,768]{1,0:T(8,128)S(1)} fusion(bf16[512,4096]{1,0:T(8,128)(2,1)S(1)} %bitcast.38, bf16[1,4096,768]{2,1,0:T(8,128)(2,1)S(1)} %copy-done.3), kind=kOutput, calls=%fused_computation.4 | convolution fusion | flops 3221225472 | bytes 12058624 | tf_op jit(solution)/shard_map/dot_general | solution.py:15
  66.8 3.5 %multiply_convert_fusion = bf16[512,768]{1,0:T(8,128)(2,1)S(1)} fusion(f32[512,768]{1,0:T(8,128)S(1)} %fusion.4, bf16[512,4096]{1,0:T(8,128)(2,1)S(1)} %bitcast.39, bf16[1,4096,768]{2,1,0:T(8,128)(2,1)S(1)} %bitcast.43), kind=kOutput, calls=%fused_computation.11 | convolution fusion | flops 3223584768 | bytes 12845056 | tf_op jit(solution)/shard_map/dot_general | solution.py:16
  70.3 5.1 %fusion.6 = bf16[512,4096]{1,0:T(8,128)(2,1)} fusion(bf16[512,768]{1,0:T(8,128)(2,1)S(1)} %multiply_convert_fusion, bf16[1,768,4096]{2,1,0:T(8,128)(2,1)S(1)} %bitcast.45), kind=kOutput, calls=%fused_computation.6 | convolution fusion | flops 3223322624 | bytes 11272192 | tf_op jit(solution)/shard_map/dot_general | solution.py:18
  75.4 5.0 %all-to-all-start.1 = ((bf16[32,16,4096]{2,1,0:T(8,128)(2,1)}), bf16[32,16,4096]{2,1,0:T(8,128)(2,1)}, u32[]{:S(2)}, u32[]{:S(2)}) async-start(bf16[32,16,4096]{2,1,0:T(8,128)(2,1)} %bitcast.36), calls=%async_computation.1 | async-start | bytes 8388608 | tf_op jit(solution)/shard_map/all_to_all | solution.py:141
  80.6 0.7 select_reduce_fusion
  81.3 0.8 fusion.12
  82.1 1.0 multiply_reduce_fusion
  83.3 0.7 concatenate.7
  84.0 2.0 %collective-permute-start.3 = (f32[136,128]{1,0:T(8,128)S(1)}, f32[136,128]{1,0:T(8,128)S(1)}, u32[]{:S(2)}, u32[]{:S(2)}) collective-permute-start(f32[136,128]{1,0:T(8,128)S(1)} %concatenate.7), channel_id=1, source_target_pairs={{0,1},{1,2},{2,3},{3,0},{4,5},{5,6},{6,7},{7,4},{8,9},{9,10},{10,1... | collective-permute-start | bytes 208904 | tf_op jit(solution)/shard_map/ppermute | solution.py:162
  86.0 3.6 %collective-permute-start.4 = (f32[136,128]{1,0:T(8,128)S(1)}, f32[136,128]{1,0:T(8,128)S(1)}, u32[]{:S(2)}, u32[]{:S(2)}) collective-permute-start(f32[136,128]{1,0:T(8,128)S(1)} %concatenate.7), channel_id=1, source_target_pairs={{0,2},{1,3},{2,0},{3,1},{4,6},{5,7},{6,4},{7,5},{8,10},{9,11},{10,... | collective-permute-start | bytes 208904 | tf_op jit(solution)/shard_map/ppermute | solution.py:162
  89.6 1.0 collective-permute-start.5
  90.6 1.0 collective-permute-start
  92.1 2.2 %collective-permute-start.2 = (bf16[512,768]{1,0:T(8,128)(2,1)S(1)}, bf16[512,768]{1,0:T(8,128)(2,1)S(1)}, u32[]{:S(2)}, u32[]{:S(2)}) collective-permute-start(bf16[512,768]{1,0:T(8,128)(2,1)S(1)} %multiply_convert_fusion), channel_id=1, source_target_pairs={{0,3},{1,0},{2,1},{3,2},{4,7},{5,4},{6,5},{7,6},{8,11},{9,8},{10,9... | collective-permute-start | bytes 2359304 | tf_op jit(solution)/shard_map/ppermute | solution.py:169
  94.3 0.7 add_add_fusion
  96.3 11.7 %cholesky.16 = f32[128,128]{1,0:T(8,128)S(1)} custom-call(f32[128,128]{1,0:T(8,128)S(1)} %fusion.19), custom_call_target="Cholesky" | custom-call | tf_op jit(solution)/shard_map/jit(cholesky)/cholesky | solution.py:165
  108.7 0.7 fusion.16
  109.3 9.8 %custom-call.7 = f32[1,128,128]{1,2,0:T(8,128)S(1)} custom-call(f32[1,128,128]{2,1,0:T(8,128)S(1)} %fusion.16), custom_call_target="InvertDiagBlocksLowerTriangular" | custom-call | tf_op jit(solution)/shard_map/jit(_solve_triangular)/triangular_solve | solution.py:181
  119.2 8.4 %collective-permute-done = bf16[512,768]{1,0:T(8,128)(2,1)S(1)} collective-permute-done((bf16[512,768]{1,0:T(8,128)(2,1)S(1)}, bf16[512,768]{1,0:T(8,128)(2,1)S(1)}, u32[]{:S(2)}, u32[]{:S(2)}) %collective-permute-start) | collective-permute-done | bytes 786464 | tf_op jit(solution)/shard_map/ppermute | solution.py:169
  128.3 1.1 convolution_multiply_fusion
  129.4 0.9 convolution_bitcast_fusion
  130.3 4.0 %all-to-all-done.1 = bf16[32,16,4096]{2,1,0:T(8,128)(2,1)} async-done(((bf16[32,16,4096]{2,1,0:T(8,128)(2,1)}), bf16[32,16,4096]{2,1,0:T(8,128)(2,1)}, u32[]{:S(2)}, u32[]{:S(2)}) %all-to-all-start.1) | async-done | bytes 4194336 | tf_op jit(solution)/shard_map/all_to_all | solution.py:141
  134.4 3.9 %shard_map.86 = bf16[128,4096]{1,0:T(8,128)(2,1)} custom-call(bf16[128,512]{1,0:T(8,128)(2,1)} %get-tuple-element.8.high_ref, bf16[128,512]{1,0:T(8,128)(2,1)} %get-tuple-element.7.low_ref, bf16[512,4096]{1,0:T(8,128)(2,1)} %bitcast.8.rows_ref), custom_call_target="tpu_custom_call" | custom-call | flops 1073741824 | bytes 5505024 | tf_op jit(solution)/shard_map/pallas_call | solution.py:38
  (35 shorter events, 2.9 us)
Async XLA Ops:
  4.7 58.6 %copy-start.3 = (bf16[1,4096,768]{2,1,0:T(8,128)(2,1)S(1)}, bf16[1,4096,768]{2,1,0:T(8,128)(2,1)}, u32[]{:S(2)}) copy-start(bf16[1,4096,768]{2,1,0:T(8,128)(2,1)} %param.9) | copy-start | bytes 18874372
  4.7 62.0 %slice-start = ((s8[6291456]{0:T(1024)(128)(4,1)}), s8[4194304]{0:T(1024)(128)(4,1)S(1)}, s32[]{:S(2)}) async-start(s8[6291456]{0:T(1024)(128)(4,1)} %bitcast.42), calls=%async_computation.2 | async-start | bytes 8388608
  4.7 65.6 %slice-start.2 = ((s8[6291456]{0:T(1024)(128)(4,1)}), s8[4194304]{0:T(1024)(128)(4,1)S(1)}, s32[]{:S(2)}) async-start(s8[6291456]{0:T(1024)(128)(4,1)} %bitcast.44), calls=%async_computation.4 | async-start | bytes 8388608
  63.4 3.4 %slice-start.1 = ((s8[6291456]{0:T(1024)(128)(4,1)}), s8[2097152]{0:T(1024)(128)(4,1)S(1)}, s32[]{:S(2)}) async-start(s8[6291456]{0:T(1024)(128)(4,1)} %bitcast.42), calls=%async_computation.3 | async-start | bytes 4194304
  63.4 6.9 %slice-start.3 = ((s8[6291456]{0:T(1024)(128)(4,1)}), s8[2097152]{0:T(1024)(128)(4,1)S(1)}, s32[]{:S(2)}) async-start(s8[6291456]{0:T(1024)(128)(4,1)} %bitcast.44), calls=%async_computation.5 | async-start | bytes 4194304
  75.4 5.0 %copy-start.2 = (s32[8,128]{1,0:T(8,128)S(1)}, s32[8,128]{1,0:T(8,128)}, u32[]{:S(2)}) copy-start(s32[8,128]{1,0:T(8,128)} %get-tuple-element.5) | copy-start | bytes 12292
  75.4 5.1 %copy-start.1 = (f32[128,8]{0,1:T(8,128)S(1)}, f32[128,8]{0,1:T(8,128)}, u32[]{:S(2)}) copy-start(f32[128,8]{0,1:T(8,128)} %param.8) | copy-start | bytes 12292
  75.4 59.0 %all-to-all-start.1 = ((bf16[32,16,4096]{2,1,0:T(8,128)(2,1)}), bf16[32,16,4096]{2,1,0:T(8,128)(2,1)}, u32[]{:S(2)}, u32[]{:S(2)}) async-start(bf16[32,16,4096]{2,1,0:T(8,128)(2,1)} %bitcast.36), calls=%async_computation.1 | async-start | bytes 8388608 | tf_op jit(solution)/shard_map/all_to_all | solution.py:141
  84.0 8.1 %collective-permute-start.3 = (f32[136,128]{1,0:T(8,128)S(1)}, f32[136,128]{1,0:T(8,128)S(1)}, u32[]{:S(2)}, u32[]{:S(2)}) collective-permute-start(f32[136,128]{1,0:T(8,128)S(1)} %concatenate.7), channel_id=1, source_target_pairs={{0,1},{1,2},{2,3},{3,0},{4,5},{5,6},{6,7},{7,4},{8,9},{9,10},{10,1... | collective-permute-start | bytes 208904 | tf_op jit(solution)/shard_map/ppermute | solution.py:162
  86.0 8.3 %collective-permute-start.4 = (f32[136,128]{1,0:T(8,128)S(1)}, f32[136,128]{1,0:T(8,128)S(1)}, u32[]{:S(2)}, u32[]{:S(2)}) collective-permute-start(f32[136,128]{1,0:T(8,128)S(1)} %concatenate.7), channel_id=1, source_target_pairs={{0,2},{1,3},{2,0},{3,1},{4,6},{5,7},{6,4},{7,5},{8,10},{9,11},{10,... | collective-permute-start | bytes 208904 | tf_op jit(solution)/shard_map/ppermute | solution.py:162
  89.6 4.7 %collective-permute-start.5 = (f32[136,128]{1,0:T(8,128)S(1)}, f32[136,128]{1,0:T(8,128)S(1)}, u32[]{:S(2)}, u32[]{:S(2)}) collective-permute-start(f32[136,128]{1,0:T(8,128)S(1)} %concatenate.7), channel_id=1, source_target_pairs={{0,3},{1,0},{2,1},{3,2},{4,7},{5,4},{6,5},{7,6},{8,11},{9,8},{10,9... | collective-permute-start | bytes 208904 | tf_op jit(solution)/shard_map/ppermute | solution.py:162
  90.6 37.0 %collective-permute-start = (bf16[512,768]{1,0:T(8,128)(2,1)S(1)}, bf16[512,768]{1,0:T(8,128)(2,1)S(1)}, u32[]{:S(2)}, u32[]{:S(2)}) collective-permute-start(bf16[512,768]{1,0:T(8,128)(2,1)S(1)} %multiply_convert_fusion), channel_id=1, source_target_pairs={{0,1},{1,2},{2,3},{3,0},{4,5},{5,6},{6,7},{7,4},{8,9},{9,10},{10,1... | collective-permute-start | bytes 2359304 | tf_op jit(solution)/shard_map/ppermute | solution.py:169
  91.6 36.0 %collective-permute-start.1 = (bf16[512,768]{1,0:T(8,128)(2,1)S(1)}, bf16[512,768]{1,0:T(8,128)(2,1)S(1)}, u32[]{:S(2)}, u32[]{:S(2)}) collective-permute-start(bf16[512,768]{1,0:T(8,128)(2,1)S(1)} %multiply_convert_fusion), channel_id=1, source_target_pairs={{0,2},{1,3},{2,0},{3,1},{4,6},{5,7},{6,4},{7,5},{8,10},{9,11},{10,... | collective-permute-start | bytes 2359304 | tf_op jit(solution)/shard_map/ppermute | solution.py:169
  92.1 35.9 %collective-permute-start.2 = (bf16[512,768]{1,0:T(8,128)(2,1)S(1)}, bf16[512,768]{1,0:T(8,128)(2,1)S(1)}, u32[]{:S(2)}, u32[]{:S(2)}) collective-permute-start(bf16[512,768]{1,0:T(8,128)(2,1)S(1)} %multiply_convert_fusion), channel_id=1, source_target_pairs={{0,3},{1,0},{2,1},{3,2},{4,7},{5,4},{6,5},{7,6},{8,11},{9,8},{10,9... | collective-permute-start | bytes 2359304 | tf_op jit(solution)/shard_map/ppermute | solution.py:169
  129.4 8.8 %copy-start = (f32[192,768]{1,0:T(8,128)}, f32[192,768]{1,0:T(8,128)S(1)}, u32[]{:S(2)}) copy-start(f32[192,768]{1,0:T(8,128)S(1)} %convolution_multiply_fusion) | copy-start | bytes 1769476
